TPU v7x, 256 devices: a whole 4x4x8 slice. The times are simulated.
256 devices in a mesh: ctx: 32 (over y, x, core), tp: 8 (over z).
Axes of the slice: x: 4, y: 4, z: 8, core: 2. Of those that a mesh axis runs over, the one named last changes fastest.
Arguments:
- queries: bfloat16 [8192, 4096], P('ctx', 'tp'), may hold values from -12 to 12, as said below
- key_rows: bfloat16 [8192, 1024], P('ctx', 'tp'), may hold values from -12 to 12, as said below
- value_rows: bfloat16 [8192, 1024], P('ctx', 'tp'), may hold values from -6 to 6
- segments: int32 [8192], replicated, may hold values from 0 to 63, never falling along the last dimension, each value on 1 to 4096 neighbouring positions
- owner_ids: int32 [8192, 1], P('ctx'), may hold values from 0 to 7; in each aligned block of 256 rows (0 to 255, 256 to 511, ...) at most 64 rows name the same one
- out_proj: bfloat16 [4096, 8192], P('tp'), may hold values from -0.09375 to 0.09375
- residual: bfloat16 [16384, 8192], P(('ctx', 'tp')), may hold values from -4 to 4
- norm_gain: float32 [8192], replicated, may hold values from 0.5 to 1.5
Outputs:
- hidden_out: bfloat16 [16384, 8192], P(('ctx', 'tp'))
- normed: bfloat16 [16384, 8192], P(('ctx', 'tp'))
Inputs may be any that keep to these rules, and one draw needn't show every extreme that they name: `segments`: never falling along the tokens; every document has 1 to 4096 tokens and one has exactly 4096. `owner_ids`: among the rows of one device's token block no owner is named more than 64 times; some owner is named exactly 64 times in some block. `queries`: Real-valued entries. `key_rows`: Real-valued entries.
All inputs are finite; a program needn't handle non-finite values.
Results may differ from a plain program's by a relative error of at most 0.01.
Values may be sent and summed in bfloat16 or wider, within the bound.
No kernel may reach another device: no remote copies, remote signals or barrier semaphores. Data moves between devices by JAX's collectives and lax.ppermute only.
A program may use at most 128 MiB of HBM per device.

v0:
```python
import math

import jax
import jax.numpy as jnp
from jax import lax
from jax.sharding import PartitionSpec as P

HEADS = 32
KV_HEADS = 8
HEAD_DIM = 128


def slot_sources(owners, row_rank, owner_here, slot_count):
    token_count = owners.shape[0]
    slot_numbers = jnp.arange(slot_count, dtype=jnp.int32)[:, None]
    matches = ((owners[None, :] == owner_here) & (row_rank[None, :] == slot_numbers)).astype(
        jnp.int32
    )
    token_index = jnp.sum(matches * jnp.arange(token_count, dtype=jnp.int32)[None, :], axis=1)
    filled = jnp.sum(matches, axis=1) > 0
    return (token_index, filled)


def on_device(queries, key_rows, value_rows, segments, owner_ids, out_proj, residual, norm_gain):
    rows_here = queries.shape[0]
    kv_local = key_rows.shape[1] // HEAD_DIM
    group_size = HEADS // KV_HEADS
    score_scale = 1.0 / math.sqrt(HEAD_DIM)
    my_start = lax.axis_index("ctx") * rows_here
    query_heads = queries.reshape(rows_here, kv_local, group_size, HEAD_DIM)
    query_pos = my_start + jnp.arange(rows_here, dtype=jnp.int32)
    query_seg = lax.dynamic_slice_in_dim(segments, my_start, rows_here, 0)
    start_state = (
        jnp.full((kv_local, group_size, rows_here), -1e30, jnp.float32),
        jnp.zeros((kv_local, group_size, rows_here), jnp.float32),
        jnp.zeros((kv_local, group_size, rows_here, HEAD_DIM), jnp.float32),
    )
    carried = start_state
    key_piece = lax.all_gather(key_rows, "ctx", axis=0, tiled=True)
    value_piece = lax.all_gather(value_rows, "ctx", axis=0, tiled=True)
    piece_rows = key_piece.shape[0]
    key_width = 512
    block_count = piece_rows // key_width
    key_blocks = key_piece.reshape(block_count, key_width, kv_local, HEAD_DIM)
    value_blocks = value_piece.reshape(block_count, key_width, kv_local, HEAD_DIM)

    def update(states, block_item):
        block_index, key_block, value_block = block_item
        key_start = block_index * key_width
        key_seg = lax.dynamic_slice_in_dim(segments, key_start, key_width, 0)
        key_pos = key_start + jnp.arange(key_width, dtype=jnp.int32)
        allowed = (query_seg[:, None] == key_seg[None, :]) & (
            key_pos[None, :] <= query_pos[:, None]
        )
        running_max, totals, weighted = states
        scores = (
            jnp.einsum("tkgd,skd->kgts", query_heads, key_block, preferred_element_type=jnp.float32)
            * score_scale
        )
        scores = jnp.where(allowed, scores, -1e30)
        new_max = jnp.maximum(running_max, jnp.max(scores, axis=-1))
        exponent = jnp.where(allowed, jnp.exp(scores - new_max[..., None]), 0.0)
        factor = jnp.exp(running_max - new_max)
        totals = totals * factor + jnp.sum(exponent, axis=-1)
        weighted = weighted * factor[..., None] + jnp.einsum(
            "kgts,skd->kgtd",
            exponent.astype(jnp.bfloat16),
            value_block,
            preferred_element_type=jnp.float32,
        )
        states = (new_max, totals, weighted)
        return (states, None)

    carried, _ = lax.scan(
        update, carried, (jnp.arange(block_count, dtype=jnp.int32), key_blocks, value_blocks)
    )
    running_max, totals, weighted = carried
    mixed_heads = weighted / totals[..., None]
    attended = jnp.transpose(mixed_heads, (2, 0, 1, 3)).reshape(rows_here, -1).astype(jnp.bfloat16)
    partial_rows = jnp.dot(attended, out_proj, preferred_element_type=jnp.float32).astype(
        jnp.bfloat16
    )
    slot_count = residual.shape[0]
    owner_count = lax.axis_size("tp")
    owner_here = lax.axis_index("tp")
    owners = owner_ids[:, 0]
    onehot = (owners[:, None] == jnp.arange(owner_count, dtype=jnp.int32)[None, :]).astype(
        jnp.int32
    )
    before = jnp.cumsum(onehot, axis=0) - onehot
    row_rank = jnp.sum(before * onehot, axis=1)
    summed = lax.psum(partial_rows.astype(jnp.float32).astype(jnp.bfloat16), "tp").astype(
        jnp.float32
    )
    token_index, filled = slot_sources(owners, row_rank, owner_here, slot_count)
    owned_rows = jnp.where(filled[:, None], jnp.take(summed, token_index, axis=0), 0.0)
    hidden_sum = residual.astype(jnp.float32) + owned_rows
    mean_square = jnp.mean(hidden_sum * hidden_sum, axis=-1, keepdims=True)
    normed = hidden_sum * lax.rsqrt(mean_square + 1e-05) * norm_gain
    return (hidden_sum.astype(jnp.bfloat16), normed.astype(jnp.bfloat16))


def solution(mesh):
    placed = (
        P("ctx", "tp"),
        P("ctx", "tp"),
        P("ctx", "tp"),
        P(),
        P("ctx", None),
        P("tp", None),
        P(("ctx", "tp"), None),
        P(),
    )
    return jax.shard_map(
        on_device,
        mesh=mesh,
        in_specs=placed,
        out_specs=(P(("ctx", "tp"), None), P(("ctx", "tp"), None)),
        check_vma=False,
    )
```

profile of v0, /device:TPU:1, one launch (start us, length us, event | category | flops | bytes accessed | tf_op | source)
XLA Modules:
  0.0 347.0 jit_solution(442870078505631397)
XLA Ops:
  8.7 1.1 copy.16
  10.0 0.8 dynamic_slice.17
  10.8 52.6 %all-gather.3.cloned.1.call-done = bf16[8192,128]{1,0:T(8,128)(2,1)} async-done(((bf16[256,128]{1,0:T(8,128)(2,1)}), bf16[8192,128]{1,0:T(8,128)(2,1)}) %all-gather.3.cloned.1.call-update) | async-done | bytes 2097168 | tf_op jit(solution)/shard_map/all_gather | solution.py:39
  63.3 50.6 %all-gather.5.cloned.1.call-done = bf16[8192,128]{1,0:T(8,128)(2,1)} async-done(((bf16[256,128]{1,0:T(8,128)(2,1)}), bf16[8192,128]{1,0:T(8,128)(2,1)}) %all-gather.5.cloned.1.call-update) | async-done | bytes 2097168 | tf_op jit(solution)/shard_map/all_gather | solution.py:40
  113.9 95.9 %while.15 = (s32[]{:T(128)}, f32[1,4,256]{2,1,0:T(4,128)S(1)}, f32[1,4,256]{2,1,0:T(4,128)S(1)}, f32[1,4,256,128]{3,2,1,0:T(8,128)S(1)}, s32[256]{0:T(256)S(1)},...) while((s32[]{:T(128)}, f32[1,4,256]{2,1,0:T(4,128)S(1)}, ...), condition=%wide.region_8.9_spmd.clone, body=%wide.region_5.8_spmd.clone.sunk | while | flops 276044544 | bytes 8468703 | solution.py:74
  116.1 1.4 fusion.41
  117.5 1.8 fusion.44
  121.1 0.8 dynamic_slice.39
  122.1 1.4 fusion.41
  123.5 1.8 fusion.44
  128.1 1.4 fusion.41
  129.5 1.8 fusion.44
  133.1 0.8 dynamic_slice.39
  134.1 1.4 fusion.41
  135.5 1.8 fusion.44
  140.1 1.4 fusion.41
  141.5 1.8 fusion.44
  145.1 0.8 dynamic_slice.39
  146.1 1.4 fusion.41
  147.5 1.8 fusion.44
  152.1 1.4 fusion.41
  153.5 1.8 fusion.44
  157.1 0.8 dynamic_slice.39
  158.1 1.4 fusion.41
  159.5 1.8 fusion.44
  164.1 1.4 fusion.41
  165.5 1.8 fusion.44
  169.1 0.8 dynamic_slice.39
  170.1 1.4 fusion.41
  171.5 1.8 fusion.44
  176.1 1.4 fusion.41
  177.5 1.8 fusion.44
  181.1 0.8 dynamic_slice.39
  182.1 1.4 fusion.41
  183.5 1.8 fusion.44
  188.1 1.4 fusion.41
  189.5 1.8 fusion.44
  194.1 1.4 fusion.41
  195.5 1.8 fusion.44
  200.1 1.4 fusion.41
  201.5 1.8 fusion.44
  206.0 1.4 fusion.41
  207.5 1.8 fusion.44
  210.1 7.7 %convolution_convert_fusion = bf16[256,8192]{1,0:T(8,128)(2,1)} fusion(bf16[256,512]{0,1:T(8,128)(2,1)S(1)} %bitcast.97, bf16[512,8192]{1,0:T(8,128)(2,1)} %param.15), kind=kOutput, calls=%fused_computation.35 | convolution fusion | flops 2149580800 | bytes 12845056 | tf_op jit(solution)/shard_map/dot_general | solution.py:80
  219.6 106.2 %all-reduce.2.cloned.1.call-done = bf16[256,8192]{1,0:T(8,128)(2,1)} async-done(((bf16[256,8192]{1,0:T(8,128)(2,1)}), bf16[256,8192]{1,0:T(8,128)(2,1)}) %all-reduce.2.cloned.1.call-update) | async-done | bytes 4194320 | tf_op jit(solution)/shard_map/psum | solution.py:92
  325.7 6.4 %convert_element_type.47 = f32[256,8192]{1,0:T(8,128)} convert(bf16[256,8192]{1,0:T(8,128)(2,1)} %all-reduce.2.cloned.1.call-done) | non-fusion elementwise | flops 2097152 | bytes 12582912 | tf_op jit(solution)/shard_map/convert_element_type | solution.py:92
  332.1 5.7 %gather_fusion = f32[64,8192]{1,0:T(8,128)S(1)} fusion(f32[256,8192]{1,0:T(8,128)} %convert_element_type.47, s32[1024]{0:T(1024)S(1)} %pad_clamp_fusion), kind=kCustom, calls=%fused_computation | custom fusion | bytes 4194560 | tf_op jit(solution)/shard_map/jit(_take)/gather | solution.py:96
  338.6 1.9 multiply_convert_fusion
  (170 shorter events, 33.9 us)
Async XLA Ops:
  7.2 56.2 %all-gather.3.cloned.1.call-start = ((), (), s32[]{:S(2)}) async-start(), calls=%async_computation | async-start | bytes 2162688 | tf_op jit(solution)/shard_map/all_gather | solution.py:39
  7.9 106.0 %all-gather.5.cloned.1.call-start = ((), (), s32[]{:S(2)}) async-start(), calls=%async_computation.1 | async-start | bytes 2162688 | tf_op jit(solution)/shard_map/all_gather | solution.py:40
  8.6 317.1 %all-reduce.2.cloned.1.call-start = ((), (), s32[]{:S(2)}) async-start(), calls=%async_computation.2 | async-start | bytes 8388608 | tf_op jit(solution)/shard_map/psum | solution.py:92
  217.8 0.7 copy-start.2
  332.1 5.7 %copy-start = (bf16[64,8192]{1,0:T(8,128)(2,1)S(1)}, bf16[64,8192]{1,0:T(8,128)(2,1)}, u32[]{:S(2)}) copy-start(bf16[64,8192]{1,0:T(8,128)(2,1)} %param.16) | copy-start | bytes 3145732
  337.8 0.8 copy-start.1
Sparse Core Ops, SparseCore 0:
  10.5 52.7 all-gather.2
  65.9 47.9 all-gather.4
  217.9 107.7 all-reduce.1
where the time goes:
time: 349 us; the launch traced here: 347 us
  waiting for transfers between devices  211 us (60%)
  matrix products  58.6 us (17%)
  local copies, waits for them, and re-layouts  30.7 us (9%)
  other arithmetic  22.1 us (6%)
  between operations  13.9 us (4%)
  loops' own time  10.9 us (3%)
    psum x1, waiting for transfers between devices, on_device(): lax.psum(partial_rows.astype(jnp.float32).astype(jnp.bfloat16), 'tp')  106 us
    all_gather x1, waiting for transfers between devices, on_device(): key_piece = lax.all_gather(key_rows, 'ctx', axis=0, tiled=True)  52.6 us
    all_gather x1, waiting for transfers between devices, on_device(): value_piece = lax.all_gather(value_rows, 'ctx', axis=0, tiled=True)  50.6 us
    dot_general x16, matrix products, update(): jnp.einsum('kgts,skd->kgtd', exponent.astype(jnp.bfloat16), value_block,...  28.7 us
    dot_general x16, matrix products, update(): jnp.einsum('tkgd,skd->kgts', query_heads, key_block, preferred_element_ty...  22.3 us
    dynamic_slice x16, local copies, waits for them, and re-layouts, update(): key_seg = lax.dynamic_slice_in_dim(segments, key_start, key_width, 0)  12.2 us
    another operation x1, loops' own time, on_device(): lax.scan(update, carried, (jnp.arange(block_count, dtype=jnp.int32), key_...  10.9 us
    dynamic_slice x16, local copies, waits for them, and re-layouts, on_device(): lax.scan(update, carried, (jnp.arange(block_count, dtype=jnp.int32), key_...  9.51 us
  transfers between devices with their start and end apart: 3, of which 3 were waited for; matrix products, arithmetic and copies ran while one was open for 1% of the time, Pallas kernels for 0%

commit v1 on v0

v1 whole, which is shorter than its diff:
```python
import math

import jax
import jax.numpy as jnp
from jax import lax
from jax.sharding import PartitionSpec as P

HEADS = 32
KV_HEADS = 8
HEAD_DIM = 128


def on_device(queries, key_rows, value_rows, segments, owner_ids, out_proj, residual, norm_gain):
    rows_here = queries.shape[0]
    kv_local = key_rows.shape[1] // HEAD_DIM
    kv_cols = kv_local * HEAD_DIM
    group_size = HEADS // KV_HEADS
    score_scale = 1.0 / math.sqrt(HEAD_DIM)
    my_block = lax.axis_index("ctx")
    my_start = my_block * rows_here
    query_heads = queries.reshape(rows_here, kv_local, group_size, HEAD_DIM)
    query_pos = my_start + jnp.arange(rows_here, dtype=jnp.int32)
    query_seg = lax.dynamic_slice_in_dim(segments, my_start, rows_here, 0)
    start_state = (
        jnp.full((kv_local, group_size, rows_here), -1e30, jnp.float32),
        jnp.zeros((kv_local, group_size, rows_here), jnp.float32),
        jnp.zeros((kv_local, group_size, rows_here, HEAD_DIM), jnp.float32),
    )
    kv_pair = jnp.concatenate([key_rows, value_rows], axis=1)
    kv_all = lax.all_gather(kv_pair, "ctx", axis=0, tiled=True)
    key_width = rows_here
    doc_start = jnp.sum((segments < query_seg[0]).astype(jnp.int32))
    first_block = doc_start // key_width

    def update(block_index, states):
        key_start = block_index * key_width
        kv_block = lax.dynamic_slice_in_dim(kv_all, key_start, key_width, 0)
        key_block = kv_block[:, :kv_cols].reshape(key_width, kv_local, HEAD_DIM)
        value_block = kv_block[:, kv_cols:].reshape(key_width, kv_local, HEAD_DIM)
        key_seg = lax.dynamic_slice_in_dim(segments, key_start, key_width, 0)
        key_pos = key_start + jnp.arange(key_width, dtype=jnp.int32)
        allowed = (query_seg[:, None] == key_seg[None, :]) & (
            key_pos[None, :] <= query_pos[:, None]
        )
        running_max, totals, weighted = states
        scores = (
            jnp.einsum("tkgd,skd->kgts", query_heads, key_block, preferred_element_type=jnp.float32)
            * score_scale
        )
        scores = jnp.where(allowed, scores, -1e30)
        new_max = jnp.maximum(running_max, jnp.max(scores, axis=-1))
        exponent = jnp.where(allowed, jnp.exp(scores - new_max[..., None]), 0.0)
        factor = jnp.exp(running_max - new_max)
        totals = totals * factor + jnp.sum(exponent, axis=-1)
        weighted = weighted * factor[..., None] + jnp.einsum(
            "kgts,skd->kgtd",
            exponent.astype(jnp.bfloat16),
            value_block,
            preferred_element_type=jnp.float32,
        )
        return (new_max, totals, weighted)

    running_max, totals, weighted = lax.fori_loop(first_block, my_block + 1, update, start_state)
    mixed_heads = weighted / totals[..., None]
    attended = jnp.transpose(mixed_heads, (2, 0, 1, 3)).reshape(rows_here, -1).astype(jnp.bfloat16)
    slot_count = residual.shape[0]
    owner_count = lax.axis_size("tp")
    owners = owner_ids[:, 0]
    onehot = (owners[:, None] == jnp.arange(owner_count, dtype=jnp.int32)[None, :]).astype(
        jnp.int32
    )
    before = jnp.cumsum(onehot, axis=0) - onehot
    row_rank = jnp.sum(before * onehot, axis=1)
    slot_of_token = owners * slot_count + row_rank
    all_slots = jnp.arange(owner_count * slot_count, dtype=jnp.int32)
    select = (slot_of_token[None, :] == all_slots[:, None]).astype(jnp.bfloat16)
    attended_slots = jnp.dot(select, attended, preferred_element_type=jnp.float32).astype(
        jnp.bfloat16
    )
    partial_slots = jnp.dot(attended_slots, out_proj, preferred_element_type=jnp.float32).astype(
        jnp.bfloat16
    )
    owned_rows = lax.psum_scatter(partial_slots, "tp", scatter_dimension=0, tiled=True).astype(
        jnp.float32
    )
    hidden_sum = residual.astype(jnp.float32) + owned_rows
    mean_square = jnp.mean(hidden_sum * hidden_sum, axis=-1, keepdims=True)
    normed = hidden_sum * lax.rsqrt(mean_square + 1e-05) * norm_gain
    return (hidden_sum.astype(jnp.bfloat16), normed.astype(jnp.bfloat16))


def solution(mesh):
    placed = (
        P("ctx", "tp"),
        P("ctx", "tp"),
        P("ctx", "tp"),
        P(),
        P("ctx", None),
        P("tp", None),
        P(("ctx", "tp"), None),
        P(),
    )
    return jax.shard_map(
        on_device,
        mesh=mesh,
        in_specs=placed,
        out_specs=(P(("ctx", "tp"), None), P(("ctx", "tp"), None)),
        check_vma=False,
    )
```

time: 349 us -> 248 us (0.71)
  matrix products: 58.6 us -> 15.5 us
  local copies, waits for them, and re-layouts: 30.7 us -> 4.54 us
  waiting for transfers between devices: 211 us -> 196 us
  loops' own time: 10.9 us -> 0.13 us
  other arithmetic: 22.1 us -> 11.9 us
    reduce_scatter x0 -> x1, waiting for transfers between devices: none -> 148 us  [on_device(): lax.psum_scatter(partial_slots, 'tp', scatter_dimension=0, tiled=True)]
    psum x1 -> x0, waiting for transfers between devices: 106 us -> none  [on_device(): lax.psum(partial_rows.astype(jnp.float32).astype(jnp.bfloat16), 'tp')]
    all_gather x2 -> x1, waiting for transfers between devices: 103 us -> 47.5 us  [on_device(): kv_all = lax.all_gather(kv_pair, 'ctx', axis=0, tiled=True)]
    dot_general x16 -> x2, matrix products: 28.7 us -> 2.71 us  [update(): jnp.einsum('kgts,skd->kgtd', exponent.astype(jnp.bfloat16), value_block,...]
    dot_general x16 -> x2, matrix products: 22.3 us -> 2.35 us  [update(): jnp.einsum('tkgd,skd->kgts', query_heads, key_block, preferred_element_ty...]
    another operation x1, loops' own time: 10.9 us -> 0.13 us  [on_device(): lax.fori_loop(first_block, my_block + 1, update, start_state)]
    dynamic_slice x16 -> x2, local copies, waits for them, and re-layouts: 12.2 us -> 1.53 us  [update(): key_seg = lax.dynamic_slice_in_dim(segments, key_start, key_width, 0)]
    dynamic_slice x16 -> x0, local copies, waits for them, and re-layouts: 9.51 us -> none  [on_device(): lax.scan(update, carried, (jnp.arange(block_count, dtype=jnp.int32), key_...]
  transfers between devices with their start and end apart: 3 -> 2, of which waited for: 3 -> 2; matrix products, arithmetic and copies ran while one was open for 1% -> 3% of each run, Pallas kernels for 0% -> 0%
where the time goes in v1:
time: 248 us; the launch traced here: 245 us
  waiting for transfers between devices  196 us (79%)
  between operations  16.6 us (7%)
  matrix products  15.5 us (6%)
  other arithmetic  11.9 us (5%)
  local copies, waits for them, and re-layouts  4.54 us (2%)
    reduce_scatter x1, waiting for transfers between devices, on_device(): lax.psum_scatter(partial_slots, 'tp', scatter_dimension=0, tiled=True)  148 us
    all_gather x1, waiting for transfers between devices, on_device(): kv_all = lax.all_gather(kv_pair, 'ctx', axis=0, tiled=True)  47.5 us
    dot_general x1, matrix products, on_device(): jnp.dot(attended_slots, out_proj, preferred_element_type=jnp.float32)  10.4 us
  transfers between devices with their start and end apart: 2, of which 2 were waited for; matrix products, arithmetic and copies ran while one was open for 3% of the time, Pallas kernels for 0%

profile of v1, /device:TPU:1, one launch (start us, length us, event | category | flops | bytes accessed | tf_op | source)
XLA Modules:
  0.0 244.5 jit_solution(14181428456914974519)
XLA Ops:
  7.2 0.0 all-gather.2.cloned.1.call-start
  7.2 1.5 pad_maximum_fusion
  8.8 0.0 all-gather.2.cloned.1.call-update
  8.8 0.0 reduce-scatter.2.cloned.1.call-start
  8.8 0.8 dynamic_slice.9
  9.6 0.5 slice.17
  10.1 2.0 convert_reduce_fusion
  14.6 0.7 fusion.21
  15.3 0.6 reduce-window.6
  15.9 0.2 slice_reduce_fusion
  16.1 1.1 copy.12
  17.2 0.2 copy.13
  17.4 0.8 fusion.20
  18.2 0.7 multiply_add_fusion
  18.9 47.5 %all-gather.2.cloned.1.call-done = bf16[8192,256]{1,0:T(8,128)(2,1)} async-done(((bf16[256,256]{1,0:T(8,128)(2,1)}), bf16[8192,256]{1,0:T(8,128)(2,1)}) %all-gather.2.cloned.1.call-update) | async-done | bytes 4194320 | tf_op jit(solution)/shard_map/all_gather | solution.py:30
  66.4 7.5 %while.15 = (s32[]{:T(128)}, f32[1,4,256]{2,1,0:T(4,128)S(1)}, f32[1,4,256]{2,1,0:T(4,128)S(1)}, f32[1,4,256,128]{3,2,1,0:T(8,128)S(1)}, s32[]{:T(128)}, /*index...) while((s32[]{:T(128)}, f32[1,4,256]{2,1,0:T(4,128)S(1)}, ...), condition=%wide.region_7.8_spmd.clone, body=%wide.region_4.7_spmd.clone.sunk | while | flops 137039360 | bytes 4923615 | solution.py:63
  66.4 0.8 dynamic_slice.13
  67.2 0.1 compare_and_fusion.2
  67.3 1.2 fusion.31
  68.5 0.2 fusion.33
  68.7 1.4 fusion.34
  70.2 0.8 dynamic_slice.13
  70.9 0.1 compare_and_fusion.2
  71.1 1.2 fusion.31
  72.3 0.2 fusion.33
  72.5 1.4 fusion.34
  73.9 0.2 copy.14
  74.1 10.4 %convolution_convert_fusion = bf16[512,8192]{1,0:T(8,128)(2,1)} fusion(bf16[512,8192]{1,0:T(8,128)(2,1)} %param.15, bf16[256,512]{0,1:T(8,128)(2,1)S(1)} %bitcast.71, s32[256]{0:T(256)S(1)} %multiply_add_fusion), kind=kOutput, calls=%fused_computation.25 | convolution fusion | flops 4433772544 | bytes 17040384 | tf_op jit(solution)/shard_map/dot_general | solution.py:80
  84.5 0.0 copy-start
  84.5 0.0 copy-start.1
  84.5 0.0 reduce-scatter.2.cloned.1.call-update
  84.6 148.4 %reduce-scatter.2.cloned.1.call-done = bf16[64,8192]{1,0:T(8,128)(2,1)} async-done(((bf16[512,8192]{1,0:T(8,128)(2,1)}), bf16[64,8192]{1,0:T(8,128)(2,1)}) %reduce-scatter.2.cloned.1.call-update) | async-done | bytes 1048592 | tf_op jit(solution)/shard_map/reduce_scatter | solution.py:83
  232.9 0.0 copy-done
  232.9 1.7 multiply_reduce_fusion
  234.6 0.0 copy-done.1
  234.6 3.1 %multiply_convert_fusion = (bf16[64,8192]{1,0:T(8,128)(2,1)}, bf16[64,8192]{1,0:T(8,128)(2,1)}) fusion(bf16[64,8192]{1,0:T(8,128)(2,1)} %reduce-scatter.2.cloned.1.call-done, bf16[64,8192]{1,0:T(8,128)(2,1)S(1)} %copy-done, f32[8192]{0:T(1024)S(1)} %copy-done.1, f32[64]{0:T(128)S(1)} %add_rsqrt_fusion), kind=kLoop, calls=%fused_computation.26 | loop fusion | flops 3670016 | bytes 4227328 | tf_op jit(solution)/shard_map/convert_element_type | solution.py:89
  (15 shorter events, 0.2 us)
Async XLA Ops:
  7.2 59.2 %all-gather.2.cloned.1.call-start = ((), (), s32[]{:S(2)}) async-start(), calls=%async_computation.1 | async-start | bytes 4325376 | tf_op jit(solution)/shard_map/all_gather | solution.py:30
  8.8 224.2 %reduce-scatter.2.cloned.1.call-start = ((), (), s32[]{:S(2)}) async-start(), calls=%async_computation.2 | async-start | bytes 9437184 | tf_op jit(solution)/shard_map/reduce_scatter | solution.py:83
  84.5 148.4 %copy-start = (bf16[64,8192]{1,0:T(8,128)(2,1)S(1)}, bf16[64,8192]{1,0:T(8,128)(2,1)}, u32[]{:S(2)}) copy-start(bf16[64,8192]{1,0:T(8,128)(2,1)} %param.16) | copy-start | bytes 3145732
  84.5 150.1 %copy-start.1 = (f32[8192]{0:T(1024)S(1)}, f32[8192]{0:T(1024)}, u32[]{:S(2)}) copy-start(f32[8192]{0:T(1024)} %param.17) | copy-start | bytes 98308
Sparse Core Ops, SparseCore 0:
  11.1 55.2 all-gather.1
  84.7 148.2 reduce-scatter.1

commit v2 on v1

v2 whole, which is shorter than its diff:
```python
import functools
import math

import jax
import jax.numpy as jnp
from jax import lax
from jax.experimental import pallas as pl
from jax.experimental.pallas import tpu as pltpu
from jax.sharding import PartitionSpec as P

HEADS = 32
KV_HEADS = 8
HEAD_DIM = 128
DOC_MOST = 4096


def attention_kernel(
    block_info, q_ref, kv_ref, qseg_ref, kseg_ref, out_ref, max_ref, total_ref, acc_ref, *, window, group
):
    step = pl.program_id(0)
    my_block = block_info[0]
    first_block = block_info[1]
    key_block = my_block - (window - 1) + step
    rows = q_ref.shape[0]
    key_width = kv_ref.shape[0]
    local_heads = acc_ref.shape[0]
    kv_cols = kv_ref.shape[1] // 2
    score_scale = 1.0 / math.sqrt(HEAD_DIM)

    @pl.when(step == 0)
    def _():
        max_ref[...] = jnp.full(max_ref.shape, -1e30, jnp.float32)
        total_ref[...] = jnp.zeros(total_ref.shape, jnp.float32)
        acc_ref[...] = jnp.zeros(acc_ref.shape, jnp.float32)

    @pl.when(key_block >= first_block)
    def _():
        query_pos = my_block * rows + lax.broadcasted_iota(jnp.int32, (rows, 1), 0)
        key_pos = key_block * key_width + lax.broadcasted_iota(jnp.int32, (1, key_width), 1)
        allowed = (qseg_ref[...] == kseg_ref[...]) & (key_pos <= query_pos)
        for head in range(local_heads):
            kv_head = head // group
            keys = kv_ref[:, kv_head * HEAD_DIM:(kv_head + 1) * HEAD_DIM]
            values = kv_ref[:, kv_cols + kv_head * HEAD_DIM:kv_cols + (kv_head + 1) * HEAD_DIM]
            query = q_ref[:, head * HEAD_DIM:(head + 1) * HEAD_DIM]
            scores = (
                lax.dot_general(
                    query, keys, (((1,), (1,)), ((), ())), preferred_element_type=jnp.float32
                )
                * score_scale
            )
            scores = jnp.where(allowed, scores, -1e30)
            running_max = max_ref[head]
            new_max = jnp.maximum(running_max, jnp.max(scores, axis=-1, keepdims=True))
            exponent = jnp.where(allowed, jnp.exp(scores - new_max), 0.0)
            factor = jnp.exp(running_max - new_max)
            total_ref[head] = total_ref[head] * factor + jnp.sum(exponent, axis=-1, keepdims=True)
            acc_ref[head] = acc_ref[head] * factor + jnp.dot(
                exponent.astype(jnp.bfloat16), values, preferred_element_type=jnp.float32
            )
            max_ref[head] = new_max

    @pl.when(step == window - 1)
    def _():
        for head in range(local_heads):
            out_ref[:, head * HEAD_DIM:(head + 1) * HEAD_DIM] = (
                acc_ref[head] / total_ref[head]
            ).astype(out_ref.dtype)


def attend_window(queries, kv_all, query_seg, segments, my_block, first_block, group):
    rows, q_cols = queries.shape
    key_width = rows
    block_count = kv_all.shape[0] // key_width
    window = min(block_count, DOC_MOST // key_width + 1)
    local_heads = q_cols // HEAD_DIM
    block_info = jnp.stack([my_block, first_block]).astype(jnp.int32)

    def kv_map(step, info):
        return (jnp.maximum(info[0] - (window - 1) + step, info[1]), 0)

    def kseg_map(step, info):
        return (0, jnp.maximum(info[0] - (window - 1) + step, info[1]))

    grid_spec = pltpu.PrefetchScalarGridSpec(
        num_scalar_prefetch=1,
        grid=(window,),
        in_specs=[
            pl.BlockSpec((rows, q_cols), lambda step, info: (0, 0)),
            pl.BlockSpec((key_width, kv_all.shape[1]), kv_map),
            pl.BlockSpec((rows, 1), lambda step, info: (0, 0)),
            pl.BlockSpec((1, key_width), kseg_map),
        ],
        out_specs=pl.BlockSpec((rows, q_cols), lambda step, info: (0, 0)),
        scratch_shapes=[
            pltpu.VMEM((local_heads, rows, 1), jnp.float32),
            pltpu.VMEM((local_heads, rows, 1), jnp.float32),
            pltpu.VMEM((local_heads, rows, HEAD_DIM), jnp.float32),
        ],
    )
    kernel = pl.pallas_call(
        functools.partial(attention_kernel, window=window, group=group),
        grid_spec=grid_spec,
        out_shape=jax.ShapeDtypeStruct((rows, q_cols), jnp.bfloat16),
        compiler_params=pltpu.CompilerParams(dimension_semantics=("arbitrary",)),
    )
    return kernel(
        block_info, queries, kv_all, query_seg.reshape(rows, 1), segments.reshape(1, -1)
    )


def on_device(queries, key_rows, value_rows, segments, owner_ids, out_proj, residual, norm_gain):
    rows_here = queries.shape[0]
    kv_local = key_rows.shape[1] // HEAD_DIM
    kv_cols = kv_local * HEAD_DIM
    group_size = HEADS // KV_HEADS
    score_scale = 1.0 / math.sqrt(HEAD_DIM)
    my_block = lax.axis_index("ctx")
    my_start = my_block * rows_here
    query_heads = queries.reshape(rows_here, kv_local, group_size, HEAD_DIM)
    query_pos = my_start + jnp.arange(rows_here, dtype=jnp.int32)
    query_seg = lax.dynamic_slice_in_dim(segments, my_start, rows_here, 0)
    kv_pair = jnp.concatenate([key_rows, value_rows], axis=1)
    kv_all = lax.all_gather(kv_pair, "ctx", axis=0, tiled=True)
    doc_start = jnp.sum((segments < query_seg[0]).astype(jnp.int32))
    first_block = doc_start // rows_here
    attended = attend_window(queries, kv_all, query_seg, segments, my_block, first_block, group_size)
    slot_count = residual.shape[0]
    owner_count = lax.axis_size("tp")
    owners = owner_ids[:, 0]
    onehot = (owners[:, None] == jnp.arange(owner_count, dtype=jnp.int32)[None, :]).astype(
        jnp.int32
    )
    before = jnp.cumsum(onehot, axis=0) - onehot
    row_rank = jnp.sum(before * onehot, axis=1)
    slot_of_token = owners * slot_count + row_rank
    all_slots = jnp.arange(owner_count * slot_count, dtype=jnp.int32)
    select = (slot_of_token[None, :] == all_slots[:, None]).astype(jnp.bfloat16)
    attended_slots = jnp.dot(select, attended, preferred_element_type=jnp.float32).astype(
        jnp.bfloat16
    )
    partial_slots = jnp.dot(attended_slots, out_proj, preferred_element_type=jnp.float32).astype(
        jnp.bfloat16
    )
    owned_rows = lax.psum_scatter(partial_slots, "tp", scatter_dimension=0, tiled=True).astype(
        jnp.float32
    )
    hidden_sum = residual.astype(jnp.float32) + owned_rows
    mean_square = jnp.mean(hidden_sum * hidden_sum, axis=-1, keepdims=True)
    normed = hidden_sum * lax.rsqrt(mean_square + 1e-05) * norm_gain
    return (hidden_sum.astype(jnp.bfloat16), normed.astype(jnp.bfloat16))


def solution(mesh):
    placed = (
        P("ctx", "tp"),
        P("ctx", "tp"),
        P("ctx", "tp"),
        P(),
        P("ctx", None),
        P("tp", None),
        P(("ctx", "tp"), None),
        P(),
    )
    return jax.shard_map(
        on_device,
        mesh=mesh,
        in_specs=placed,
        out_specs=(P(("ctx", "tp"), None), P(("ctx", "tp"), None)),
        check_vma=False,
    )
```

time: 248 us -> 224 us (0.903); the launches traced: 245 us -> 223 us
  waiting for transfers between devices: 196 us -> 177 us
  Pallas kernels: 0 us -> 8.2 us
  matrix products: 15.5 us -> 9.26 us
    reduce_scatter x1, waiting for transfers between devices: 148 us -> 129 us  [on_device(): lax.psum_scatter(partial_slots, 'tp', scatter_dimension=0, tiled=True)]
    pallas_call x0 -> x1, Pallas kernels: none -> 8.2 us  [attend_window(): kernel(block_info, queries, kv_all, query_seg.reshape(rows, 1), segments....]
    dot_general x4 -> x0, matrix products: 5.06 us -> none  [the longest x2 2.71 us: update(): jnp.einsum('kgts,skd->kgtd', exponent.astype(jnp.bfloat16), value_block,...]
where the time goes in v2:
time: 224 us; the launch traced here: 223 us
  waiting for transfers between devices  177 us (79%)
  between operations  16.5 us (7%)
  other arithmetic  10.5 us (5%)
  matrix products  9.26 us (4%)
  Pallas kernels  8.2 us (4%)
  local copies, waits for them, and re-layouts  2.32 us (1%)
    reduce_scatter x1, waiting for transfers between devices, on_device(): lax.psum_scatter(partial_slots, 'tp', scatter_dimension=0, tiled=True)  129 us
    all_gather x1, waiting for transfers between devices, on_device(): kv_all = lax.all_gather(kv_pair, 'ctx', axis=0, tiled=True)  47.3 us
    dot_general x1, matrix products, on_device(): jnp.dot(attended_slots, out_proj, preferred_element_type=jnp.float32)  9.26 us
    pallas_call x1, Pallas kernels, attend_window(): kernel(block_info, queries, kv_all, query_seg.reshape(rows, 1), segments....  8.2 us
  transfers between devices with their start and end apart: 2, of which 2 were waited for; matrix products, arithmetic and copies ran while one was open for 3% of the time, Pallas kernels for 0%

profile of v2, /device:TPU:1, one launch (start us, length us, event | category | flops | bytes accessed | tf_op | source)
XLA Modules:
  0.0 223.4 jit_solution(12272902439154503121)
XLA Ops:
  7.2 0.0 all-gather.2.cloned.1.call-start
  7.2 1.5 pad_maximum_fusion
  8.8 0.0 all-gather.2.cloned.1.call-update
  8.8 0.0 reduce-scatter.2.cloned.1.call-start
  8.8 0.8 dynamic_slice.3
  9.6 0.5 slice.11
  10.1 2.1 convert_reduce_fusion
  14.6 0.7 fusion.5
  15.3 0.6 reduce-window.6
  15.9 0.2 slice_reduce_fusion
  16.1 0.8 copy.10.qseg_ref
  17.0 0.6 pad_add_fusion.block_info
  17.6 0.8 fusion.4
  18.3 0.7 multiply_add_fusion
  19.0 47.3 %all-gather.2.cloned.1.call-done.kv_ref = bf16[8192,256]{1,0:T(8,128)(2,1)} async-done(((bf16[256,256]{1,0:T(8,128)(2,1)}), bf16[8192,256]{1,0:T(8,128)(2,1)}) %all-gather.2.cloned.1.call-update) | async-done | bytes 4194320 | tf_op jit(solution)/shard_map/all_gather | solution.py:124
  66.4 8.2 %shard_map.95 = bf16[256,512]{1,0:T(8,128)(2,1)} custom-call(s32[2]{0:T(128)} %pad_add_fusion.block_info, bf16[256,512]{1,0:T(8,128)(2,1)} %q_ref.1, bf16[8192,256]{1,0:T(8,128)(2,1)} %all-gather.2.cloned.1.call-done.kv_ref, s32[256,1]{1,0:T(8,128)} %copy.10.qseg_ref, s32[1,8192]{1,0:T(1,128)} %bitcast.17), custom_call_target="tpu_custom_call" | custom-call | tf_op jit(solution)/shard_map/pallas_call | solution.py:107
  74.6 9.3 %convolution_convert_fusion = bf16[512,8192]{1,0:T(8,128)(2,1)} fusion(bf16[512,8192]{1,0:T(8,128)(2,1)} %param.13, bf16[256,512]{1,0:T(8,128)(2,1)} %shard_map.95, s32[256]{0:T(256)S(1)} %multiply_add_fusion), kind=kOutput, calls=%fused_computation | convolution fusion | flops 4433772544 | bytes 17040384 | tf_op jit(solution)/shard_map/dot_general | solution.py:142
  83.8 0.0 copy-start
  83.8 0.0 reduce-scatter.2.cloned.1.call-update
  83.8 0.0 copy-start.2
  83.9 129.1 %reduce-scatter.2.cloned.1.call-done = bf16[64,8192]{1,0:T(8,128)(2,1)} async-done(((bf16[512,8192]{1,0:T(8,128)(2,1)}), bf16[64,8192]{1,0:T(8,128)(2,1)}) %reduce-scatter.2.cloned.1.call-update) | async-done | bytes 1048592 | tf_op jit(solution)/shard_map/reduce_scatter | solution.py:145
  213.0 0.0 copy-done
  213.0 0.0 copy-start.1
  213.0 1.8 multiply_reduce_fusion
  214.8 0.0 copy-done.2
  214.8 0.0 copy-done.1
  214.8 1.8 multiply_convert_fusion
  (3 shorter events, 0.0 us)
Async XLA Ops:
  7.2 59.2 %all-gather.2.cloned.1.call-start = ((), (), s32[]{:S(2)}) async-start(), calls=%async_computation.1 | async-start | bytes 4325376 | tf_op jit(solution)/shard_map/all_gather | solution.py:124
  8.8 204.2 %reduce-scatter.2.cloned.1.call-start = ((), (), s32[]{:S(2)}) async-start(), calls=%async_computation.2 | async-start | bytes 9437184 | tf_op jit(solution)/shard_map/reduce_scatter | solution.py:145
  83.8 129.2 %copy-start = (bf16[64,8192]{1,0:T(8,128)(2,1)S(1)}, bf16[64,8192]{1,0:T(8,128)(2,1)}, u32[]{:S(2)}) copy-start(bf16[64,8192]{1,0:T(8,128)(2,1)} %param.14) | copy-start | bytes 3145732
  83.8 130.9 %copy-start.2 = (f32[8192]{0:T(1024)S(1)}, f32[8192]{0:T(1024)}, u32[]{:S(2)}) copy-start(f32[8192]{0:T(1024)} %param.15) | copy-start | bytes 98308
  213.0 1.8 copy-start.1
Sparse Core Ops, SparseCore 0:
  11.1 55.2 all-gather.1
  84.0 128.9 reduce-scatter.1

commit v3 on v2

--- a/solution.py
+++ b/solution.py
@@ -68,16 +68,14 @@
             ).astype(out_ref.dtype)
 
 
-def attend_window(queries, kv_all, query_seg, segments, my_block, first_block, group):
+def attend_window(queries, kv_all, query_seg, segments, my_block, first_block, group, window):
     rows, q_cols = queries.shape
     key_width = rows
-    block_count = kv_all.shape[0] // key_width
-    window = min(block_count, DOC_MOST // key_width + 1)
     local_heads = q_cols // HEAD_DIM
     block_info = jnp.stack([my_block, first_block]).astype(jnp.int32)
 
     def kv_map(step, info):
-        return (jnp.maximum(info[0] - (window - 1) + step, info[1]), 0)
+        return (jnp.maximum(step, info[1] - info[0] + (window - 1)), 0)
 
     def kseg_map(step, info):
         return (0, jnp.maximum(info[0] - (window - 1) + step, info[1]))
@@ -121,10 +119,20 @@
     query_pos = my_start + jnp.arange(rows_here, dtype=jnp.int32)
     query_seg = lax.dynamic_slice_in_dim(segments, my_start, rows_here, 0)
     kv_pair = jnp.concatenate([key_rows, value_rows], axis=1)
-    kv_all = lax.all_gather(kv_pair, "ctx", axis=0, tiled=True)
+    block_total = lax.axis_size("ctx")
+    window = min(block_total, DOC_MOST // rows_here + 1)
+    pieces = []
+    for distance in range(window - 1, 0, -1):
+        pairs = [(source, source + distance) for source in range(block_total - distance)]
+        pieces.append(lax.ppermute(kv_pair, "ctx", pairs))
+    pieces.append(kv_pair)
+    kv_window = jnp.concatenate(pieces, axis=0)
     doc_start = jnp.sum((segments < query_seg[0]).astype(jnp.int32))
     first_block = doc_start // rows_here
-    attended = attend_window(queries, kv_all, query_seg, segments, my_block, first_block, group_size)
+    first_block = jnp.maximum(first_block, my_block - (window - 1))
+    attended = attend_window(
+        queries, kv_window, query_seg, segments, my_block, first_block, group_size, window
+    )
     slot_count = residual.shape[0]
     owner_count = lax.axis_size("tp")
     owners = owner_ids[:, 0]

time: 224 us -> 251 us (1.12)
  starting transfers between devices: 0.08 us -> 62.5 us
  waiting for transfers between devices: 177 us -> 140 us
  local copies, waits for them, and re-layouts: 2.32 us -> 5.6 us
    ppermute x0 -> x16, starting transfers between devices: none -> 62.4 us  [on_device(): pieces.append(lax.ppermute(kv_pair, 'ctx', pairs))]
    all_gather x1 -> x0, waiting for transfers between devices: 47.3 us -> none  [on_device(): kv_all = lax.all_gather(kv_pair, 'ctx', axis=0, tiled=True)]
    reduce_scatter x1, waiting for transfers between devices: 129 us -> 135 us  [on_device(): lax.psum_scatter(partial_slots, 'tp', scatter_dimension=0, tiled=True)]
    ppermute x0 -> x16, waiting for transfers between devices: none -> 5.03 us  [on_device(): pieces.append(lax.ppermute(kv_pair, 'ctx', pairs))]
  transfers between devices with their start and end apart: 2 -> 17, of which waited for: 2 -> 6; matrix products, arithmetic and copies ran while one was open for 3% -> 3% of each run, Pallas kernels for 0% -> 0%
where the time goes in v3:
time: 251 us
  waiting for transfers between devices  140 us (56%)
  starting transfers between devices  62.5 us (25%)
  between operations  16.7 us (7%)
  matrix products  9.19 us (4%)
  other arithmetic  8.94 us (4%)
  Pallas kernels  8.26 us (3%)
  local copies, waits for them, and re-layouts  5.6 us (2%)
    reduce_scatter x1, waiting for transfers between devices, on_device(): lax.psum_scatter(partial_slots, 'tp', scatter_dimension=0, tiled=True)  135 us
    ppermute x16, starting transfers between devices, on_device(): pieces.append(lax.ppermute(kv_pair, 'ctx', pairs))  62.4 us
    dot_general x1, matrix products, on_device(): jnp.dot(attended_slots, out_proj, preferred_element_type=jnp.float32)  9.19 us
    pallas_call x1, Pallas kernels, attend_window(): kernel(block_info, queries, kv_all, query_seg.reshape(rows, 1), segments....  8.26 us
    ppermute x16, waiting for transfers between devices, on_device(): pieces.append(lax.ppermute(kv_pair, 'ctx', pairs))  5.03 us
  transfers between devices with their start and end apart: 17, of which 6 were waited for; matrix products, arithmetic and copies ran while one was open for 3% of the time, Pallas kernels for 0%

profile of v3, /device:TPU:1, one launch (start us, length us, event | category | flops | bytes accessed | tf_op | source)
XLA Modules:
  0.0 251.1 jit_solution(2851627184745354240)
XLA Ops:
  7.2 0.0 reduce-scatter.2.cloned.1.call-start
  7.2 0.9 constant_dynamic-update-slice_fusion.1
  8.1 0.9 constant_dynamic-update-slice_fusion
  8.9 4.5 %collective-permute-start.15 = (bf16[256,256]{1,0:T(8,128)(2,1)S(1)}, bf16[256,256]{1,0:T(8,128)(2,1)S(1)}, u32[]{:S(2)}, u32[]{:S(2)}) collective-permute-start(bf16[256,256]{1,0:T(8,128)(2,1)S(1)} %constant_dynamic-update-slice_fusion), channel_id=1, source_target_pairs={{0,8},{8,16},{16,24},{24,32},{32,40},{40,48},{48,56},{56,64},{64,7... | collective-permute-start | bytes 393224 | tf_op jit(solution)/shard_map/ppermute | solution.py:127
  13.4 3.1 %collective-permute-start.14 = (bf16[256,256]{1,0:T(8,128)(2,1)S(1)}, bf16[256,256]{1,0:T(8,128)(2,1)S(1)}, u32[]{:S(2)}, u32[]{:S(2)}) collective-permute-start(bf16[256,256]{1,0:T(8,128)(2,1)S(1)} %constant_dynamic-update-slice_fusion), channel_id=1, source_target_pairs={{0,16},{8,24},{16,32},{24,40},{32,48},{40,56},{48,64},{56,72},{64,... | collective-permute-start | bytes 393224 | tf_op jit(solution)/shard_map/ppermute | solution.py:127
  16.6 3.4 %collective-permute-start.13 = (bf16[256,256]{1,0:T(8,128)(2,1)S(1)}, bf16[256,256]{1,0:T(8,128)(2,1)S(1)}, u32[]{:S(2)}, u32[]{:S(2)}) collective-permute-start(bf16[256,256]{1,0:T(8,128)(2,1)S(1)} %constant_dynamic-update-slice_fusion), channel_id=1, source_target_pairs={{0,24},{8,32},{16,40},{24,48},{32,56},{40,64},{48,72},{56,80},{64,... | collective-permute-start | bytes 393224 | tf_op jit(solution)/shard_map/ppermute | solution.py:127
  20.0 4.5 %collective-permute-start.1 = (bf16[256,256]{1,0:T(8,128)(2,1)S(1)}, bf16[256,256]{1,0:T(8,128)(2,1)S(1)}, u32[]{:S(2)}, u32[]{:S(2)}) collective-permute-start(bf16[256,256]{1,0:T(8,128)(2,1)S(1)} %constant_dynamic-update-slice_fusion), channel_id=1, source_target_pairs={{0,120},{8,128},{16,136},{24,144},{32,152},{40,160},{48,168},{56,1... | collective-permute-start | bytes 393224 | tf_op jit(solution)/shard_map/ppermute | solution.py:127
  24.5 1.6 collective-permute-start
  26.1 0.8 dynamic_slice.3
  26.9 0.5 slice.11
  27.4 0.7 fusion.5
  28.1 0.6 reduce-window.6
  28.7 0.2 slice_reduce_fusion
  29.0 0.8 fusion.4
  29.7 0.7 multiply_add_fusion
  30.4 2.0 convert_reduce_fusion
  34.7 0.6 pad_add_fusion.block_info
  35.3 0.8 copy.10.qseg_ref
  36.1 0.0 collective-permute-done
  36.1 2.2 collective-permute-start.2
  38.3 0.0 collective-permute-done.1
  38.4 1.6 collective-permute-start.3
  40.0 1.4 collective-permute-done.2
  41.4 1.4 collective-permute-start.4
  42.8 0.9 collective-permute-done.3
  43.7 9.4 %collective-permute-start.5 = (bf16[256,256]{1,0:T(8,128)(2,1)S(1)}, bf16[256,256]{1,0:T(8,128)(2,1)S(1)}, u32[]{:S(2)}, u32[]{:S(2)}) collective-permute-start(bf16[256,256]{1,0:T(8,128)(2,1)S(1)} %constant_dynamic-update-slice_fusion), channel_id=1, source_target_pairs={{0,88},{8,96},{16,104},{24,112},{32,120},{40,128},{48,136},{56,144... | collective-permute-start | bytes 393224 | tf_op jit(solution)/shard_map/ppermute | solution.py:127
  53.1 0.0 collective-permute-done.4
  53.2 1.3 collective-permute-start.6
  54.5 0.6 collective-permute-done.5
  55.0 7.6 %collective-permute-start.7 = (bf16[256,256]{1,0:T(8,128)(2,1)S(1)}, bf16[256,256]{1,0:T(8,128)(2,1)S(1)}, u32[]{:S(2)}, u32[]{:S(2)}) collective-permute-start(bf16[256,256]{1,0:T(8,128)(2,1)S(1)} %constant_dynamic-update-slice_fusion), channel_id=1, source_target_pairs={{0,72},{8,80},{16,88},{24,96},{32,104},{40,112},{48,120},{56,128},... | collective-permute-start | bytes 393224 | tf_op jit(solution)/shard_map/ppermute | solution.py:127
  62.7 1.9 collective-permute-start.8
  64.7 6.6 %collective-permute-start.9 = (bf16[256,256]{1,0:T(8,128)(2,1)S(1)}, bf16[256,256]{1,0:T(8,128)(2,1)S(1)}, u32[]{:S(2)}, u32[]{:S(2)}) collective-permute-start(bf16[256,256]{1,0:T(8,128)(2,1)S(1)} %constant_dynamic-update-slice_fusion), channel_id=1, source_target_pairs={{0,56},{8,64},{16,72},{24,80},{32,88},{40,96},{48,104},{56,112},{6... | collective-permute-start | bytes 393224 | tf_op jit(solution)/shard_map/ppermute | solution.py:127
  71.3 1.7 collective-permute-start.10
  73.0 0.2 collective-permute-done.9
  73.2 3.8 %collective-permute-start.11 = (bf16[256,256]{1,0:T(8,128)(2,1)S(1)}, bf16[256,256]{1,0:T(8,128)(2,1)S(1)}, u32[]{:S(2)}, u32[]{:S(2)}) collective-permute-start(bf16[256,256]{1,0:T(8,128)(2,1)S(1)} %constant_dynamic-update-slice_fusion), channel_id=1, source_target_pairs={{0,40},{8,48},{16,56},{24,64},{32,72},{40,80},{48,88},{56,96},{64,... | collective-permute-start | bytes 393224 | tf_op jit(solution)/shard_map/ppermute | solution.py:127
  77.0 0.0 collective-permute-done.10
  77.0 7.9 %collective-permute-start.12 = (bf16[256,256]{1,0:T(8,128)(2,1)S(1)}, bf16[256,256]{1,0:T(8,128)(2,1)S(1)}, u32[]{:S(2)}, u32[]{:S(2)}) collective-permute-start(bf16[256,256]{1,0:T(8,128)(2,1)S(1)} %constant_dynamic-update-slice_fusion), channel_id=1, source_target_pairs={{0,32},{8,40},{16,48},{24,56},{32,64},{40,72},{48,80},{56,88},{64,... | collective-permute-start | bytes 393224 | tf_op jit(solution)/shard_map/ppermute | solution.py:127
  84.9 0.0 collective-permute-done.11
  84.9 1.9 collective-permute-done.12
  86.8 0.0 collective-permute-done.13
  86.9 0.0 collective-permute-done.15
  87.0 1.4 copy-done.2
  88.3 8.3 %shard_map.95 = bf16[256,512]{1,0:T(8,128)(2,1)} custom-call(s32[2]{0:T(128)} %pad_add_fusion.block_info, bf16[256,512]{1,0:T(8,128)(2,1)} %q_ref.1, bf16[4352,256]{1,0:T(8,128)(2,1)} %copy-done.2, s32[256,1]{1,0:T(8,128)} %copy.10.qseg_ref, s32[1,8192]{1,0:T(1,128)} %bitcast.17), custom_call_target="tpu_custom_call" | custom-call | tf_op jit(solution)/shard_map/pallas_call | solution.py:105
  96.6 9.2 %convolution_convert_fusion = bf16[512,8192]{1,0:T(8,128)(2,1)} fusion(bf16[512,8192]{1,0:T(8,128)(2,1)} %param.13, bf16[256,512]{1,0:T(8,128)(2,1)} %shard_map.95, s32[256]{0:T(256)S(1)} %multiply_add_fusion), kind=kOutput, calls=%fused_computation | convolution fusion | flops 4433772544 | bytes 17040384 | tf_op jit(solution)/shard_map/dot_general | solution.py:150
  105.8 0.0 reduce-scatter.2.cloned.1.call-update
  105.8 134.9 %reduce-scatter.2.cloned.1.call-done = bf16[64,8192]{1,0:T(8,128)(2,1)} async-done(((bf16[512,8192]{1,0:T(8,128)(2,1)}), bf16[64,8192]{1,0:T(8,128)(2,1)}) %reduce-scatter.2.cloned.1.call-update) | async-done | bytes 1048592 | tf_op jit(solution)/shard_map/reduce_scatter | solution.py:153
  240.7 1.8 multiply_reduce_fusion
  242.5 1.8 multiply_convert_fusion
  (36 shorter events, 0.3 us)
Async XLA Ops:
  7.2 233.6 %reduce-scatter.2.cloned.1.call-start = ((), (), s32[]{:S(2)}) async-start(), calls=%async_computation.1 | async-start | bytes 9437184 | tf_op jit(solution)/shard_map/reduce_scatter | solution.py:153
  8.9 78.0 %collective-permute-start.15 = (bf16[256,256]{1,0:T(8,128)(2,1)S(1)}, bf16[256,256]{1,0:T(8,128)(2,1)S(1)}, u32[]{:S(2)}, u32[]{:S(2)}) collective-permute-start(bf16[256,256]{1,0:T(8,128)(2,1)S(1)} %constant_dynamic-update-slice_fusion), channel_id=1, source_target_pairs={{0,8},{8,16},{16,24},{24,32},{32,40},{40,48},{48,56},{56,64},{64,7... | collective-permute-start | bytes 393224 | tf_op jit(solution)/shard_map/ppermute | solution.py:127
  13.4 73.4 %collective-permute-start.14 = (bf16[256,256]{1,0:T(8,128)(2,1)S(1)}, bf16[256,256]{1,0:T(8,128)(2,1)S(1)}, u32[]{:S(2)}, u32[]{:S(2)}) collective-permute-start(bf16[256,256]{1,0:T(8,128)(2,1)S(1)} %constant_dynamic-update-slice_fusion), channel_id=1, source_target_pairs={{0,16},{8,24},{16,32},{24,40},{32,48},{40,56},{48,64},{56,72},{64,... | collective-permute-start | bytes 393224 | tf_op jit(solution)/shard_map/ppermute | solution.py:127
  16.6 70.3 %collective-permute-start.13 = (bf16[256,256]{1,0:T(8,128)(2,1)S(1)}, bf16[256,256]{1,0:T(8,128)(2,1)S(1)}, u32[]{:S(2)}, u32[]{:S(2)}) collective-permute-start(bf16[256,256]{1,0:T(8,128)(2,1)S(1)} %constant_dynamic-update-slice_fusion), channel_id=1, source_target_pairs={{0,24},{8,32},{16,40},{24,48},{32,56},{40,64},{48,72},{56,80},{64,... | collective-permute-start | bytes 393224 | tf_op jit(solution)/shard_map/ppermute | solution.py:127
  20.0 18.3 %collective-permute-start.1 = (bf16[256,256]{1,0:T(8,128)(2,1)S(1)}, bf16[256,256]{1,0:T(8,128)(2,1)S(1)}, u32[]{:S(2)}, u32[]{:S(2)}) collective-permute-start(bf16[256,256]{1,0:T(8,128)(2,1)S(1)} %constant_dynamic-update-slice_fusion), channel_id=1, source_target_pairs={{0,120},{8,128},{16,136},{24,144},{32,152},{40,160},{48,168},{56,1... | collective-permute-start | bytes 393224 | tf_op jit(solution)/shard_map/ppermute | solution.py:127
  24.5 11.6 %collective-permute-start = (bf16[256,256]{1,0:T(8,128)(2,1)S(1)}, bf16[256,256]{1,0:T(8,128)(2,1)S(1)}, u32[]{:S(2)}, u32[]{:S(2)}) collective-permute-start(bf16[256,256]{1,0:T(8,128)(2,1)S(1)} %constant_dynamic-update-slice_fusion), channel_id=1, source_target_pairs={{0,128},{8,136},{16,144},{24,152},{32,160},{40,168},{48,176},{56,1... | collective-permute-start | bytes 393224 | tf_op jit(solution)/shard_map/ppermute | solution.py:127
  27.4 59.5 %copy-start.3 = (bf16[256,128]{1,0:T(8,128)(2,1)S(1)}, bf16[256,128]{1,0:T(8,128)(2,1)}, u32[]{:S(2)}) copy-start(bf16[256,128]{1,0:T(8,128)(2,1)} %param.9) | copy-start | bytes 196612
  35.3 51.6 %copy-start.4 = (bf16[256,128]{1,0:T(8,128)(2,1)S(1)}, bf16[256,128]{1,0:T(8,128)(2,1)}, u32[]{:S(2)}) copy-start(bf16[256,128]{1,0:T(8,128)(2,1)} %param.10) | copy-start | bytes 196612
  36.1 5.3 %collective-permute-start.2 = (bf16[256,256]{1,0:T(8,128)(2,1)S(1)}, bf16[256,256]{1,0:T(8,128)(2,1)S(1)}, u32[]{:S(2)}, u32[]{:S(2)}) collective-permute-start(bf16[256,256]{1,0:T(8,128)(2,1)S(1)} %constant_dynamic-update-slice_fusion), channel_id=1, source_target_pairs={{0,112},{8,120},{16,128},{24,136},{32,144},{40,152},{48,160},{56,1... | collective-permute-start | bytes 393224 | tf_op jit(solution)/shard_map/ppermute | solution.py:127
  38.4 5.4 %collective-permute-start.3 = (bf16[256,256]{1,0:T(8,128)(2,1)S(1)}, bf16[256,256]{1,0:T(8,128)(2,1)S(1)}, u32[]{:S(2)}, u32[]{:S(2)}) collective-permute-start(bf16[256,256]{1,0:T(8,128)(2,1)S(1)} %constant_dynamic-update-slice_fusion), channel_id=1, source_target_pairs={{0,104},{8,112},{16,120},{24,128},{32,136},{40,144},{48,152},{56,1... | collective-permute-start | bytes 393224 | tf_op jit(solution)/shard_map/ppermute | solution.py:127
  41.4 11.7 %collective-permute-start.4 = (bf16[256,256]{1,0:T(8,128)(2,1)S(1)}, bf16[256,256]{1,0:T(8,128)(2,1)S(1)}, u32[]{:S(2)}, u32[]{:S(2)}) collective-permute-start(bf16[256,256]{1,0:T(8,128)(2,1)S(1)} %constant_dynamic-update-slice_fusion), channel_id=1, source_target_pairs={{0,96},{8,104},{16,112},{24,120},{32,128},{40,136},{48,144},{56,15... | collective-permute-start | bytes 393224 | tf_op jit(solution)/shard_map/ppermute | solution.py:127
  43.7 11.3 %collective-permute-start.5 = (bf16[256,256]{1,0:T(8,128)(2,1)S(1)}, bf16[256,256]{1,0:T(8,128)(2,1)S(1)}, u32[]{:S(2)}, u32[]{:S(2)}) collective-permute-start(bf16[256,256]{1,0:T(8,128)(2,1)S(1)} %constant_dynamic-update-slice_fusion), channel_id=1, source_target_pairs={{0,88},{8,96},{16,104},{24,112},{32,120},{40,128},{48,136},{56,144... | collective-permute-start | bytes 393224 | tf_op jit(solution)/shard_map/ppermute | solution.py:127
  53.2 9.5 %collective-permute-start.6 = (bf16[256,256]{1,0:T(8,128)(2,1)S(1)}, bf16[256,256]{1,0:T(8,128)(2,1)S(1)}, u32[]{:S(2)}, u32[]{:S(2)}) collective-permute-start(bf16[256,256]{1,0:T(8,128)(2,1)S(1)} %constant_dynamic-update-slice_fusion), channel_id=1, source_target_pairs={{0,80},{8,88},{16,96},{24,104},{32,112},{40,120},{48,128},{56,136}... | collective-permute-start | bytes 393224 | tf_op jit(solution)/shard_map/ppermute | solution.py:127
  55.0 9.6 %collective-permute-start.7 = (bf16[256,256]{1,0:T(8,128)(2,1)S(1)}, bf16[256,256]{1,0:T(8,128)(2,1)S(1)}, u32[]{:S(2)}, u32[]{:S(2)}) collective-permute-start(bf16[256,256]{1,0:T(8,128)(2,1)S(1)} %constant_dynamic-update-slice_fusion), channel_id=1, source_target_pairs={{0,72},{8,80},{16,88},{24,96},{32,104},{40,112},{48,120},{56,128},... | collective-permute-start | bytes 393224 | tf_op jit(solution)/shard_map/ppermute | solution.py:127
  62.7 8.6 %collective-permute-start.8 = (bf16[256,256]{1,0:T(8,128)(2,1)S(1)}, bf16[256,256]{1,0:T(8,128)(2,1)S(1)}, u32[]{:S(2)}, u32[]{:S(2)}) collective-permute-start(bf16[256,256]{1,0:T(8,128)(2,1)S(1)} %constant_dynamic-update-slice_fusion), channel_id=1, source_target_pairs={{0,64},{8,72},{16,80},{24,88},{32,96},{40,104},{48,112},{56,120},{... | collective-permute-start | bytes 393224 | tf_op jit(solution)/shard_map/ppermute | solution.py:127
  64.7 8.6 %collective-permute-start.9 = (bf16[256,256]{1,0:T(8,128)(2,1)S(1)}, bf16[256,256]{1,0:T(8,128)(2,1)S(1)}, u32[]{:S(2)}, u32[]{:S(2)}) collective-permute-start(bf16[256,256]{1,0:T(8,128)(2,1)S(1)} %constant_dynamic-update-slice_fusion), channel_id=1, source_target_pairs={{0,56},{8,64},{16,72},{24,80},{32,88},{40,96},{48,104},{56,112},{6... | collective-permute-start | bytes 393224 | tf_op jit(solution)/shard_map/ppermute | solution.py:127
  71.3 5.7 %collective-permute-start.10 = (bf16[256,256]{1,0:T(8,128)(2,1)S(1)}, bf16[256,256]{1,0:T(8,128)(2,1)S(1)}, u32[]{:S(2)}, u32[]{:S(2)}) collective-permute-start(bf16[256,256]{1,0:T(8,128)(2,1)S(1)} %constant_dynamic-update-slice_fusion), channel_id=1, source_target_pairs={{0,48},{8,56},{16,64},{24,72},{32,80},{40,88},{48,96},{56,104},{64... | collective-permute-start | bytes 393224 | tf_op jit(solution)/shard_map/ppermute | solution.py:127
  73.2 11.7 %collective-permute-start.11 = (bf16[256,256]{1,0:T(8,128)(2,1)S(1)}, bf16[256,256]{1,0:T(8,128)(2,1)S(1)}, u32[]{:S(2)}, u32[]{:S(2)}) collective-permute-start(bf16[256,256]{1,0:T(8,128)(2,1)S(1)} %constant_dynamic-update-slice_fusion), channel_id=1, source_target_pairs={{0,40},{8,48},{16,56},{24,64},{32,72},{40,80},{48,88},{56,96},{64,... | collective-permute-start | bytes 393224 | tf_op jit(solution)/shard_map/ppermute | solution.py:127
  77.0 9.8 %collective-permute-start.12 = (bf16[256,256]{1,0:T(8,128)(2,1)S(1)}, bf16[256,256]{1,0:T(8,128)(2,1)S(1)}, u32[]{:S(2)}, u32[]{:S(2)}) collective-permute-start(bf16[256,256]{1,0:T(8,128)(2,1)S(1)} %constant_dynamic-update-slice_fusion), channel_id=1, source_target_pairs={{0,32},{8,40},{16,48},{24,56},{32,64},{40,72},{48,80},{56,88},{64,... | collective-permute-start | bytes 393224 | tf_op jit(solution)/shard_map/ppermute | solution.py:127
  87.0 1.4 copy-start.2
  105.8 134.9 %copy-start = (bf16[64,8192]{1,0:T(8,128)(2,1)S(1)}, bf16[64,8192]{1,0:T(8,128)(2,1)}, u32[]{:S(2)}) copy-start(bf16[64,8192]{1,0:T(8,128)(2,1)} %param.14) | copy-start | bytes 3145732
  105.8 136.7 %copy-start.5 = (f32[8192]{0:T(1024)S(1)}, f32[8192]{0:T(1024)}, u32[]{:S(2)}) copy-start(f32[8192]{0:T(1024)} %param.15) | copy-start | bytes 98308
  240.7 1.8 copy-start.1
Sparse Core Ops, SparseCore 0:
  105.9 134.7 reduce-scatter.1

commit v4 on v2

--- a/solution.py
+++ b/solution.py
@@ -12,6 +12,9 @@
 KV_HEADS = 8
 HEAD_DIM = 128
 DOC_MOST = 4096
+CHIP_AXES = ("ctx_y", "ctx_x")
+CORE_AXIS = "ctx_core"
+CTX_AXES = CHIP_AXES + (CORE_AXIS,)
 
 
 def attention_kernel(
@@ -115,13 +118,18 @@
     kv_cols = kv_local * HEAD_DIM
     group_size = HEADS // KV_HEADS
     score_scale = 1.0 / math.sqrt(HEAD_DIM)
-    my_block = lax.axis_index("ctx")
+    my_block = lax.axis_index(CTX_AXES)
     my_start = my_block * rows_here
     query_heads = queries.reshape(rows_here, kv_local, group_size, HEAD_DIM)
     query_pos = my_start + jnp.arange(rows_here, dtype=jnp.int32)
     query_seg = lax.dynamic_slice_in_dim(segments, my_start, rows_here, 0)
     kv_pair = jnp.concatenate([key_rows, value_rows], axis=1)
-    kv_all = lax.all_gather(kv_pair, "ctx", axis=0, tiled=True)
+    chip_pair = lax.all_gather(kv_pair, CORE_AXIS, axis=0, tiled=True)
+    core = lax.axis_index(CORE_AXIS)
+    half = lax.dynamic_slice_in_dim(chip_pair, core * kv_cols, kv_cols, 1)
+    half_all = lax.all_gather(half, CHIP_AXES, axis=0, tiled=True)
+    both = lax.all_gather(half_all, CORE_AXIS, axis=1, tiled=True)
+    kv_all = both
     doc_start = jnp.sum((segments < query_seg[0]).astype(jnp.int32))
     first_block = doc_start // rows_here
     attended = attend_window(queries, kv_all, query_seg, segments, my_block, first_block, group_size)
@@ -152,20 +160,28 @@
 
 
 def solution(mesh):
+    ctx_size = mesh.shape["ctx"]
+    cores = 2 if ctx_size % 2 == 0 else 1
+    chips = ctx_size // cores
+    rows_of_chips = math.isqrt(chips) if math.isqrt(chips) ** 2 == chips else 1
+    split_shape = (rows_of_chips, chips // rows_of_chips, cores, mesh.shape["tp"])
+    split_mesh = jax.sharding.Mesh(
+        mesh.devices.reshape(split_shape), CTX_AXES + ("tp",)
+    )
     placed = (
-        P("ctx", "tp"),
-        P("ctx", "tp"),
-        P("ctx", "tp"),
+        P(CTX_AXES, "tp"),
+        P(CTX_AXES, "tp"),
+        P(CTX_AXES, "tp"),
         P(),
-        P("ctx", None),
+        P(CTX_AXES, None),
         P("tp", None),
-        P(("ctx", "tp"), None),
+        P(CTX_AXES + ("tp",), None),
         P(),
     )
     return jax.shard_map(
         on_device,
-        mesh=mesh,
+        mesh=split_mesh,
         in_specs=placed,
-        out_specs=(P(("ctx", "tp"), None), P(("ctx", "tp"), None)),
+        out_specs=(P(CTX_AXES + ("tp",), None), P(CTX_AXES + ("tp",), None)),
         check_vma=False,
     )

time: 224 us -> 243 us (1.085)
  waiting for transfers between devices: 177 us -> 194 us
  blocking collectives: 0 us -> 4.83 us
  other arithmetic: 10.5 us -> 7 us
    all_gather x1 -> x2, waiting for transfers between devices: 47.3 us -> 64.4 us  [the longest x1 49.5 us: on_device(): half_all = lax.all_gather(half, CHIP_AXES, axis=0, tiled=True)]
    all_gather x0 -> x1, blocking collectives: none -> 4.83 us  [on_device(): chip_pair = lax.all_gather(kv_pair, CORE_AXIS, axis=0, tiled=True)]
  transfers between devices with their start and end apart: 2 -> 3, of which waited for: 2 -> 3; matrix products, arithmetic and copies ran while one was open for 3% -> 2% of each run, Pallas kernels for 0% -> 0%
where the time goes in v4:
time: 243 us; the launch traced here: 242 us
  waiting for transfers between devices  194 us (80%)
  between operations  16.2 us (7%)
  matrix products  9.25 us (4%)
  Pallas kernels  8.2 us (3%)
  other arithmetic  7 us (3%)
  blocking collectives  4.83 us (2%)
    reduce_scatter x1, waiting for transfers between devices, on_device(): lax.psum_scatter(partial_slots, 'tp', scatter_dimension=0, tiled=True)  129 us
    all_gather x1, waiting for transfers between devices, on_device(): half_all = lax.all_gather(half, CHIP_AXES, axis=0, tiled=True)  49.5 us
    all_gather x1, waiting for transfers between devices, on_device(): both = lax.all_gather(half_all, CORE_AXIS, axis=1, tiled=True)  15 us
    dot_general x1, matrix products, on_device(): jnp.dot(attended_slots, out_proj, preferred_element_type=jnp.float32)  9.25 us
    pallas_call x1, Pallas kernels, attend_window(): kernel(block_info, queries, kv_all, query_seg.reshape(rows, 1), segments....  8.2 us
  transfers between devices with their start and end apart: 3, of which 3 were waited for; matrix products, arithmetic and copies ran while one was open for 2% of the time, Pallas kernels for 0%

profile of v4, /device:TPU:1, one launch (start us, length us, event | category | flops | bytes accessed | tf_op | source)
XLA Modules:
  0.0 241.5 jit_solution(13663006407875477103)
XLA Ops:
  7.2 0.0 copy-start.2
  7.2 0.0 copy-start.4
  7.2 0.0 all-gather.3.cloned.1.call-start
  7.2 0.9 pad_maximum_fusion
  8.1 4.8 %all_gather.9 = bf16[512,256]{1,0:T(8,128)(2,1)S(1)} all-gather(bf16[256,256]{1,0:T(8,128)(2,1)S(1)} %pad_maximum_fusion), channel_id=1, replica_groups=mesh['ctx_y'=4,'ctx_x'=4,'ctx_core'=2,'tp'=8] {'ctx_core'}, dimensions={0}, use_global_device_ids=true | all-gather | bytes 393216 | tf_op jit(solution)/shard_map/all_gather | solution.py:127
  13.0 0.7 constant_dynamic-slice_fusion
  13.6 0.0 all-gather.3.cloned.1.call-update
  13.6 0.0 all-gather.5.cloned.1.call-start
  13.7 49.5 %all-gather.3.cloned.1.call-done = bf16[8192,128]{1,0:T(8,128)(2,1)} async-done(((bf16[512,128]{1,0:T(8,128)(2,1)}), bf16[8192,128]{1,0:T(8,128)(2,1)}) %all-gather.3.cloned.1.call-update) | async-done | bytes 2097168 | tf_op jit(solution)/shard_map/all_gather | solution.py:130
  63.2 0.0 all-gather.5.cloned.1.call-update
  63.2 0.0 reduce-scatter.2.cloned.1.call-start
  63.3 0.0 copy-done.2
  63.3 0.1 dynamic_slice.6
  63.3 0.5 slice.11
  63.9 1.3 convert_reduce_fusion
  67.5 0.0 copy-done.4
  67.5 0.6 reduce-window.6
  68.1 0.2 slice_reduce_fusion
  68.3 0.8 copy.10.qseg_ref
  69.1 0.6 pad_add_fusion.block_info
  69.7 0.1 fusion.4
  69.8 15.0 %all-gather.5.cloned.1.call-done.kv_ref = bf16[8192,256]{1,0:T(8,128)(2,1)} async-done(((bf16[8192,128]{1,0:T(8,128)(2,1)}), bf16[8192,256]{1,0:T(8,128)(2,1)}) %all-gather.5.cloned.1.call-update) | async-done | bytes 4194320 | tf_op jit(solution)/shard_map/all_gather | solution.py:131
  84.8 8.2 %shard_map.95 = bf16[256,512]{1,0:T(8,128)(2,1)} custom-call(s32[2]{0:T(128)} %pad_add_fusion.block_info, bf16[256,512]{1,0:T(8,128)(2,1)} %q_ref.1, bf16[8192,256]{1,0:T(8,128)(2,1)} %all-gather.5.cloned.1.call-done.kv_ref, s32[256,1]{1,0:T(8,128)} %copy.10.qseg_ref, s32[1,8192]{1,0:T(1,128)} %bitcast.17), custom_call_target="tpu_custom_call" | custom-call | tf_op jit(solution)/shard_map/pallas_call | solution.py:110
  93.0 9.2 %convolution_convert_fusion = bf16[512,8192]{1,0:T(8,128)(2,1)} fusion(bf16[512,8192]{1,0:T(8,128)(2,1)} %param.13, bf16[256,512]{1,0:T(8,128)(2,1)} %shard_map.95, s32[256]{0:T(256)S(1)} %multiply_add_fusion), kind=kOutput, calls=%fused_computation | convolution fusion | flops 4433772544 | bytes 17040384 | tf_op jit(solution)/shard_map/dot_general | solution.py:150
  102.2 0.0 copy-start
  102.2 0.0 reduce-scatter.2.cloned.1.call-update
  102.3 0.0 copy-start.3
  102.3 129.2 %reduce-scatter.2.cloned.1.call-done = bf16[64,8192]{1,0:T(8,128)(2,1)} async-done(((bf16[512,8192]{1,0:T(8,128)(2,1)}), bf16[64,8192]{1,0:T(8,128)(2,1)}) %reduce-scatter.2.cloned.1.call-update) | async-done | bytes 1048592 | tf_op jit(solution)/shard_map/reduce_scatter | solution.py:153
  231.5 0.0 copy-done
  231.5 0.0 copy-start.1
  231.5 1.8 multiply_reduce_fusion
  233.2 0.0 copy-done.3
  233.2 0.0 copy-done.1
  233.2 1.8 multiply_convert_fusion
  (5 shorter events, 0.1 us)
Async XLA Ops:
  7.2 56.1 %copy-start.2 = (s32[8192]{0:T(1024)S(1)}, s32[8192]{0:T(1024)}, u32[]{:S(2)}) copy-start(s32[8192]{0:T(1024)} %param.11) | copy-start | bytes 98308
  7.2 60.3 %copy-start.4 = (s32[256,1]{0,1:T(1,128)S(1)}, s32[256,1]{0,1:T(1,128)}, u32[]{:S(2)}) copy-start(s32[256,1]{0,1:T(1,128)} %param.12) | copy-start | bytes 3076
  7.2 56.0 %all-gather.3.cloned.1.call-start = ((), (), s32[]{:S(2)}) async-start(), calls=%async_computation.1 | async-start | bytes 2228224 | tf_op jit(solution)/shard_map/all_gather | solution.py:130
  13.6 71.1 %all-gather.5.cloned.1.call-start = ((), (), s32[]{:S(2)}) async-start(), calls=%async_computation.2 | async-start | bytes 6291456 | tf_op jit(solution)/shard_map/all_gather | solution.py:131
  63.2 168.3 %reduce-scatter.2.cloned.1.call-start = ((), (), s32[]{:S(2)}) async-start(), calls=%async_computation.3 | async-start | bytes 9437184 | tf_op jit(solution)/shard_map/reduce_scatter | solution.py:153
  102.2 129.2 %copy-start = (bf16[64,8192]{1,0:T(8,128)(2,1)S(1)}, bf16[64,8192]{1,0:T(8,128)(2,1)}, u32[]{:S(2)}) copy-start(bf16[64,8192]{1,0:T(8,128)(2,1)} %param.14) | copy-start | bytes 3145732
  102.3 131.0 %copy-start.3 = (f32[8192]{0:T(1024)S(1)}, f32[8192]{0:T(1024)}, u32[]{:S(2)}) copy-start(f32[8192]{0:T(1024)} %param.15) | copy-start | bytes 98308
  231.5 1.8 copy-start.1
Sparse Core Ops, SparseCore 0:
  13.8 49.3 all-gather.2
  65.0 19.7 all-gather.4
  102.4 129.0 reduce-scatter.1

commit v5 on v2

--- a/solution.py
+++ b/solution.py
@@ -29,15 +29,15 @@
 
     @pl.when(step == 0)
     def _():
-        max_ref[...] = jnp.full(max_ref.shape, -1e30, jnp.float32)
+        max_ref[...] = jnp.full(max_ref.shape, -1e29, jnp.float32)
         total_ref[...] = jnp.zeros(total_ref.shape, jnp.float32)
         acc_ref[...] = jnp.zeros(acc_ref.shape, jnp.float32)
 
-    @pl.when(key_block >= first_block)
-    def _():
-        query_pos = my_block * rows + lax.broadcasted_iota(jnp.int32, (rows, 1), 0)
-        key_pos = key_block * key_width + lax.broadcasted_iota(jnp.int32, (1, key_width), 1)
-        allowed = (qseg_ref[...] == kseg_ref[...]) & (key_pos <= query_pos)
+    def accumulate(masked):
+        if masked:
+            query_pos = my_block * rows + lax.broadcasted_iota(jnp.int32, (rows, 1), 0)
+            key_pos = key_block * key_width + lax.broadcasted_iota(jnp.int32, (1, key_width), 1)
+            allowed = (qseg_ref[...] == kseg_ref[...]) & (key_pos <= query_pos)
         for head in range(local_heads):
             kv_head = head // group
             keys = kv_ref[:, kv_head * HEAD_DIM:(kv_head + 1) * HEAD_DIM]
@@ -49,16 +49,28 @@
                 )
                 * score_scale
             )
-            scores = jnp.where(allowed, scores, -1e30)
+            if masked:
+                scores = jnp.where(allowed, scores, -1e30)
             running_max = max_ref[head]
             new_max = jnp.maximum(running_max, jnp.max(scores, axis=-1, keepdims=True))
-            exponent = jnp.where(allowed, jnp.exp(scores - new_max), 0.0)
+            exponent = jnp.exp(scores - new_max)
             factor = jnp.exp(running_max - new_max)
             total_ref[head] = total_ref[head] * factor + jnp.sum(exponent, axis=-1, keepdims=True)
             acc_ref[head] = acc_ref[head] * factor + jnp.dot(
                 exponent.astype(jnp.bfloat16), values, preferred_element_type=jnp.float32
             )
             max_ref[head] = new_max
+
+    active = key_block >= first_block
+    whole = block_info[2 + step] == 1
+
+    @pl.when(active & whole)
+    def _():
+        accumulate(False)
+
+    @pl.when(active & jnp.logical_not(whole))
+    def _():
+        accumulate(True)
 
     @pl.when(step == window - 1)
     def _():
@@ -74,7 +86,20 @@
     block_count = kv_all.shape[0] // key_width
     window = min(block_count, DOC_MOST // key_width + 1)
     local_heads = q_cols // HEAD_DIM
-    block_info = jnp.stack([my_block, first_block]).astype(jnp.int32)
+    global_blocks = my_block - (window - 1) + jnp.arange(window, dtype=jnp.int32)
+    clamped = jnp.clip(global_blocks, 0, segments.shape[0] // key_width - 1)
+    key_first = segments[clamped * key_width]
+    key_last = segments[clamped * key_width + key_width - 1]
+    whole = (
+        (key_first == key_last)
+        & (key_first == query_seg[0])
+        & (query_seg[0] == query_seg[rows - 1])
+        & (global_blocks < my_block)
+        & (global_blocks >= 0)
+    )
+    block_info = jnp.concatenate(
+        [jnp.stack([my_block, first_block]), whole.astype(jnp.int32)]
+    ).astype(jnp.int32)
 
     def kv_map(step, info):
         return (jnp.maximum(info[0] - (window - 1) + step, info[1]), 0)

time: 224 us -> 221 us (0.987)
  waiting for transfers between devices: 177 us -> 169 us
  local copies, waits for them, and re-layouts: 2.32 us -> 5.31 us
    all_gather x1, waiting for transfers between devices: 47.3 us -> 42.1 us  [on_device(): kv_all = lax.all_gather(kv_pair, 'ctx', axis=0, tiled=True)]
    gather x0 -> x2, local copies, waits for them, and re-layouts: none -> 2.92 us  [the longest x1 1.46 us: attend_window(): key_first = segments[clamped * key_width]]
    reduce_scatter x1, waiting for transfers between devices: 129 us -> 127 us  [on_device(): lax.psum_scatter(partial_slots, 'tp', scatter_dimension=0, tiled=True)]
  transfers between devices with their start and end apart: 2 -> 2, of which waited for: 2 -> 2; matrix products, arithmetic and copies ran while one was open for 3% -> 5% of each run, Pallas kernels for 0% -> 0%
where the time goes in v5:
time: 221 us
  waiting for transfers between devices  169 us (76%)
  between operations  18.1 us (8%)
  other arithmetic  11.1 us (5%)
  matrix products  9.26 us (4%)
  Pallas kernels  8.12 us (4%)
  local copies, waits for them, and re-layouts  5.31 us (2%)
    reduce_scatter x1, waiting for transfers between devices, on_device(): lax.psum_scatter(partial_slots, 'tp', scatter_dimension=0, tiled=True)  127 us
    all_gather x1, waiting for transfers between devices, on_device(): kv_all = lax.all_gather(kv_pair, 'ctx', axis=0, tiled=True)  42.1 us
    dot_general x1, matrix products, on_device(): jnp.dot(attended_slots, out_proj, preferred_element_type=jnp.float32)  9.26 us
    pallas_call x1, Pallas kernels, attend_window(): kernel(block_info, queries, kv_all, query_seg.reshape(rows, 1), segments....  8.12 us
  transfers between devices with their start and end apart: 2, of which 2 were waited for; matrix products, arithmetic and copies ran while one was open for 5% of the time, Pallas kernels for 0%

profile of v5, /device:TPU:1, one launch (start us, length us, event | category | flops | bytes accessed | tf_op | source)
XLA Modules:
  0.0 220.8 jit_solution(13159294812049579479)
XLA Ops:
  7.2 0.0 all-gather.2.cloned.1.call-start
  7.2 1.5 pad_maximum_fusion
  8.8 0.0 all-gather.2.cloned.1.call-update
  8.8 0.0 reduce-scatter.2.cloned.1.call-start
  8.8 0.8 dynamic_slice.3
  9.6 0.6 fusion.8
  10.2 2.1 convert_reduce_fusion
  16.3 1.5 gather_fusion
  17.8 1.5 gather_fusion.1
  19.3 0.7 fusion.5
  19.9 0.6 reduce-window.6
  20.5 0.2 slice_reduce_fusion
  20.8 0.8 copy.10.qseg_ref
  21.6 0.6 and_convert_fusion
  22.2 0.6 pad_add_fusion.block_info
  22.8 0.8 fusion.4
  23.6 0.7 multiply_add_fusion
  24.3 42.1 %all-gather.2.cloned.1.call-done.kv_ref = bf16[8192,256]{1,0:T(8,128)(2,1)} async-done(((bf16[256,256]{1,0:T(8,128)(2,1)}), bf16[8192,256]{1,0:T(8,128)(2,1)}) %all-gather.2.cloned.1.call-update) | async-done | bytes 4194320 | tf_op jit(solution)/shard_map/all_gather | solution.py:149
  66.4 8.1 %shard_map.95 = bf16[256,512]{1,0:T(8,128)(2,1)} custom-call(s32[19]{0:T(128)} %pad_add_fusion.block_info, bf16[256,512]{1,0:T(8,128)(2,1)} %q_ref.1, bf16[8192,256]{1,0:T(8,128)(2,1)} %all-gather.2.cloned.1.call-done.kv_ref, s32[256,1]{1,0:T(8,128)} %copy.10.qseg_ref, s32[1,8192]{1,0:T(1,128)} %bitcast.22), custom_call_target="tpu_custom_call" | custom-call | tf_op jit(solution)/shard_map/pallas_call | solution.py:132
  74.5 9.3 %convolution_convert_fusion = bf16[512,8192]{1,0:T(8,128)(2,1)} fusion(bf16[512,8192]{1,0:T(8,128)(2,1)} %param.13, bf16[256,512]{1,0:T(8,128)(2,1)} %shard_map.95, s32[256]{0:T(256)S(1)} %multiply_add_fusion), kind=kOutput, calls=%fused_computation.2 | convolution fusion | flops 4433772544 | bytes 17040384 | tf_op jit(solution)/shard_map/dot_general | solution.py:167
  83.7 0.0 copy-start
  83.7 0.0 reduce-scatter.2.cloned.1.call-update
  83.8 0.0 copy-start.2
  83.8 126.6 %reduce-scatter.2.cloned.1.call-done = bf16[64,8192]{1,0:T(8,128)(2,1)} async-done(((bf16[512,8192]{1,0:T(8,128)(2,1)}), bf16[64,8192]{1,0:T(8,128)(2,1)}) %reduce-scatter.2.cloned.1.call-update) | async-done | bytes 1048592 | tf_op jit(solution)/shard_map/reduce_scatter | solution.py:170
  210.4 0.0 copy-done
  210.4 0.0 copy-start.1
  210.4 1.8 multiply_reduce_fusion
  212.1 0.0 copy-done.2
  212.2 0.0 copy-done.1
  212.2 1.8 multiply_convert_fusion
  (6 shorter events, 0.1 us)
Async XLA Ops:
  7.2 59.2 %all-gather.2.cloned.1.call-start = ((), (), s32[]{:S(2)}) async-start(), calls=%async_computation.1 | async-start | bytes 4325376 | tf_op jit(solution)/shard_map/all_gather | solution.py:149
  8.8 201.6 %reduce-scatter.2.cloned.1.call-start = ((), (), s32[]{:S(2)}) async-start(), calls=%async_computation.2 | async-start | bytes 9437184 | tf_op jit(solution)/shard_map/reduce_scatter | solution.py:170
  83.7 126.6 %copy-start = (bf16[64,8192]{1,0:T(8,128)(2,1)S(1)}, bf16[64,8192]{1,0:T(8,128)(2,1)}, u32[]{:S(2)}) copy-start(bf16[64,8192]{1,0:T(8,128)(2,1)} %param.14) | copy-start | bytes 3145732
  83.8 128.4 %copy-start.2 = (f32[8192]{0:T(1024)S(1)}, f32[8192]{0:T(1024)}, u32[]{:S(2)}) copy-start(f32[8192]{0:T(1024)} %param.15) | copy-start | bytes 98308
  210.4 1.8 copy-start.1
Sparse Core Ops, SparseCore 0:
  11.1 55.2 all-gather.1
  83.9 126.4 reduce-scatter.1

commit v6 on v5

--- a/solution.py
+++ b/solution.py
@@ -35,7 +35,7 @@
 
     def accumulate(masked):
         if masked:
-            query_pos = my_block * rows + lax.broadcasted_iota(jnp.int32, (rows, 1), 0)
+            query_pos = block_info[2] + lax.broadcasted_iota(jnp.int32, (rows, 1), 0)
             key_pos = key_block * key_width + lax.broadcasted_iota(jnp.int32, (1, key_width), 1)
             allowed = (qseg_ref[...] == kseg_ref[...]) & (key_pos <= query_pos)
         for head in range(local_heads):
@@ -62,7 +62,7 @@
             max_ref[head] = new_max
 
     active = key_block >= first_block
-    whole = block_info[2 + step] == 1
+    whole = block_info[3 + step] == 1
 
     @pl.when(active & whole)
     def _():
@@ -80,9 +80,10 @@
             ).astype(out_ref.dtype)
 
 
-def attend_window(queries, kv_all, query_seg, segments, my_block, first_block, group):
+def attend_window(
+    queries, kv_all, query_seg, segments, my_block, first_block, group, query_start, key_width
+):
     rows, q_cols = queries.shape
-    key_width = rows
     block_count = kv_all.shape[0] // key_width
     window = min(block_count, DOC_MOST // key_width + 1)
     local_heads = q_cols // HEAD_DIM
@@ -98,7 +99,7 @@
         & (global_blocks >= 0)
     )
     block_info = jnp.concatenate(
-        [jnp.stack([my_block, first_block]), whole.astype(jnp.int32)]
+        [jnp.stack([my_block, first_block, query_start]), whole.astype(jnp.int32)]
     ).astype(jnp.int32)
 
     def kv_map(step, info):
@@ -147,9 +148,6 @@
     query_seg = lax.dynamic_slice_in_dim(segments, my_start, rows_here, 0)
     kv_pair = jnp.concatenate([key_rows, value_rows], axis=1)
     kv_all = lax.all_gather(kv_pair, "ctx", axis=0, tiled=True)
-    doc_start = jnp.sum((segments < query_seg[0]).astype(jnp.int32))
-    first_block = doc_start // rows_here
-    attended = attend_window(queries, kv_all, query_seg, segments, my_block, first_block, group_size)
     slot_count = residual.shape[0]
     owner_count = lax.axis_size("tp")
     owners = owner_ids[:, 0]
@@ -159,17 +157,35 @@
     before = jnp.cumsum(onehot, axis=0) - onehot
     row_rank = jnp.sum(before * onehot, axis=1)
     slot_of_token = owners * slot_count + row_rank
-    all_slots = jnp.arange(owner_count * slot_count, dtype=jnp.int32)
-    select = (slot_of_token[None, :] == all_slots[:, None]).astype(jnp.bfloat16)
-    attended_slots = jnp.dot(select, attended, preferred_element_type=jnp.float32).astype(
-        jnp.bfloat16
-    )
-    partial_slots = jnp.dot(attended_slots, out_proj, preferred_element_type=jnp.float32).astype(
-        jnp.bfloat16
-    )
-    owned_rows = lax.psum_scatter(partial_slots, "tp", scatter_dimension=0, tiled=True).astype(
-        jnp.float32
-    )
+    my_slots = lax.axis_index("tp") * slot_count + jnp.arange(slot_count, dtype=jnp.int32)
+    select = (slot_of_token[None, :] == my_slots[:, None]).astype(jnp.bfloat16)
+    halves = 2
+    half_rows = rows_here // halves
+    summed_parts = []
+    for part in range(halves):
+        part_rows = slice(part * half_rows, (part + 1) * half_rows)
+        part_seg = query_seg[part_rows]
+        doc_start = jnp.sum((segments < part_seg[0]).astype(jnp.int32))
+        first_block = doc_start // rows_here
+        attended = attend_window(
+            queries[part_rows],
+            kv_all,
+            part_seg,
+            segments,
+            my_block,
+            first_block,
+            group_size,
+            my_start + part * half_rows,
+            rows_here,
+        )
+        partial_rows = jnp.dot(attended, out_proj, preferred_element_type=jnp.float32).astype(
+            jnp.bfloat16
+        )
+        if summed_parts:
+            partial_rows, _ = lax.optimization_barrier((partial_rows, summed_parts[-1]))
+        summed_parts.append(lax.psum(partial_rows, "tp"))
+    summed = jnp.concatenate(summed_parts, axis=0)
+    owned_rows = jnp.dot(select, summed, preferred_element_type=jnp.float32)
     hidden_sum = residual.astype(jnp.float32) + owned_rows
     mean_square = jnp.mean(hidden_sum * hidden_sum, axis=-1, keepdims=True)
     normed = hidden_sum * lax.rsqrt(mean_square + 1e-05) * norm_gain

time: 221 us -> 269 us (1.22); the launches traced: 221 us -> 265 us
  waiting for transfers between devices: 169 us -> 201 us
  matrix products: 9.26 us -> 14.9 us
  Pallas kernels: 8.12 us -> 11.4 us
  between operations: 18.1 us -> 21.3 us
    psum x0 -> x2, waiting for transfers between devices: none -> 160 us  [on_device(): summed_parts.append(lax.psum(partial_rows, 'tp'))]
    reduce_scatter x1 -> x0, waiting for transfers between devices: 127 us -> none  [on_device(): lax.psum_scatter(partial_slots, 'tp', scatter_dimension=0, tiled=True)]
    dot_general x1 -> x3, matrix products: 9.26 us -> 14.9 us  [the longest x2 12.2 us: on_device(): jnp.dot(attended, out_proj, preferred_element_type=jnp.float32)]
    pallas_call x1 -> x2, Pallas kernels: 8.12 us -> 11.4 us  [attend_window(): kernel(block_info, queries, kv_all, query_seg.reshape(rows, 1), segments....]
  transfers between devices with their start and end apart: 2 -> 3, of which waited for: 2 -> 3; matrix products, arithmetic and copies ran while one was open for 5% -> 7% of each run, Pallas kernels for 0% -> 2%
where the time goes in v6:
time: 269 us; the launch traced here: 265 us
  waiting for transfers between devices  201 us (75%)
  between operations  21.3 us (8%)
  matrix products  14.9 us (6%)
  Pallas kernels  11.4 us (4%)
  other arithmetic  8.99 us (3%)
  local copies, waits for them, and re-layouts  7.68 us (3%)
    psum x2, waiting for transfers between devices, on_device(): summed_parts.append(lax.psum(partial_rows, 'tp'))  160 us
    all_gather x1, waiting for transfers between devices, on_device(): kv_all = lax.all_gather(kv_pair, 'ctx', axis=0, tiled=True)  40.9 us
    dot_general x2, matrix products, on_device(): jnp.dot(attended, out_proj, preferred_element_type=jnp.float32)  12.2 us
    pallas_call x2, Pallas kernels, attend_window(): kernel(block_info, queries, kv_all, query_seg.reshape(rows, 1), segments....  11.4 us
  transfers between devices with their start and end apart: 3, of which 3 were waited for; matrix products, arithmetic and copies ran while one was open for 7% of the time, Pallas kernels for 2%

profile of v6, /device:TPU:1, one launch (start us, length us, event | category | flops | bytes accessed | tf_op | source)
XLA Modules:
  0.0 265.2 jit_solution(13115335028871127400)
XLA Ops:
  7.2 0.0 all-gather.2.cloned.1.call-start
  7.2 1.5 pad_maximum_fusion
  8.7 0.0 all-gather.2.cloned.1.call-update
  8.8 0.0 all-reduce.3.cloned.1.call-start
  8.8 0.8 dynamic_slice.3
  9.6 0.6 fusion.13
  10.2 2.6 convert_reduce_fusion.1
  17.8 1.5 gather_fusion
  19.2 1.5 gather_fusion.1
  20.7 0.7 copy.12.qseg_ref
  21.4 1.2 and_convert_fusion.1
  22.6 0.6 pad_add_fusion.block_info
  23.2 1.7 fusion.12
  24.9 40.9 %all-gather.2.cloned.1.call-done.kv_ref = bf16[8192,256]{1,0:T(8,128)(2,1)} async-done(((bf16[256,256]{1,0:T(8,128)(2,1)}), bf16[8192,256]{1,0:T(8,128)(2,1)}) %all-gather.2.cloned.1.call-update) | async-done | bytes 4194320 | tf_op jit(solution)/shard_map/all_gather | solution.py:150
  65.8 5.7 %shard_map.95 = bf16[128,512]{1,0:T(8,128)(2,1)} custom-call(s32[20]{0:T(128)} %pad_add_fusion.block_info, bf16[128,512]{1,0:T(8,128)(2,1)} %get-tuple-element.8.q_ref, bf16[8192,256]{1,0:T(8,128)(2,1)} %all-gather.2.cloned.1.call-done.kv_ref, s32[128,1]{1,0:T(8,128)} %copy.12.qseg_ref, s32[1,8192]{1,0:T(1,128)} %bitcast.32), custom_call_target="tpu_custom_call" | custom-call | tf_op jit(solution)/shard_map/pallas_call | solution.py:133
  71.5 6.1 %convolution_convert_fusion.1 = bf16[128,8192]{1,0:T(8,128)(2,1)} fusion(bf16[128,512]{1,0:T(8,128)(2,1)} %shard_map.95, bf16[512,8192]{1,0:T(8,128)(2,1)} %param.13), kind=kOutput, calls=%fused_computation.3 | convolution fusion | flops 1074790400 | bytes 10616832 | tf_op jit(solution)/shard_map/dot_general | solution.py:181
  77.5 0.0 all-reduce.3.cloned.1.call-update
  77.6 0.0 all-reduce.5.cloned.1.call-start
  80.1 0.7 copy.13.qseg_ref
  80.9 0.7 pad_add_fusion.1.block_info
  81.5 5.7 %shard_map.96 = bf16[128,512]{1,0:T(8,128)(2,1)} custom-call(s32[20]{0:T(128)} %pad_add_fusion.1.block_info, bf16[128,512]{1,0:T(8,128)(2,1)} %get-tuple-element.9.q_ref, bf16[8192,256]{1,0:T(8,128)(2,1)} %all-gather.2.cloned.1.call-done.kv_ref, s32[128,1]{1,0:T(8,128)} %copy.13.qseg_ref, s32[1,8192]{1,0:T(1,128)} %bitcast.33), custom_call_target="tpu_custom_call" | custom-call | tf_op jit(solution)/shard_map/pallas_call | solution.py:133
  87.2 0.0 copy-start.3
  87.2 6.1 %convolution_convert_fusion = bf16[128,8192]{1,0:T(8,128)(2,1)} fusion(bf16[128,512]{1,0:T(8,128)(2,1)} %shard_map.96, bf16[512,8192]{1,0:T(8,128)(2,1)} %param.13), kind=kOutput, calls=%fused_computation.2 | convolution fusion | flops 1074790400 | bytes 10616832 | tf_op jit(solution)/shard_map/dot_general | solution.py:181
  93.3 0.0 copy-start.1
  93.3 77.5 %all-reduce.3.cloned.1.call-done = bf16[128,8192]{1,0:T(8,128)(2,1)} async-done(((bf16[128,8192]{1,0:T(8,128)(2,1)}), bf16[128,8192]{1,0:T(8,128)(2,1)}) %all-reduce.3.cloned.1.call-update) | async-done | bytes 2097168 | tf_op jit(solution)/shard_map/psum | solution.py:186
  170.8 0.0 copy-start.2
  170.8 0.0 all-reduce.5.cloned.1.call-update
  170.8 0.0 copy-done.1
  170.9 0.6 reduce-window.6
  171.4 0.2 slice_reduce_fusion
  171.7 0.1 fusion.7
  171.8 0.0 copy-start
  171.8 82.5 %all-reduce.5.cloned.1.call-done = bf16[128,8192]{1,0:T(8,128)(2,1)} async-done(((bf16[128,8192]{1,0:T(8,128)(2,1)}), bf16[128,8192]{1,0:T(8,128)(2,1)}) %all-reduce.5.cloned.1.call-update) | async-done | bytes 2097168 | tf_op jit(solution)/shard_map/psum | solution.py:186
  254.3 0.0 copy-done.3
  254.3 0.0 copy-done.2
  254.4 2.7 %multiply_reduce_fusion = (f32[64]{0:T(128)S(1)}, f32[64,8192]{1,0:T(8,128)S(1)}) fusion(bf16[128,8192]{1,0:T(8,128)(2,1)} %all-reduce.5.cloned.1.call-done, bf16[128,8192]{1,0:T(8,128)(2,1)S(1)} %copy-done.2, s32[256]{0:T(256)S(1)} %multiply_add_fusion, s32[64]{0:T(128)S(1)} %iota_add_fusion.1, bf16[64,8192]{1,0:T(8,128)(2,1)S(1)} %copy-done.3), kind=kOutput, calls=%fused_computation.9 | convolution fusion | flops 278937536 | bytes 7341568 | tf_op jit(solution)/shard_map/dot_general | solution.py:188
  257.1 0.0 copy-done
  257.1 1.6 multiply_convert_fusion
  (10 shorter events, 0.1 us)
Async XLA Ops:
  7.2 58.6 %all-gather.2.cloned.1.call-start = ((), (), s32[]{:S(2)}) async-start(), calls=%async_computation | async-start | bytes 4325376 | tf_op jit(solution)/shard_map/all_gather | solution.py:150
  8.8 162.0 %all-reduce.3.cloned.1.call-start = ((), (), s32[]{:S(2)}) async-start(), calls=%async_computation.1 | async-start | bytes 4194304 | tf_op jit(solution)/shard_map/psum | solution.py:186
  77.6 176.8 %all-reduce.5.cloned.1.call-start = ((), (), s32[]{:S(2)}) async-start(), calls=%async_computation.2 | async-start | bytes 4194304 | tf_op jit(solution)/shard_map/psum | solution.py:186
  87.2 167.2 %copy-start.3 = (bf16[64,8192]{1,0:T(8,128)(2,1)S(1)}, bf16[64,8192]{1,0:T(8,128)(2,1)}, u32[]{:S(2)}) copy-start(bf16[64,8192]{1,0:T(8,128)(2,1)} %param.14) | copy-start | bytes 3145732
  93.3 77.5 %copy-start.1 = (s32[256,1]{0,1:T(1,128)S(1)}, s32[256,1]{0,1:T(1,128)}, u32[]{:S(2)}) copy-start(s32[256,1]{0,1:T(1,128)} %param.12) | copy-start | bytes 3076
  170.8 83.5 %copy-start.2 = (bf16[128,8192]{1,0:T(8,128)(2,1)S(1)}, bf16[128,8192]{1,0:T(8,128)(2,1)}, u32[]{:S(2)}) copy-start(bf16[128,8192]{1,0:T(8,128)(2,1)} %all-reduce.3.cloned.1.call-done) | copy-start | bytes 6291460
  171.8 85.3 %copy-start = (f32[8192]{0:T(1024)S(1)}, f32[8192]{0:T(1024)}, u32[]{:S(2)}) copy-start(f32[8192]{0:T(1024)} %param.15) | copy-start | bytes 98308
Sparse Core Ops, SparseCore 0:
  10.5 55.2 all-gather.1
  77.7 93.0 all-reduce.2
  173.2 81.1 all-reduce.4

commit v7 on v5

--- a/solution.py
+++ b/solution.py
@@ -15,16 +15,27 @@
 
 
 def attention_kernel(
-    block_info, q_ref, kv_ref, qseg_ref, kseg_ref, out_ref, max_ref, total_ref, acc_ref, *, window, group
+    block_info,
+    qt_ref,
+    k_ref,
+    vt_ref,
+    qseg_ref,
+    kseg_ref,
+    out_ref,
+    max_ref,
+    total_ref,
+    acc_ref,
+    *,
+    window,
+    group,
 ):
     step = pl.program_id(0)
     my_block = block_info[0]
     first_block = block_info[1]
     key_block = my_block - (window - 1) + step
-    rows = q_ref.shape[0]
-    key_width = kv_ref.shape[0]
+    rows = qt_ref.shape[1]
+    key_width = k_ref.shape[0]
     local_heads = acc_ref.shape[0]
-    kv_cols = kv_ref.shape[1] // 2
     score_scale = 1.0 / math.sqrt(HEAD_DIM)
 
     @pl.when(step == 0)
@@ -35,34 +46,29 @@
 
     def accumulate(masked):
         if masked:
-            query_pos = my_block * rows + lax.broadcasted_iota(jnp.int32, (rows, 1), 0)
-            key_pos = key_block * key_width + lax.broadcasted_iota(jnp.int32, (1, key_width), 1)
-            allowed = (qseg_ref[...] == kseg_ref[...]) & (key_pos <= query_pos)
+            query_pos = block_info[2] + lax.broadcasted_iota(jnp.int32, (1, rows), 1)
+            key_pos = key_block * key_width + lax.broadcasted_iota(jnp.int32, (key_width, 1), 0)
+            allowed = (kseg_ref[...] == qseg_ref[...]) & (key_pos <= query_pos)
         for head in range(local_heads):
             kv_head = head // group
-            keys = kv_ref[:, kv_head * HEAD_DIM:(kv_head + 1) * HEAD_DIM]
-            values = kv_ref[:, kv_cols + kv_head * HEAD_DIM:kv_cols + (kv_head + 1) * HEAD_DIM]
-            query = q_ref[:, head * HEAD_DIM:(head + 1) * HEAD_DIM]
-            scores = (
-                lax.dot_general(
-                    query, keys, (((1,), (1,)), ((), ())), preferred_element_type=jnp.float32
-                )
-                * score_scale
-            )
+            keys = k_ref[:, kv_head * HEAD_DIM:(kv_head + 1) * HEAD_DIM]
+            values_t = vt_ref[kv_head * HEAD_DIM:(kv_head + 1) * HEAD_DIM, :]
+            query_t = qt_ref[head * HEAD_DIM:(head + 1) * HEAD_DIM, :]
+            scores = jnp.dot(keys, query_t, preferred_element_type=jnp.float32) * score_scale
             if masked:
                 scores = jnp.where(allowed, scores, -1e30)
             running_max = max_ref[head]
-            new_max = jnp.maximum(running_max, jnp.max(scores, axis=-1, keepdims=True))
+            new_max = jnp.maximum(running_max, jnp.max(scores, axis=0, keepdims=True))
             exponent = jnp.exp(scores - new_max)
             factor = jnp.exp(running_max - new_max)
-            total_ref[head] = total_ref[head] * factor + jnp.sum(exponent, axis=-1, keepdims=True)
+            total_ref[head] = total_ref[head] * factor + jnp.sum(exponent, axis=0, keepdims=True)
             acc_ref[head] = acc_ref[head] * factor + jnp.dot(
-                exponent.astype(jnp.bfloat16), values, preferred_element_type=jnp.float32
+                values_t, exponent.astype(jnp.bfloat16), preferred_element_type=jnp.float32
             )
             max_ref[head] = new_max
 
     active = key_block >= first_block
-    whole = block_info[2 + step] == 1
+    whole = block_info[3 + step] == 1
 
     @pl.when(active & whole)
     def _():
@@ -75,7 +81,7 @@
     @pl.when(step == window - 1)
     def _():
         for head in range(local_heads):
-            out_ref[:, head * HEAD_DIM:(head + 1) * HEAD_DIM] = (
+            out_ref[head * HEAD_DIM:(head + 1) * HEAD_DIM, :] = (
                 acc_ref[head] / total_ref[head]
             ).astype(out_ref.dtype)
 
@@ -86,8 +92,9 @@
     block_count = kv_all.shape[0] // key_width
     window = min(block_count, DOC_MOST // key_width + 1)
     local_heads = q_cols // HEAD_DIM
+    kv_cols = kv_all.shape[1] // 2
     global_blocks = my_block - (window - 1) + jnp.arange(window, dtype=jnp.int32)
-    clamped = jnp.clip(global_blocks, 0, segments.shape[0] // key_width - 1)
+    clamped = jnp.clip(global_blocks, 0, block_count - 1)
     key_first = segments[clamped * key_width]
     key_last = segments[clamped * key_width + key_width - 1]
     whole = (
@@ -98,40 +105,44 @@
         & (global_blocks >= 0)
     )
     block_info = jnp.concatenate(
-        [jnp.stack([my_block, first_block]), whole.astype(jnp.int32)]
+        [jnp.stack([my_block, first_block, my_block * rows]), whole.astype(jnp.int32)]
     ).astype(jnp.int32)
 
-    def kv_map(step, info):
-        return (jnp.maximum(info[0] - (window - 1) + step, info[1]), 0)
-
-    def kseg_map(step, info):
-        return (0, jnp.maximum(info[0] - (window - 1) + step, info[1]))
+    def key_index(step, info):
+        return jnp.maximum(info[0] - (window - 1) + step, info[1])
 
     grid_spec = pltpu.PrefetchScalarGridSpec(
         num_scalar_prefetch=1,
         grid=(window,),
         in_specs=[
-            pl.BlockSpec((rows, q_cols), lambda step, info: (0, 0)),
-            pl.BlockSpec((key_width, kv_all.shape[1]), kv_map),
-            pl.BlockSpec((rows, 1), lambda step, info: (0, 0)),
-            pl.BlockSpec((1, key_width), kseg_map),
+            pl.BlockSpec((q_cols, rows), lambda step, info: (0, 0)),
+            pl.BlockSpec((key_width, kv_cols), lambda step, info: (key_index(step, info), 0)),
+            pl.BlockSpec((kv_cols, key_width), lambda step, info: (0, key_index(step, info))),
+            pl.BlockSpec((1, rows), lambda step, info: (0, 0)),
+            pl.BlockSpec((key_width, 1), lambda step, info: (key_index(step, info), 0)),
         ],
-        out_specs=pl.BlockSpec((rows, q_cols), lambda step, info: (0, 0)),
+        out_specs=pl.BlockSpec((q_cols, rows), lambda step, info: (0, 0)),
         scratch_shapes=[
-            pltpu.VMEM((local_heads, rows, 1), jnp.float32),
-            pltpu.VMEM((local_heads, rows, 1), jnp.float32),
-            pltpu.VMEM((local_heads, rows, HEAD_DIM), jnp.float32),
+            pltpu.VMEM((local_heads, 1, rows), jnp.float32),
+            pltpu.VMEM((local_heads, 1, rows), jnp.float32),
+            pltpu.VMEM((local_heads, HEAD_DIM, rows), jnp.float32),
         ],
     )
     kernel = pl.pallas_call(
         functools.partial(attention_kernel, window=window, group=group),
         grid_spec=grid_spec,
-        out_shape=jax.ShapeDtypeStruct((rows, q_cols), jnp.bfloat16),
+        out_shape=jax.ShapeDtypeStruct((q_cols, rows), jnp.bfloat16),
         compiler_params=pltpu.CompilerParams(dimension_semantics=("arbitrary",)),
     )
-    return kernel(
-        block_info, queries, kv_all, query_seg.reshape(rows, 1), segments.reshape(1, -1)
-    )
+    attended_t = kernel(
+        block_info,
+        queries.T,
+        kv_all,
+        kv_all[:, kv_cols:].T,
+        query_seg.reshape(1, rows),
+        segments.reshape(-1, 1),
+    )
+    return attended_t.T
 
 
 def on_device(queries, key_rows, value_rows, segments, owner_ids, out_proj, residual, norm_gain):

time: 221 us -> 216 us (0.977)
  waiting for transfers between devices: 169 us -> 153 us
  local copies, waits for them, and re-layouts: 5.31 us -> 20.1 us
  other arithmetic: 11.1 us -> 8.16 us
    reduce_scatter x1, waiting for transfers between devices: 127 us -> 111 us  [on_device(): lax.psum_scatter(partial_slots, 'tp', scatter_dimension=0, tiled=True)]
    all_gather x0 -> x1, local copies, waits for them, and re-layouts: none -> 6.35 us  [on_device(): kv_all = lax.all_gather(kv_pair, 'ctx', axis=0, tiled=True)]
    transpose x0 -> x1, local copies, waits for them, and re-layouts: none -> 3.14 us  [attend_window(): kv_all[:, kv_cols:]]
    unnamed x6 -> x15, local copies, waits for them, and re-layouts: 0.01 us -> 2.74 us
    reshape x1, local copies, waits for them, and re-layouts: 0.81 us -> 3.4 us  [attend_window(): segments.reshape(-1, 1)]
  transfers between devices with their start and end apart: 2 -> 2, of which waited for: 2 -> 2; matrix products, arithmetic and copies ran while one was open for 5% -> 6% of each run, Pallas kernels for 0% -> 0%
where the time goes in v7:
time: 216 us; the launch traced here: 215 us
  waiting for transfers between devices  153 us (71%)
  local copies, waits for them, and re-layouts  20.1 us (9%)
  between operations  17.8 us (8%)
  matrix products  9.32 us (4%)
  other arithmetic  8.16 us (4%)
  Pallas kernels  6.12 us (3%)
    reduce_scatter x1, waiting for transfers between devices, on_device(): lax.psum_scatter(partial_slots, 'tp', scatter_dimension=0, tiled=True)  111 us
    all_gather x1, waiting for transfers between devices, on_device(): kv_all = lax.all_gather(kv_pair, 'ctx', axis=0, tiled=True)  42.5 us
    dot_general x1, matrix products, on_device(): jnp.dot(attended_slots, out_proj, preferred_element_type=jnp.float32)  9.32 us
    all_gather x1, local copies, waits for them, and re-layouts, on_device(): kv_all = lax.all_gather(kv_pair, 'ctx', axis=0, tiled=True)  6.35 us
    pallas_call x1, Pallas kernels, attend_window(): kernel(block_info, queries.T, kv_all, kv_all[:, kv_cols:].T, query_seg.re...  6.12 us
  transfers between devices with their start and end apart: 2, of which 2 were waited for; matrix products, arithmetic and copies ran while one was open for 6% of the time, Pallas kernels for 0%

profile of v7, /device:TPU:1, one launch (start us, length us, event | category | flops | bytes accessed | tf_op | source)
XLA Modules:
  0.0 215.1 jit_solution(1726945649083379993)
XLA Ops:
  7.2 0.0 all-gather.2.cloned.1.call-start
  7.2 0.9 copy.15
  8.2 0.9 copy.16
  9.1 0.7 pad_maximum_fusion
  9.8 0.0 all-gather.2.cloned.1.call-update
  9.8 0.0 reduce-scatter.2.cloned.1.call-start
  9.8 0.8 dynamic_slice.3
  10.6 0.0 copy-start.4
  10.6 0.6 fusion.8
  11.2 2.0 convert_reduce_fusion
  16.9 1.5 gather_fusion
  18.4 1.5 gather_fusion.1
  19.8 0.0 copy-start.2
  19.8 0.0 copy-start.5
  19.8 3.4 %copy.18.kseg_ref = s32[8192,1]{1,0:T(8,128)} copy(s32[8192,1]{0,1:T(1,128)} %bitcast.26) | data formatting | bytes 65536 | tf_op jit(solution)/shard_map/reshape | solution.py:143
  23.2 0.0 copy-done.4
  23.3 0.0 copy-done.2
  23.3 0.8 copy.14
  24.1 0.0 copy-done.5
  24.1 0.6 reduce-window.6
  24.7 0.2 slice_reduce_fusion
  24.9 0.6 and_convert_fusion
  25.5 0.7 pad_add_fusion.block_info
  26.2 0.1 fusion.4
  26.3 42.5 %all-gather.2.cloned.1.call-done = bf16[8192,256]{0,1:T(8,128)(2,1)} async-done(((bf16[256,256]{0,1:T(8,128)(2,1)}), bf16[8192,256]{0,1:T(8,128)(2,1)}) %all-gather.2.cloned.1.call-update) | async-done | bytes 4194320 | tf_op jit(solution)/shard_map/all_gather | solution.py:160
  68.9 6.4 %copy.17.k_ref = bf16[8192,256]{1,0:T(8,128)(2,1)} copy(bf16[8192,256]{0,1:T(8,128)(2,1)} %all-gather.2.cloned.1.call-done) | data formatting | bytes 8388608 | tf_op jit(solution)/shard_map/all_gather | solution.py:160
  75.2 3.1 %slice_bitcast_fusion.vt_ref = bf16[128,8192]{1,0:T(8,128)(2,1)} fusion(bf16[8192,256]{0,1:T(8,128)(2,1)} %all-gather.2.cloned.1.call-done), kind=kLoop, calls=%fused_computation.3 | loop fusion | bytes 4194304 | tf_op jit(solution)/shard_map/transpose | solution.py:141
  78.3 6.1 %shard_map.95 = bf16[512,256]{1,0:T(8,128)(2,1)} custom-call(s32[20]{0:T(128)} %pad_add_fusion.block_info, bf16[512,256]{1,0:T(8,128)(2,1)} %bitcast.27, bf16[8192,256]{1,0:T(8,128)(2,1)} %copy.17.k_ref, bf16[128,8192]{1,0:T(8,128)(2,1)} %slice_bitcast_fusion.vt_ref, s32[1,256]{1,0:T(1,128)} %bitcast.28, s32[8192,1]{1,0:T(8,128)} %copy.18.kseg_ref), custom_call_target="tpu_custom_call" | custom-call | tf_op jit(solution)/shard_map/pallas_call | solution.py:137
  84.5 9.3 %convolution_convert_fusion = bf16[512,8192]{1,0:T(8,128)(2,1)} fusion(bf16[512,8192]{1,0:T(8,128)(2,1)} %param.13, bf16[512,256]{1,0:T(8,128)(2,1)} %shard_map.95, s32[256]{0:T(256)S(1)} %multiply_add_fusion), kind=kOutput, calls=%fused_computation.2 | convolution fusion | flops 4433772544 | bytes 17040384 | tf_op jit(solution)/shard_map/dot_general | solution.py:178
  93.8 0.0 copy-start
  93.8 0.0 reduce-scatter.2.cloned.1.call-update
  93.8 0.0 copy-start.3
  93.8 110.9 %reduce-scatter.2.cloned.1.call-done = bf16[64,8192]{1,0:T(8,128)(2,1)} async-done(((bf16[512,8192]{1,0:T(8,128)(2,1)}), bf16[64,8192]{1,0:T(8,128)(2,1)}) %reduce-scatter.2.cloned.1.call-update) | async-done | bytes 1048592 | tf_op jit(solution)/shard_map/reduce_scatter | solution.py:181
  204.7 0.0 copy-done
  204.7 0.0 copy-start.1
  204.7 1.8 multiply_reduce_fusion
  206.5 0.0 copy-done.3
  206.5 0.0 copy-done.1
  206.5 1.8 multiply_convert_fusion
  (8 shorter events, 0.1 us)
Async XLA Ops:
  7.2 61.7 %all-gather.2.cloned.1.call-start = ((), (), s32[]{:S(2)}) async-start(), calls=%async_computation.1 | async-start | bytes 4325376 | tf_op jit(solution)/shard_map/all_gather | solution.py:160
  9.8 194.9 %reduce-scatter.2.cloned.1.call-start = ((), (), s32[]{:S(2)}) async-start(), calls=%async_computation.2 | async-start | bytes 9437184 | tf_op jit(solution)/shard_map/reduce_scatter | solution.py:181
  10.6 12.6 %copy-start.4 = (s32[256]{0:T(256)}, s32[256]{0:T(256)S(1)}, u32[]{:S(2)}) copy-start(s32[256]{0:T(256)S(1)} %dynamic_slice.3) | copy-start | bytes 3076
  19.8 3.4 %copy-start.2 = (bf16[256,512]{1,0:T(8,128)(2,1)S(1)}, bf16[256,512]{1,0:T(8,128)(2,1)}, u32[]{:S(2)}) copy-start(bf16[256,512]{1,0:T(8,128)(2,1)} %param.8) | copy-start | bytes 786436
  19.8 4.3 %copy-start.5 = (s32[256,1]{0,1:T(1,128)S(1)}, s32[256,1]{0,1:T(1,128)}, u32[]{:S(2)}) copy-start(s32[256,1]{0,1:T(1,128)} %param.12) | copy-start | bytes 3076
  93.8 110.9 %copy-start = (bf16[64,8192]{1,0:T(8,128)(2,1)S(1)}, bf16[64,8192]{1,0:T(8,128)(2,1)}, u32[]{:S(2)}) copy-start(bf16[64,8192]{1,0:T(8,128)(2,1)} %param.14) | copy-start | bytes 3145732
  93.8 112.7 %copy-start.3 = (f32[8192]{0:T(1024)S(1)}, f32[8192]{0:T(1024)}, u32[]{:S(2)}) copy-start(f32[8192]{0:T(1024)} %param.15) | copy-start | bytes 98308
  204.7 1.8 copy-start.1
Sparse Core Ops, SparseCore 0:
  11.0 57.7 all-gather.1
  93.9 110.7 reduce-scatter.1

commit v8 on v7

--- a/solution.py
+++ b/solution.py
@@ -17,8 +17,7 @@
 def attention_kernel(
     block_info,
     qt_ref,
-    k_ref,
-    vt_ref,
+    kv_ref,
     qseg_ref,
     kseg_ref,
     out_ref,
@@ -34,8 +33,9 @@
     first_block = block_info[1]
     key_block = my_block - (window - 1) + step
     rows = qt_ref.shape[1]
-    key_width = k_ref.shape[0]
+    key_width = kv_ref.shape[0]
     local_heads = acc_ref.shape[0]
+    kv_cols = kv_ref.shape[1] // 2
     score_scale = 1.0 / math.sqrt(HEAD_DIM)
 
     @pl.when(step == 0)
@@ -49,10 +49,13 @@
             query_pos = block_info[2] + lax.broadcasted_iota(jnp.int32, (1, rows), 1)
             key_pos = key_block * key_width + lax.broadcasted_iota(jnp.int32, (key_width, 1), 0)
             allowed = (kseg_ref[...] == qseg_ref[...]) & (key_pos <= query_pos)
+        values_t = []
+        for kv_head in range(local_heads // group):
+            values = kv_ref[:, kv_cols + kv_head * HEAD_DIM:kv_cols + (kv_head + 1) * HEAD_DIM]
+            values_t.append(values.astype(jnp.float32).T.astype(jnp.bfloat16))
         for head in range(local_heads):
             kv_head = head // group
-            keys = k_ref[:, kv_head * HEAD_DIM:(kv_head + 1) * HEAD_DIM]
-            values_t = vt_ref[kv_head * HEAD_DIM:(kv_head + 1) * HEAD_DIM, :]
+            keys = kv_ref[:, kv_head * HEAD_DIM:(kv_head + 1) * HEAD_DIM]
             query_t = qt_ref[head * HEAD_DIM:(head + 1) * HEAD_DIM, :]
             scores = jnp.dot(keys, query_t, preferred_element_type=jnp.float32) * score_scale
             if masked:
@@ -63,7 +66,7 @@
             factor = jnp.exp(running_max - new_max)
             total_ref[head] = total_ref[head] * factor + jnp.sum(exponent, axis=0, keepdims=True)
             acc_ref[head] = acc_ref[head] * factor + jnp.dot(
-                values_t, exponent.astype(jnp.bfloat16), preferred_element_type=jnp.float32
+                values_t[kv_head], exponent.astype(jnp.bfloat16), preferred_element_type=jnp.float32
             )
             max_ref[head] = new_max
 
@@ -116,8 +119,7 @@
         grid=(window,),
         in_specs=[
             pl.BlockSpec((q_cols, rows), lambda step, info: (0, 0)),
-            pl.BlockSpec((key_width, kv_cols), lambda step, info: (key_index(step, info), 0)),
-            pl.BlockSpec((kv_cols, key_width), lambda step, info: (0, key_index(step, info))),
+            pl.BlockSpec((key_width, 2 * kv_cols), lambda step, info: (key_index(step, info), 0)),
             pl.BlockSpec((1, rows), lambda step, info: (0, 0)),
             pl.BlockSpec((key_width, 1), lambda step, info: (key_index(step, info), 0)),
         ],
@@ -138,7 +140,6 @@
         block_info,
         queries.T,
         kv_all,
-        kv_all[:, kv_cols:].T,
         query_seg.reshape(1, rows),
         segments.reshape(-1, 1),
     )

time: 216 us -> 204 us (0.944)
  local copies, waits for them, and re-layouts: 20.1 us -> 8.97 us
    all_gather x1 -> x0, local copies, waits for them, and re-layouts: 6.35 us -> none  [on_device(): kv_all = lax.all_gather(kv_pair, 'ctx', axis=0, tiled=True)]
    transpose x1 -> x0, local copies, waits for them, and re-layouts: 3.14 us -> none  [attend_window(): kv_all[:, kv_cols:]]
    all_gather x1, waiting for transfers between devices: 42.5 us -> 40.1 us  [on_device(): kv_all = lax.all_gather(kv_pair, 'ctx', axis=0, tiled=True)]
  transfers between devices with their start and end apart: 2 -> 2, of which waited for: 2 -> 2; matrix products, arithmetic and copies ran while one was open for 6% -> 7% of each run, Pallas kernels for 0% -> 0%
where the time goes in v8:
time: 204 us; the launch traced here: 203 us
  waiting for transfers between devices  151 us (74%)
  between operations  17.9 us (9%)
  other arithmetic  9.73 us (5%)
  matrix products  9.32 us (5%)
  local copies, waits for them, and re-layouts  8.97 us (4%)
  Pallas kernels  5.95 us (3%)
    reduce_scatter x1, waiting for transfers between devices, on_device(): lax.psum_scatter(partial_slots, 'tp', scatter_dimension=0, tiled=True)  111 us
    all_gather x1, waiting for transfers between devices, on_device(): kv_all = lax.all_gather(kv_pair, 'ctx', axis=0, tiled=True)  40.1 us
    dot_general x1, matrix products, on_device(): jnp.dot(attended_slots, out_proj, preferred_element_type=jnp.float32)  9.32 us
    pallas_call x1, Pallas kernels, attend_window(): kernel(block_info, queries.T, kv_all, query_seg.reshape(1, rows), segment...  5.95 us
  transfers between devices with their start and end apart: 2, of which 2 were waited for; matrix products, arithmetic and copies ran while one was open for 7% of the time, Pallas kernels for 0%

profile of v8, /device:TPU:1, one launch (start us, length us, event | category | flops | bytes accessed | tf_op | source)
XLA Modules:
  0.0 203.0 jit_solution(14666244410684698397)
XLA Ops:
  7.2 0.0 copy-start
  7.2 0.0 all-gather.2.cloned.1.call-start
  7.2 1.5 pad_maximum_fusion
  8.8 0.0 all-gather.2.cloned.1.call-update
  8.8 0.0 reduce-scatter.2.cloned.1.call-start
  8.8 0.8 dynamic_slice.3
  9.6 0.0 copy-start.4
  9.6 0.6 fusion.8
  10.2 2.0 convert_reduce_fusion
  16.0 1.5 gather_fusion
  17.5 1.5 gather_fusion.1
  18.9 0.7 fusion.5
  19.6 0.6 reduce-window.6
  20.2 0.2 slice_reduce_fusion
  20.4 1.8 copy.11
  22.2 0.0 copy-done
  22.2 0.0 copy-start.5
  22.2 2.7 %copy.12.kseg_ref = s32[8192,1]{1,0:T(8,128)} copy(s32[8192,1]{0,1:T(1,128)S(1)} %bitcast.24) | data formatting | bytes 65536 | tf_op jit(solution)/shard_map/reshape | solution.py:144
  24.9 0.0 copy-done.4
  24.9 0.6 and_convert_fusion
  25.5 0.6 pad_add_fusion.block_info
  26.1 0.0 copy-done.5
  26.1 0.1 fusion.4
  26.2 40.1 %all-gather.2.cloned.1.call-done.kv_ref = bf16[8192,256]{1,0:T(8,128)(2,1)} async-done(((bf16[256,256]{1,0:T(8,128)(2,1)}), bf16[8192,256]{1,0:T(8,128)(2,1)}) %all-gather.2.cloned.1.call-update) | async-done | bytes 4194320 | tf_op jit(solution)/shard_map/all_gather | solution.py:161
  66.4 5.9 %shard_map.95 = bf16[512,256]{1,0:T(8,128)(2,1)} custom-call(s32[20]{0:T(128)} %pad_add_fusion.block_info, bf16[512,256]{1,0:T(8,128)(2,1)} %bitcast.25, bf16[8192,256]{1,0:T(8,128)(2,1)} %all-gather.2.cloned.1.call-done.kv_ref, s32[1,256]{1,0:T(1,128)} %bitcast.26, s32[8192,1]{1,0:T(8,128)} %copy.12.kseg_ref), custom_call_target="tpu_custom_call" | custom-call | tf_op jit(solution)/shard_map/pallas_call | solution.py:139
  72.3 9.3 %convolution_convert_fusion = bf16[512,8192]{1,0:T(8,128)(2,1)} fusion(bf16[512,8192]{1,0:T(8,128)(2,1)} %param.13, bf16[512,256]{1,0:T(8,128)(2,1)} %shard_map.95, s32[256]{0:T(256)S(1)} %multiply_add_fusion), kind=kOutput, calls=%fused_computation.2 | convolution fusion | flops 4433772544 | bytes 17040384 | tf_op jit(solution)/shard_map/dot_general | solution.py:179
  81.6 0.0 copy-start.1
  81.6 0.0 reduce-scatter.2.cloned.1.call-update
  81.7 0.0 copy-start.3
  81.7 110.9 %reduce-scatter.2.cloned.1.call-done = bf16[64,8192]{1,0:T(8,128)(2,1)} async-done(((bf16[512,8192]{1,0:T(8,128)(2,1)}), bf16[64,8192]{1,0:T(8,128)(2,1)}) %reduce-scatter.2.cloned.1.call-update) | async-done | bytes 1048592 | tf_op jit(solution)/shard_map/reduce_scatter | solution.py:182
  192.6 0.0 copy-done.1
  192.6 0.0 copy-start.2
  192.6 1.8 multiply_reduce_fusion
  194.4 0.0 copy-done.3
  194.4 0.0 copy-done.2
  194.4 1.8 multiply_convert_fusion
  (7 shorter events, 0.1 us)
Async XLA Ops:
  7.2 15.1 %copy-start = (s32[8192]{0:T(1024)S(1)}, s32[8192]{0:T(1024)}, u32[]{:S(2)}) copy-start(s32[8192]{0:T(1024)} %param.11) | copy-start | bytes 98308
  7.2 59.2 %all-gather.2.cloned.1.call-start = ((), (), s32[]{:S(2)}) async-start(), calls=%async_computation.1 | async-start | bytes 4325376 | tf_op jit(solution)/shard_map/all_gather | solution.py:161
  8.8 183.8 %reduce-scatter.2.cloned.1.call-start = ((), (), s32[]{:S(2)}) async-start(), calls=%async_computation.2 | async-start | bytes 9437184 | tf_op jit(solution)/shard_map/reduce_scatter | solution.py:182
  9.6 15.3 %copy-start.4 = (s32[256]{0:T(256)}, s32[256]{0:T(256)S(1)}, u32[]{:S(2)}) copy-start(s32[256]{0:T(256)S(1)} %dynamic_slice.3) | copy-start | bytes 3076
  22.2 3.9 %copy-start.5 = (s32[256,1]{0,1:T(1,128)S(1)}, s32[256,1]{0,1:T(1,128)}, u32[]{:S(2)}) copy-start(s32[256,1]{0,1:T(1,128)} %param.12) | copy-start | bytes 3076
  81.6 111.0 %copy-start.1 = (bf16[64,8192]{1,0:T(8,128)(2,1)S(1)}, bf16[64,8192]{1,0:T(8,128)(2,1)}, u32[]{:S(2)}) copy-start(bf16[64,8192]{1,0:T(8,128)(2,1)} %param.14) | copy-start | bytes 3145732
  81.7 112.7 %copy-start.3 = (f32[8192]{0:T(1024)S(1)}, f32[8192]{0:T(1024)}, u32[]{:S(2)}) copy-start(f32[8192]{0:T(1024)} %param.15) | copy-start | bytes 98308
  192.6 1.8 copy-start.2
Sparse Core Ops, SparseCore 0:
  11.1 55.2 all-gather.1
  81.8 110.7 reduce-scatter.1

commit v9 on v8

--- a/solution.py
+++ b/solution.py
@@ -32,9 +32,9 @@
     my_block = block_info[0]
     first_block = block_info[1]
     key_block = my_block - (window - 1) + step
-    rows = qt_ref.shape[1]
+    rows = qt_ref.shape[1] // group
     key_width = kv_ref.shape[0]
-    local_heads = acc_ref.shape[0]
+    local_heads = acc_ref.shape[0] * group
     kv_cols = kv_ref.shape[1] // 2
     score_scale = 1.0 / math.sqrt(HEAD_DIM)
 
@@ -46,29 +46,29 @@
 
     def accumulate(masked):
         if masked:
-            query_pos = block_info[2] + lax.broadcasted_iota(jnp.int32, (1, rows), 1)
+            lane = lax.broadcasted_iota(jnp.int32, (1, group * rows), 1)
+            query_pos = block_info[2] + lane % rows
             key_pos = key_block * key_width + lax.broadcasted_iota(jnp.int32, (key_width, 1), 0)
             allowed = (kseg_ref[...] == qseg_ref[...]) & (key_pos <= query_pos)
-        values_t = []
         for kv_head in range(local_heads // group):
+            keys = kv_ref[:, kv_head * HEAD_DIM:(kv_head + 1) * HEAD_DIM]
             values = kv_ref[:, kv_cols + kv_head * HEAD_DIM:kv_cols + (kv_head + 1) * HEAD_DIM]
-            values_t.append(values.astype(jnp.float32).T.astype(jnp.bfloat16))
-        for head in range(local_heads):
-            kv_head = head // group
-            keys = kv_ref[:, kv_head * HEAD_DIM:(kv_head + 1) * HEAD_DIM]
-            query_t = qt_ref[head * HEAD_DIM:(head + 1) * HEAD_DIM, :]
+            values_t = values.astype(jnp.float32).T.astype(jnp.bfloat16)
+            query_t = qt_ref[kv_head * HEAD_DIM:(kv_head + 1) * HEAD_DIM, :]
             scores = jnp.dot(keys, query_t, preferred_element_type=jnp.float32) * score_scale
             if masked:
                 scores = jnp.where(allowed, scores, -1e30)
-            running_max = max_ref[head]
+            running_max = max_ref[kv_head]
             new_max = jnp.maximum(running_max, jnp.max(scores, axis=0, keepdims=True))
             exponent = jnp.exp(scores - new_max)
             factor = jnp.exp(running_max - new_max)
-            total_ref[head] = total_ref[head] * factor + jnp.sum(exponent, axis=0, keepdims=True)
-            acc_ref[head] = acc_ref[head] * factor + jnp.dot(
-                values_t[kv_head], exponent.astype(jnp.bfloat16), preferred_element_type=jnp.float32
+            total_ref[kv_head] = total_ref[kv_head] * factor + jnp.sum(
+                exponent, axis=0, keepdims=True
             )
-            max_ref[head] = new_max
+            acc_ref[kv_head] = acc_ref[kv_head] * factor + jnp.dot(
+                values_t, exponent.astype(jnp.bfloat16), preferred_element_type=jnp.float32
+            )
+            max_ref[kv_head] = new_max
 
     active = key_block >= first_block
     whole = block_info[3 + step] == 1
@@ -83,9 +83,9 @@
 
     @pl.when(step == window - 1)
     def _():
-        for head in range(local_heads):
-            out_ref[head * HEAD_DIM:(head + 1) * HEAD_DIM, :] = (
-                acc_ref[head] / total_ref[head]
+        for kv_head in range(local_heads // group):
+            out_ref[kv_head * HEAD_DIM:(kv_head + 1) * HEAD_DIM, :] = (
+                acc_ref[kv_head] / total_ref[kv_head]
             ).astype(out_ref.dtype)
 
 
@@ -96,6 +96,12 @@
     window = min(block_count, DOC_MOST // key_width + 1)
     local_heads = q_cols // HEAD_DIM
     kv_cols = kv_all.shape[1] // 2
+    kv_local = local_heads // group
+    queries_t = (
+        queries.reshape(rows, kv_local, group, HEAD_DIM)
+        .transpose(1, 3, 2, 0)
+        .reshape(kv_local * HEAD_DIM, group * rows)
+    )
     global_blocks = my_block - (window - 1) + jnp.arange(window, dtype=jnp.int32)
     clamped = jnp.clip(global_blocks, 0, block_count - 1)
     key_first = segments[clamped * key_width]
@@ -118,32 +124,36 @@
         num_scalar_prefetch=1,
         grid=(window,),
         in_specs=[
-            pl.BlockSpec((q_cols, rows), lambda step, info: (0, 0)),
+            pl.BlockSpec((kv_cols, group * rows), lambda step, info: (0, 0)),
             pl.BlockSpec((key_width, 2 * kv_cols), lambda step, info: (key_index(step, info), 0)),
-            pl.BlockSpec((1, rows), lambda step, info: (0, 0)),
+            pl.BlockSpec((1, group * rows), lambda step, info: (0, 0)),
             pl.BlockSpec((key_width, 1), lambda step, info: (key_index(step, info), 0)),
         ],
-        out_specs=pl.BlockSpec((q_cols, rows), lambda step, info: (0, 0)),
+        out_specs=pl.BlockSpec((kv_cols, group * rows), lambda step, info: (0, 0)),
         scratch_shapes=[
-            pltpu.VMEM((local_heads, 1, rows), jnp.float32),
-            pltpu.VMEM((local_heads, 1, rows), jnp.float32),
-            pltpu.VMEM((local_heads, HEAD_DIM, rows), jnp.float32),
+            pltpu.VMEM((kv_local, 1, group * rows), jnp.float32),
+            pltpu.VMEM((kv_local, 1, group * rows), jnp.float32),
+            pltpu.VMEM((kv_local, HEAD_DIM, group * rows), jnp.float32),
         ],
     )
     kernel = pl.pallas_call(
         functools.partial(attention_kernel, window=window, group=group),
         grid_spec=grid_spec,
-        out_shape=jax.ShapeDtypeStruct((q_cols, rows), jnp.bfloat16),
+        out_shape=jax.ShapeDtypeStruct((kv_cols, group * rows), jnp.bfloat16),
         compiler_params=pltpu.CompilerParams(dimension_semantics=("arbitrary",)),
     )
     attended_t = kernel(
         block_info,
-        queries.T,
+        queries_t,
         kv_all,
-        query_seg.reshape(1, rows),
+        jnp.tile(query_seg, group).reshape(1, group * rows),
         segments.reshape(-1, 1),
     )
-    return attended_t.T
+    return (
+        attended_t.reshape(kv_local, HEAD_DIM, group, rows)
+        .transpose(3, 0, 2, 1)
+        .reshape(rows, q_cols)
+    )
 
 
 def on_device(queries, key_rows, value_rows, segments, owner_ids, out_proj, residual, norm_gain):

time: 204 us -> 200 us (0.980)
  waiting for transfers between devices: 151 us -> 145 us
    reduce_scatter x1, waiting for transfers between devices: 111 us -> 105 us  [on_device(): lax.psum_scatter(partial_slots, 'tp', scatter_dimension=0, tiled=True)]
    reshape x0 -> x4, local copies, waits for them, and re-layouts: none -> 2.42 us  [the longest x2 1.25 us: attend_window(): queries.reshape(rows, kv_local, group, HEAD_DIM).transpose(1, 3, 2, 0)]
where the time goes in v9:
time: 200 us; the launch traced here: 199 us
  waiting for transfers between devices  145 us (72%)
  between operations  17.9 us (9%)
  local copies, waits for them, and re-layouts  10.9 us (5%)
  matrix products  10.4 us (5%)
  other arithmetic  9.73 us (5%)
  Pallas kernels  5.1 us (3%)
    reduce_scatter x1, waiting for transfers between devices, on_device(): lax.psum_scatter(partial_slots, 'tp', scatter_dimension=0, tiled=True)  105 us
    all_gather x1, waiting for transfers between devices, on_device(): kv_all = lax.all_gather(kv_pair, 'ctx', axis=0, tiled=True)  39.4 us
    dot_general x1, matrix products, on_device(): jnp.dot(attended_slots, out_proj, preferred_element_type=jnp.float32)  10.4 us
    pallas_call x1, Pallas kernels, attend_window(): kernel(block_info, queries_t, kv_all, jnp.tile(query_seg, group).reshape(...  5.1 us
  transfers between devices with their start and end apart: 2, of which 2 were waited for; matrix products, arithmetic and copies ran while one was open for 7% of the time, Pallas kernels for 0%

profile of v9, /device:TPU:1, one launch (start us, length us, event | category | flops | bytes accessed | tf_op | source)
XLA Modules:
  0.0 198.7 jit_solution(1071737666168028430)
XLA Ops:
  7.2 0.0 copy-start
  7.2 0.0 all-gather.2.cloned.1.call-start
  7.2 1.5 pad_maximum_fusion
  8.8 0.0 all-gather.2.cloned.1.call-update
  8.8 0.0 reduce-scatter.2.cloned.1.call-start
  8.8 0.8 dynamic_slice.3
  9.6 0.6 fusion.8
  10.2 2.0 %convert_reduce_fusion = s32[]{:T(128)} fusion(s32[8192]{0:T(1024)} %param.11, s32[]{:T(128)} %bitcast.5), kind=kLoop, calls=%fused_computation.11 | loop fusion | flops 24575 | bytes 32776 | tf_op jit(solution)/shard_map/reduce_sum | solution.py:172
  16.0 0.6 copy.15
  16.6 1.5 gather_fusion
  18.1 1.5 gather_fusion.1
  19.5 0.7 fusion.5
  20.2 0.6 reduce-window.6
  20.8 0.2 slice_reduce_fusion
  21.0 1.0 reshape.89
  22.1 0.2 copy.11
  22.3 0.7 copy.14
  23.0 0.0 copy-done
  23.0 0.0 copy-start.4
  23.0 2.6 %copy.12.kseg_ref = s32[8192,1]{1,0:T(8,128)} copy(s32[8192,1]{0,1:T(1,128)S(1)} %bitcast.33) | data formatting | bytes 65536 | tf_op jit(solution)/shard_map/reshape | solution.py:150
  25.7 0.6 and_convert_fusion
  26.3 0.6 pad_add_fusion.block_info
  26.9 0.0 copy-done.4
  26.9 0.1 fusion.4
  27.0 39.4 %all-gather.2.cloned.1.call-done.kv_ref = bf16[8192,256]{1,0:T(8,128)(2,1)} async-done(((bf16[256,256]{1,0:T(8,128)(2,1)}), bf16[8192,256]{1,0:T(8,128)(2,1)}) %all-gather.2.cloned.1.call-update) | async-done | bytes 4194320 | tf_op jit(solution)/shard_map/all_gather | solution.py:171
  66.4 5.1 %shard_map.95 = bf16[128,1024]{1,0:T(8,128)(2,1)} custom-call(s32[20]{0:T(128)} %pad_add_fusion.block_info, bf16[128,1024]{1,0:T(8,128)(2,1)} %bitcast.34, bf16[8192,256]{1,0:T(8,128)(2,1)} %all-gather.2.cloned.1.call-done.kv_ref, s32[1,1024]{1,0:T(1,128)} %bitcast.37, s32[8192,1]{1,0:T(8,128)} %copy.12.kseg_ref), custom_call_target="tpu_custom_call" | custom-call | tf_op jit(solution)/shard_map/pallas_call | solution.py:145
  71.5 1.1 reshape.92
  72.6 10.4 %convolution_convert_fusion = bf16[512,8192]{1,0:T(8,128)(2,1)} fusion(bf16[512,8192]{1,0:T(8,128)(2,1)} %param.13, bf16[256,512]{0,1:T(8,128)(2,1)S(1)} %bitcast.36, s32[256]{0:T(256)S(1)} %multiply_add_fusion), kind=kOutput, calls=%fused_computation.2 | convolution fusion | flops 4433772544 | bytes 17040384 | tf_op jit(solution)/shard_map/dot_general | solution.py:189
  83.1 0.0 copy-start.1
  83.1 0.0 reduce-scatter.2.cloned.1.call-update
  83.1 0.0 copy-start.3
  83.1 105.2 %reduce-scatter.2.cloned.1.call-done = bf16[64,8192]{1,0:T(8,128)(2,1)} async-done(((bf16[512,8192]{1,0:T(8,128)(2,1)}), bf16[64,8192]{1,0:T(8,128)(2,1)}) %reduce-scatter.2.cloned.1.call-update) | async-done | bytes 1048592 | tf_op jit(solution)/shard_map/reduce_scatter | solution.py:192
  188.3 0.0 copy-done.1
  188.3 0.0 copy-start.2
  188.3 1.8 multiply_reduce_fusion
  190.1 0.0 copy-done.3
  190.1 0.0 copy-done.2
  190.1 1.8 multiply_convert_fusion
  (9 shorter events, 0.1 us)
Async XLA Ops:
  7.2 15.9 %copy-start = (s32[8192]{0:T(1024)S(1)}, s32[8192]{0:T(1024)}, u32[]{:S(2)}) copy-start(s32[8192]{0:T(1024)} %param.11) | copy-start | bytes 98308
  7.2 59.2 %all-gather.2.cloned.1.call-start = ((), (), s32[]{:S(2)}) async-start(), calls=%async_computation.1 | async-start | bytes 4325376 | tf_op jit(solution)/shard_map/all_gather | solution.py:171
  8.8 179.5 %reduce-scatter.2.cloned.1.call-start = ((), (), s32[]{:S(2)}) async-start(), calls=%async_computation.2 | async-start | bytes 9437184 | tf_op jit(solution)/shard_map/reduce_scatter | solution.py:192
  23.0 3.9 %copy-start.4 = (s32[256,1]{0,1:T(1,128)S(1)}, s32[256,1]{0,1:T(1,128)}, u32[]{:S(2)}) copy-start(s32[256,1]{0,1:T(1,128)} %param.12) | copy-start | bytes 3076
  83.1 105.3 %copy-start.1 = (bf16[64,8192]{1,0:T(8,128)(2,1)S(1)}, bf16[64,8192]{1,0:T(8,128)(2,1)}, u32[]{:S(2)}) copy-start(bf16[64,8192]{1,0:T(8,128)(2,1)} %param.14) | copy-start | bytes 3145732
  83.1 107.0 %copy-start.3 = (f32[8192]{0:T(1024)S(1)}, f32[8192]{0:T(1024)}, u32[]{:S(2)}) copy-start(f32[8192]{0:T(1024)} %param.15) | copy-start | bytes 98308
  188.3 1.8 copy-start.2
Sparse Core Ops, SparseCore 0:
  11.1 55.2 all-gather.1
  83.2 105.0 reduce-scatter.1

commit v10 on v9

--- a/solution.py
+++ b/solution.py
@@ -18,8 +18,10 @@
     block_info,
     qt_ref,
     kv_ref,
+    kv_next_ref,
     qseg_ref,
     kseg_ref,
+    kseg_next_ref,
     out_ref,
     max_ref,
     total_ref,
@@ -31,7 +33,7 @@
     step = pl.program_id(0)
     my_block = block_info[0]
     first_block = block_info[1]
-    key_block = my_block - (window - 1) + step
+    steps = (window + 1) // 2
     rows = qt_ref.shape[1] // group
     key_width = kv_ref.shape[0]
     local_heads = acc_ref.shape[0] * group
@@ -44,7 +46,7 @@
         total_ref[...] = jnp.zeros(total_ref.shape, jnp.float32)
         acc_ref[...] = jnp.zeros(acc_ref.shape, jnp.float32)
 
-    def accumulate(masked):
+    def accumulate(masked, kv_ref, kseg_ref, key_block):
         if masked:
             lane = lax.broadcasted_iota(jnp.int32, (1, group * rows), 1)
             query_pos = block_info[2] + lane % rows
@@ -70,18 +72,21 @@
             )
             max_ref[kv_head] = new_max
 
-    active = key_block >= first_block
-    whole = block_info[3 + step] == 1
-
-    @pl.when(active & whole)
-    def _():
-        accumulate(False)
-
-    @pl.when(active & jnp.logical_not(whole))
-    def _():
-        accumulate(True)
-
-    @pl.when(step == window - 1)
+    for sub, (kv_sub, kseg_sub) in enumerate(((kv_ref, kseg_ref), (kv_next_ref, kseg_next_ref))):
+        place = 2 * step + sub
+        key_block = my_block - (window - 1) + place
+        active = (key_block >= first_block) & (place < window)
+        whole = block_info[3 + place] == 1
+
+        @pl.when(active & whole)
+        def _():
+            accumulate(False, kv_sub, kseg_sub, key_block)
+
+        @pl.when(active & jnp.logical_not(whole))
+        def _():
+            accumulate(True, kv_sub, kseg_sub, key_block)
+
+    @pl.when(step == steps - 1)
     def _():
         for kv_head in range(local_heads // group):
             out_ref[kv_head * HEAD_DIM:(kv_head + 1) * HEAD_DIM, :] = (
@@ -113,21 +118,32 @@
         & (global_blocks < my_block)
         & (global_blocks >= 0)
     )
+    steps = (window + 1) // 2
     block_info = jnp.concatenate(
-        [jnp.stack([my_block, first_block, my_block * rows]), whole.astype(jnp.int32)]
+        [
+            jnp.stack([my_block, first_block, my_block * rows]),
+            whole.astype(jnp.int32),
+            jnp.zeros((2 * steps - window,), jnp.int32),
+        ]
     ).astype(jnp.int32)
 
-    def key_index(step, info):
-        return jnp.maximum(info[0] - (window - 1) + step, info[1])
+    def key_index(place, info):
+        return jnp.minimum(jnp.maximum(info[0] - (window - 1) + place, info[1]), info[0])
 
     grid_spec = pltpu.PrefetchScalarGridSpec(
         num_scalar_prefetch=1,
-        grid=(window,),
+        grid=(steps,),
         in_specs=[
             pl.BlockSpec((kv_cols, group * rows), lambda step, info: (0, 0)),
-            pl.BlockSpec((key_width, 2 * kv_cols), lambda step, info: (key_index(step, info), 0)),
+            pl.BlockSpec(
+                (key_width, 2 * kv_cols), lambda step, info: (key_index(2 * step, info), 0)
+            ),
+            pl.BlockSpec(
+                (key_width, 2 * kv_cols), lambda step, info: (key_index(2 * step + 1, info), 0)
+            ),
             pl.BlockSpec((1, group * rows), lambda step, info: (0, 0)),
-            pl.BlockSpec((key_width, 1), lambda step, info: (key_index(step, info), 0)),
+            pl.BlockSpec((key_width, 1), lambda step, info: (key_index(2 * step, info), 0)),
+            pl.BlockSpec((key_width, 1), lambda step, info: (key_index(2 * step + 1, info), 0)),
         ],
         out_specs=pl.BlockSpec((kv_cols, group * rows), lambda step, info: (0, 0)),
         scratch_shapes=[
@@ -146,7 +162,9 @@
         block_info,
         queries_t,
         kv_all,
+        kv_all,
         jnp.tile(query_seg, group).reshape(1, group * rows),
+        segments.reshape(-1, 1),
         segments.reshape(-1, 1),
     )
     return (

time: 200 us -> 199 us (level)
  no operation moved by 1% of the time
where the time goes in v10:
time: 199 us; the launch traced here: 198 us
  waiting for transfers between devices  144 us (72%)
  between operations  17.9 us (9%)
  local copies, waits for them, and re-layouts  11.5 us (6%)
  matrix products  10.4 us (5%)
  other arithmetic  9.13 us (5%)
  Pallas kernels  5.21 us (3%)
    reduce_scatter x1, waiting for transfers between devices, on_device(): lax.psum_scatter(partial_slots, 'tp', scatter_dimension=0, tiled=True)  105 us
    all_gather x1, waiting for transfers between devices, on_device(): kv_all = lax.all_gather(kv_pair, 'ctx', axis=0, tiled=True)  39.3 us
    dot_general x1, matrix products, on_device(): jnp.dot(attended_slots, out_proj, preferred_element_type=jnp.float32)  10.4 us
    pallas_call x1, Pallas kernels, attend_window(): kernel(block_info, queries_t, kv_all, kv_all, jnp.tile(query_seg, group)....  5.21 us
  transfers between devices with their start and end apart: 2, of which 2 were waited for; matrix products, arithmetic and copies ran while one was open for 7% of the time, Pallas kernels for 0%

profile of v10, /device:TPU:1, one launch (start us, length us, event | category | flops | bytes accessed | tf_op | source)
XLA Modules:
  0.0 198.3 jit_solution(13249465844623461040)
XLA Ops:
  7.2 0.0 copy-start
  7.2 0.0 all-gather.2.cloned.1.call-start
  7.2 1.5 pad_maximum_fusion
  8.8 0.0 all-gather.2.cloned.1.call-update
  8.8 0.0 reduce-scatter.2.cloned.1.call-start
  8.8 0.8 dynamic_slice.3
  9.6 0.6 fusion.8
  10.2 2.0 %convert_reduce_fusion = s32[]{:T(128)} fusion(s32[8192]{0:T(1024)} %param.11, s32[]{:T(128)} %bitcast.5), kind=kLoop, calls=%fused_computation.11 | loop fusion | flops 24575 | bytes 32776 | tf_op jit(solution)/shard_map/reduce_sum | solution.py:190
  16.0 0.6 copy.16
  16.6 1.5 gather_fusion
  18.1 1.5 gather_fusion.1
  19.5 0.7 fusion.5
  20.2 0.6 reduce-window.6
  20.8 0.2 slice_reduce_fusion
  21.0 1.0 reshape.90
  22.1 0.2 copy.11
  22.3 0.7 copy.15
  23.0 0.0 copy-done
  23.0 0.0 copy-start.4
  23.0 2.6 %copy.12.kseg_ref.kseg_next_ref = s32[8192,1]{1,0:T(8,128)} copy(s32[8192,1]{0,1:T(1,128)S(1)} %bitcast.33) | data formatting | bytes 65536 | tf_op jit(solution)/shard_map/reshape | solution.py:167
  25.7 0.6 and_convert_fusion
  26.3 0.6 concatenate.6.block_info
  26.9 0.0 copy-done.4
  26.9 0.1 fusion.4
  27.0 39.3 %all-gather.2.cloned.1.call-done.kv_ref.kv_next_ref = bf16[8192,256]{1,0:T(8,128)(2,1)} async-done(((bf16[256,256]{1,0:T(8,128)(2,1)}), bf16[8192,256]{1,0:T(8,128)(2,1)}) %all-gather.2.cloned.1.call-update) | async-done | bytes 4194320 | tf_op jit(solution)/shard_map/all_gather | solution.py:189
  66.4 5.2 %shard_map.95 = bf16[128,1024]{1,0:T(8,128)(2,1)} custom-call(s32[21]{0:T(128)} %concatenate.6.block_info, bf16[128,1024]{1,0:T(8,128)(2,1)} %bitcast.34, bf16[8192,256]{1,0:T(8,128)(2,1)} %all-gather.2.cloned.1.call-done.kv_ref.kv_next_ref, bf16[8192,256]{1,0:T(8,128)(2,1)} %all-gather.2.cloned.1.call-done.kv_ref.kv_next_ref, s32[1,1024]{1,0:T(1,128)} %bitcast.37, ...), custom_call_target="tpu_custom_call" | custom-call | tf_op jit(solution)/shard_map/pallas_call | solution.py:161
  71.6 1.1 reshape.93
  72.8 10.4 %convolution_convert_fusion = bf16[512,8192]{1,0:T(8,128)(2,1)} fusion(bf16[512,8192]{1,0:T(8,128)(2,1)} %param.13, bf16[256,512]{0,1:T(8,128)(2,1)S(1)} %bitcast.36, s32[256]{0:T(256)S(1)} %multiply_add_fusion), kind=kOutput, calls=%fused_computation.2 | convolution fusion | flops 4433772544 | bytes 17040384 | tf_op jit(solution)/shard_map/dot_general | solution.py:207
  83.2 0.0 copy-start.1
  83.2 0.0 reduce-scatter.2.cloned.1.call-update
  83.2 0.0 copy-start.3
  83.2 104.6 %reduce-scatter.2.cloned.1.call-done = bf16[64,8192]{1,0:T(8,128)(2,1)} async-done(((bf16[512,8192]{1,0:T(8,128)(2,1)}), bf16[64,8192]{1,0:T(8,128)(2,1)}) %reduce-scatter.2.cloned.1.call-update) | async-done | bytes 1048592 | tf_op jit(solution)/shard_map/reduce_scatter | solution.py:210
  187.9 0.0 copy-done.1
  187.9 0.0 copy-start.2
  187.9 1.8 multiply_reduce_fusion
  189.6 0.0 copy-done.3
  189.6 0.0 copy-done.2
  189.6 1.8 multiply_convert_fusion
  (9 shorter events, 0.1 us)
Async XLA Ops:
  7.2 15.9 %copy-start = (s32[8192]{0:T(1024)S(1)}, s32[8192]{0:T(1024)}, u32[]{:S(2)}) copy-start(s32[8192]{0:T(1024)} %param.11) | copy-start | bytes 98308
  7.2 59.2 %all-gather.2.cloned.1.call-start = ((), (), s32[]{:S(2)}) async-start(), calls=%async_computation.1 | async-start | bytes 4325376 | tf_op jit(solution)/shard_map/all_gather | solution.py:189
  8.8 179.1 %reduce-scatter.2.cloned.1.call-start = ((), (), s32[]{:S(2)}) async-start(), calls=%async_computation.2 | async-start | bytes 9437184 | tf_op jit(solution)/shard_map/reduce_scatter | solution.py:210
  23.0 3.9 %copy-start.4 = (s32[256,1]{0,1:T(1,128)S(1)}, s32[256,1]{0,1:T(1,128)}, u32[]{:S(2)}) copy-start(s32[256,1]{0,1:T(1,128)} %param.12) | copy-start | bytes 3076
  83.2 104.7 %copy-start.1 = (bf16[64,8192]{1,0:T(8,128)(2,1)S(1)}, bf16[64,8192]{1,0:T(8,128)(2,1)}, u32[]{:S(2)}) copy-start(bf16[64,8192]{1,0:T(8,128)(2,1)} %param.14) | copy-start | bytes 3145732
  83.2 106.4 %copy-start.3 = (f32[8192]{0:T(1024)S(1)}, f32[8192]{0:T(1024)}, u32[]{:S(2)}) copy-start(f32[8192]{0:T(1024)} %param.15) | copy-start | bytes 98308
  187.9 1.8 copy-start.2
Sparse Core Ops, SparseCore 0:
  11.1 55.2 all-gather.1
  83.3 104.4 reduce-scatter.1

commit v11 on v10

--- a/solution.py
+++ b/solution.py
@@ -88,10 +88,11 @@
 
     @pl.when(step == steps - 1)
     def _():
-        for kv_head in range(local_heads // group):
-            out_ref[kv_head * HEAD_DIM:(kv_head + 1) * HEAD_DIM, :] = (
-                acc_ref[kv_head] / total_ref[kv_head]
-            ).astype(out_ref.dtype)
+        for head in range(local_heads):
+            kv_head, member = divmod(head, group)
+            lanes = slice(member * rows, (member + 1) * rows)
+            mixed = acc_ref[kv_head, :, lanes] / total_ref[kv_head, :, lanes]
+            out_ref[:, head * HEAD_DIM:(head + 1) * HEAD_DIM] = mixed.T.astype(out_ref.dtype)
 
 
 def attend_window(queries, kv_all, query_seg, segments, my_block, first_block, group):
@@ -145,7 +146,7 @@
             pl.BlockSpec((key_width, 1), lambda step, info: (key_index(2 * step, info), 0)),
             pl.BlockSpec((key_width, 1), lambda step, info: (key_index(2 * step + 1, info), 0)),
         ],
-        out_specs=pl.BlockSpec((kv_cols, group * rows), lambda step, info: (0, 0)),
+        out_specs=pl.BlockSpec((rows, q_cols), lambda step, info: (0, 0)),
         scratch_shapes=[
             pltpu.VMEM((kv_local, 1, group * rows), jnp.float32),
             pltpu.VMEM((kv_local, 1, group * rows), jnp.float32),
@@ -155,7 +156,7 @@
     kernel = pl.pallas_call(
         functools.partial(attention_kernel, window=window, group=group),
         grid_spec=grid_spec,
-        out_shape=jax.ShapeDtypeStruct((kv_cols, group * rows), jnp.bfloat16),
+        out_shape=jax.ShapeDtypeStruct((rows, q_cols), jnp.bfloat16),
         compiler_params=pltpu.CompilerParams(dimension_semantics=("arbitrary",)),
     )
     attended_t = kernel(
@@ -167,11 +168,7 @@
         segments.reshape(-1, 1),
         segments.reshape(-1, 1),
     )
-    return (
-        attended_t.reshape(kv_local, HEAD_DIM, group, rows)
-        .transpose(3, 0, 2, 1)
-        .reshape(rows, q_cols)
-    )
+    return attended_t
 
 
 def on_device(queries, key_rows, value_rows, segments, owner_ids, out_proj, residual, norm_gain):

time: 199 us -> 196 us (0.985)
  no operation moved by 1% of the time
where the time goes in v11:
time: 196 us; the launch traced here: 195 us
  waiting for transfers between devices  143 us (73%)
  between operations  17.9 us (9%)
  local copies, waits for them, and re-layouts  10.4 us (5%)
  matrix products  9.26 us (5%)
  other arithmetic  9.13 us (5%)
  Pallas kernels  5.32 us (3%)
    reduce_scatter x1, waiting for transfers between devices, on_device(): lax.psum_scatter(partial_slots, 'tp', scatter_dimension=0, tiled=True)  104 us
    all_gather x1, waiting for transfers between devices, on_device(): kv_all = lax.all_gather(kv_pair, 'ctx', axis=0, tiled=True)  39.3 us
    dot_general x1, matrix products, on_device(): jnp.dot(attended_slots, out_proj, preferred_element_type=jnp.float32)  9.26 us
    pallas_call x1, Pallas kernels, attend_window(): kernel(block_info, queries_t, kv_all, kv_all, jnp.tile(query_seg, group)....  5.32 us
  transfers between devices with their start and end apart: 2, of which 2 were waited for; matrix products, arithmetic and copies ran while one was open for 7% of the time, Pallas kernels for 0%

profile of v11, /device:TPU:1, one launch (start us, length us, event | category | flops | bytes accessed | tf_op | source)
XLA Modules:
  0.0 195.1 jit_solution(2999335458518889575)
XLA Ops:
  7.2 0.0 copy-start
  7.2 0.0 all-gather.2.cloned.1.call-start
  7.2 1.5 pad_maximum_fusion
  8.8 0.0 all-gather.2.cloned.1.call-update
  8.8 0.0 reduce-scatter.2.cloned.1.call-start
  8.8 0.8 dynamic_slice.3
  9.6 0.6 fusion.8
  10.2 2.0 %convert_reduce_fusion = s32[]{:T(128)} fusion(s32[8192]{0:T(1024)} %param.11, s32[]{:T(128)} %bitcast.5), kind=kLoop, calls=%fused_computation.11 | loop fusion | flops 24575 | bytes 32776 | tf_op jit(solution)/shard_map/reduce_sum | solution.py:187
  16.0 0.6 copy.15
  16.6 1.5 gather_fusion
  18.1 1.5 gather_fusion.1
  19.5 0.7 fusion.5
  20.2 0.6 reduce-window.6
  20.8 0.2 slice_reduce_fusion
  21.0 1.0 reshape.84
  22.1 0.2 copy.11
  22.3 0.7 copy.14
  23.0 0.0 copy-done
  23.0 0.0 copy-start.4
  23.0 2.6 %copy.12.kseg_ref.kseg_next_ref = s32[8192,1]{1,0:T(8,128)} copy(s32[8192,1]{0,1:T(1,128)S(1)} %bitcast.30) | data formatting | bytes 65536 | tf_op jit(solution)/shard_map/reshape | solution.py:168
  25.7 0.6 and_convert_fusion
  26.3 0.6 concatenate.6.block_info
  26.9 0.0 copy-done.4
  26.9 0.1 fusion.4
  27.0 39.3 %all-gather.2.cloned.1.call-done.kv_ref.kv_next_ref = bf16[8192,256]{1,0:T(8,128)(2,1)} async-done(((bf16[256,256]{1,0:T(8,128)(2,1)}), bf16[8192,256]{1,0:T(8,128)(2,1)}) %all-gather.2.cloned.1.call-update) | async-done | bytes 4194320 | tf_op jit(solution)/shard_map/all_gather | solution.py:186
  66.4 5.3 %shard_map.95 = bf16[256,512]{1,0:T(8,128)(2,1)} custom-call(s32[21]{0:T(128)} %concatenate.6.block_info, bf16[128,1024]{1,0:T(8,128)(2,1)} %bitcast.31, bf16[8192,256]{1,0:T(8,128)(2,1)} %all-gather.2.cloned.1.call-done.kv_ref.kv_next_ref, bf16[8192,256]{1,0:T(8,128)(2,1)} %all-gather.2.cloned.1.call-done.kv_ref.kv_next_ref, s32[1,1024]{1,0:T(1,128)} %bitcast.33, ...), custom_call_target="tpu_custom_call" | custom-call | tf_op jit(solution)/shard_map/pallas_call | solution.py:162
  71.7 9.3 %convolution_convert_fusion = bf16[512,8192]{1,0:T(8,128)(2,1)} fusion(bf16[512,8192]{1,0:T(8,128)(2,1)} %param.13, bf16[256,512]{1,0:T(8,128)(2,1)} %shard_map.95, s32[256]{0:T(256)S(1)} %multiply_add_fusion), kind=kOutput, calls=%fused_computation.2 | convolution fusion | flops 4433772544 | bytes 17040384 | tf_op jit(solution)/shard_map/dot_general | solution.py:204
  80.9 0.0 copy-start.1
  80.9 0.0 reduce-scatter.2.cloned.1.call-update
  81.0 0.0 copy-start.3
  81.0 103.8 %reduce-scatter.2.cloned.1.call-done = bf16[64,8192]{1,0:T(8,128)(2,1)} async-done(((bf16[512,8192]{1,0:T(8,128)(2,1)}), bf16[64,8192]{1,0:T(8,128)(2,1)}) %reduce-scatter.2.cloned.1.call-update) | async-done | bytes 1048592 | tf_op jit(solution)/shard_map/reduce_scatter | solution.py:207
  184.7 0.0 copy-done.1
  184.7 0.0 copy-start.2
  184.7 1.8 multiply_reduce_fusion
  186.5 0.0 copy-done.3
  186.5 0.0 copy-done.2
  186.5 1.8 multiply_convert_fusion
  (8 shorter events, 0.1 us)
Async XLA Ops:
  7.2 15.9 %copy-start = (s32[8192]{0:T(1024)S(1)}, s32[8192]{0:T(1024)}, u32[]{:S(2)}) copy-start(s32[8192]{0:T(1024)} %param.11) | copy-start | bytes 98308
  7.2 59.2 %all-gather.2.cloned.1.call-start = ((), (), s32[]{:S(2)}) async-start(), calls=%async_computation.1 | async-start | bytes 4325376 | tf_op jit(solution)/shard_map/all_gather | solution.py:186
  8.8 175.9 %reduce-scatter.2.cloned.1.call-start = ((), (), s32[]{:S(2)}) async-start(), calls=%async_computation.2 | async-start | bytes 9437184 | tf_op jit(solution)/shard_map/reduce_scatter | solution.py:207
  23.0 3.9 %copy-start.4 = (s32[256,1]{0,1:T(1,128)S(1)}, s32[256,1]{0,1:T(1,128)}, u32[]{:S(2)}) copy-start(s32[256,1]{0,1:T(1,128)} %param.12) | copy-start | bytes 3076
  80.9 103.8 %copy-start.1 = (bf16[64,8192]{1,0:T(8,128)(2,1)S(1)}, bf16[64,8192]{1,0:T(8,128)(2,1)}, u32[]{:S(2)}) copy-start(bf16[64,8192]{1,0:T(8,128)(2,1)} %param.14) | copy-start | bytes 3145732
  81.0 105.5 %copy-start.3 = (f32[8192]{0:T(1024)S(1)}, f32[8192]{0:T(1024)}, u32[]{:S(2)}) copy-start(f32[8192]{0:T(1024)} %param.15) | copy-start | bytes 98308
  184.7 1.8 copy-start.2
Sparse Core Ops, SparseCore 0:
  11.1 55.2 all-gather.1
  81.1 103.5 reduce-scatter.1

commit v12 on v11

--- a/solution.py
+++ b/solution.py
@@ -171,6 +171,30 @@
     return attended_t
 
 
+def norm_kernel(residual_ref, rows_ref, gain_ref, hidden_ref, normed_ref):
+    hidden_sum = residual_ref[...].astype(jnp.float32) + rows_ref[...].astype(jnp.float32)
+    mean_square = jnp.mean(hidden_sum * hidden_sum, axis=-1, keepdims=True)
+    normed = hidden_sum * lax.rsqrt(mean_square + 1e-05) * gain_ref[...]
+    hidden_ref[...] = hidden_sum.astype(hidden_ref.dtype)
+    normed_ref[...] = normed.astype(normed_ref.dtype)
+
+
+def add_and_norm(residual, owned_rows, norm_gain):
+    slot_count, width = residual.shape
+    block_rows = 16 if slot_count % 16 == 0 else slot_count
+    row_spec = pl.BlockSpec((block_rows, width), lambda step: (step, 0))
+    return pl.pallas_call(
+        norm_kernel,
+        grid=(slot_count // block_rows,),
+        in_specs=[row_spec, row_spec, pl.BlockSpec((1, width), lambda step: (0, 0))],
+        out_specs=(row_spec, row_spec),
+        out_shape=(
+            jax.ShapeDtypeStruct((slot_count, width), jnp.bfloat16),
+            jax.ShapeDtypeStruct((slot_count, width), jnp.bfloat16),
+        ),
+    )(residual, owned_rows, norm_gain.reshape(1, width))
+
+
 def on_device(queries, key_rows, value_rows, segments, owner_ids, out_proj, residual, norm_gain):
     rows_here = queries.shape[0]
     kv_local = key_rows.shape[1] // HEAD_DIM
@@ -204,13 +228,8 @@
     partial_slots = jnp.dot(attended_slots, out_proj, preferred_element_type=jnp.float32).astype(
         jnp.bfloat16
     )
-    owned_rows = lax.psum_scatter(partial_slots, "tp", scatter_dimension=0, tiled=True).astype(
-        jnp.float32
-    )
-    hidden_sum = residual.astype(jnp.float32) + owned_rows
-    mean_square = jnp.mean(hidden_sum * hidden_sum, axis=-1, keepdims=True)
-    normed = hidden_sum * lax.rsqrt(mean_square + 1e-05) * norm_gain
-    return (hidden_sum.astype(jnp.bfloat16), normed.astype(jnp.bfloat16))
+    owned_rows = lax.psum_scatter(partial_slots, "tp", scatter_dimension=0, tiled=True)
+    return add_and_norm(residual, owned_rows, norm_gain)
 
 
 def solution(mesh):

time: 196 us -> 197 us (level)
  Pallas kernels: 5.32 us -> 9.3 us
  other arithmetic: 9.13 us -> 6.96 us
    pallas_call x0 -> x1, Pallas kernels: none -> 3.99 us  [add_and_norm(): pl.pallas_call(norm_kernel, grid=(slot_count // block_rows,), in_specs=[r...]
    all_gather x1, waiting for transfers between devices: 39.3 us -> 37.3 us  [on_device(): kv_all = lax.all_gather(kv_pair, 'ctx', axis=0, tiled=True)]
  transfers between devices with their start and end apart: 2 -> 2, of which waited for: 2 -> 2; matrix products, arithmetic and copies ran while one was open for 7% -> 8% of each run, Pallas kernels for 0% -> 0%
where the time goes in v12:
time: 197 us; the launch traced here: 196 us
  waiting for transfers between devices  142 us (72%)
  between operations  17.8 us (9%)
  local copies, waits for them, and re-layouts  11 us (6%)
  Pallas kernels  9.3 us (5%)
  matrix products  9.26 us (5%)
  other arithmetic  6.96 us (4%)
    reduce_scatter x1, waiting for transfers between devices, on_device(): lax.psum_scatter(partial_slots, 'tp', scatter_dimension=0, tiled=True)  105 us
    all_gather x1, waiting for transfers between devices, on_device(): kv_all = lax.all_gather(kv_pair, 'ctx', axis=0, tiled=True)  37.3 us
    dot_general x1, matrix products, on_device(): jnp.dot(attended_slots, out_proj, preferred_element_type=jnp.float32)  9.26 us
    pallas_call x1, Pallas kernels, attend_window(): kernel(block_info, queries_t, kv_all, kv_all, jnp.tile(query_seg, group)....  5.32 us
    pallas_call x1, Pallas kernels, add_and_norm(): pl.pallas_call(norm_kernel, grid=(slot_count // block_rows,), in_specs=[r...  3.99 us
  transfers between devices with their start and end apart: 2, of which 2 were waited for; matrix products, arithmetic and copies ran while one was open for 8% of the time, Pallas kernels for 0%

profile of v12, /device:TPU:1, one launch (start us, length us, event | category | flops | bytes accessed | tf_op | source)
XLA Modules:
  0.0 196.4 jit_solution(14269876031160878313)
XLA Ops:
  7.2 0.0 all-gather.2.cloned.1.call-start
  7.2 1.5 pad_maximum_fusion
  8.8 0.0 all-gather.2.cloned.1.call-update
  8.8 0.0 reduce-scatter.2.cloned.1.call-start
  8.8 0.8 dynamic_slice.3
  9.6 0.6 fusion.7
  10.2 2.0 %convert_reduce_fusion = s32[]{:T(128)} fusion(s32[8192]{0:T(1024)} %param.11, s32[]{:T(128)} %bitcast.5), kind=kLoop, calls=%fused_computation.7 | loop fusion | flops 24575 | bytes 32776 | tf_op jit(solution)/shard_map/reduce_sum | solution.py:211
  16.0 0.6 copy.15
  16.6 1.5 gather_fusion
  18.1 1.5 gather_fusion.1
  19.5 0.7 fusion.4
  20.2 0.6 reduce-window.6
  20.8 0.2 slice_reduce_fusion
  21.0 1.0 reshape.78
  22.1 0.2 copy.11
  22.3 0.7 copy.14
  23.0 3.4 %copy.12.kseg_ref.kseg_next_ref = s32[8192,1]{1,0:T(8,128)} copy(s32[8192,1]{0,1:T(1,128)} %bitcast.31) | data formatting | bytes 65536 | tf_op jit(solution)/shard_map/reshape | solution.py:168
  26.4 0.6 and_convert_fusion
  27.0 0.6 concatenate.6.block_info
  27.6 0.8 fusion.3
  28.4 0.7 multiply_add_fusion
  29.1 37.3 %all-gather.2.cloned.1.call-done.kv_ref.kv_next_ref = bf16[8192,256]{1,0:T(8,128)(2,1)} async-done(((bf16[256,256]{1,0:T(8,128)(2,1)}), bf16[8192,256]{1,0:T(8,128)(2,1)}) %all-gather.2.cloned.1.call-update) | async-done | bytes 4194320 | tf_op jit(solution)/shard_map/all_gather | solution.py:210
  66.4 5.3 %shard_map.95 = bf16[256,512]{1,0:T(8,128)(2,1)} custom-call(s32[21]{0:T(128)} %concatenate.6.block_info, bf16[128,1024]{1,0:T(8,128)(2,1)} %bitcast.32, bf16[8192,256]{1,0:T(8,128)(2,1)} %all-gather.2.cloned.1.call-done.kv_ref.kv_next_ref, bf16[8192,256]{1,0:T(8,128)(2,1)} %all-gather.2.cloned.1.call-done.kv_ref.kv_next_ref, s32[1,1024]{1,0:T(1,128)} %bitcast.35, ...), custom_call_target="tpu_custom_call" | custom-call | tf_op jit(solution)/shard_map/pallas_call | solution.py:162
  71.7 9.3 %convolution_convert_fusion = bf16[512,8192]{1,0:T(8,128)(2,1)} fusion(bf16[512,8192]{1,0:T(8,128)(2,1)} %param.13, bf16[256,512]{1,0:T(8,128)(2,1)} %shard_map.95, s32[256]{0:T(256)S(1)} %multiply_add_fusion), kind=kOutput, calls=%fused_computation.2 | convolution fusion | flops 4433772544 | bytes 17040384 | tf_op jit(solution)/shard_map/dot_general | solution.py:228
  80.9 0.0 reduce-scatter.2.cloned.1.call-update
  81.0 104.7 %reduce-scatter.2.cloned.1.call-done.rows_ref = bf16[64,8192]{1,0:T(8,128)(2,1)} async-done(((bf16[512,8192]{1,0:T(8,128)(2,1)}), bf16[64,8192]{1,0:T(8,128)(2,1)}) %reduce-scatter.2.cloned.1.call-update) | async-done | bytes 1048592 | tf_op jit(solution)/shard_map/reduce_scatter | solution.py:231
  185.6 4.0 %shard_map.96 = (bf16[64,8192]{1,0:T(8,128)(2,1)}, bf16[64,8192]{1,0:T(8,128)(2,1)}) custom-call(bf16[64,8192]{1,0:T(8,128)(2,1)} %residual_ref.1, bf16[64,8192]{1,0:T(8,128)(2,1)} %reduce-scatter.2.cloned.1.call-done.rows_ref, f32[1,8192]{1,0:T(1,128)} %bitcast.34), custom_call_target="tpu_custom_call" | custom-call | tf_op jit(solution)/shard_map/pallas_call | solution.py:186
  (6 shorter events, 0.1 us)
Async XLA Ops:
  7.2 59.2 %all-gather.2.cloned.1.call-start = ((), (), s32[]{:S(2)}) async-start(), calls=%async_computation.1 | async-start | bytes 4325376 | tf_op jit(solution)/shard_map/all_gather | solution.py:210
  8.8 176.8 %reduce-scatter.2.cloned.1.call-start = ((), (), s32[]{:S(2)}) async-start(), calls=%async_computation.2 | async-start | bytes 9437184 | tf_op jit(solution)/shard_map/reduce_scatter | solution.py:231
Sparse Core Ops, SparseCore 0:
  11.1 55.2 all-gather.1
  81.1 104.4 reduce-scatter.1

commit v13 on v11

--- a/solution.py
+++ b/solution.py
@@ -201,6 +201,7 @@
     attended_slots = jnp.dot(select, attended, preferred_element_type=jnp.float32).astype(
         jnp.bfloat16
     )
+    attended_slots = lax.optimization_barrier(attended_slots)
     partial_slots = jnp.dot(attended_slots, out_proj, preferred_element_type=jnp.float32).astype(
         jnp.bfloat16
     )

time: 196 us -> 199 us (1.015)
  matrix products: 9.26 us -> 11.3 us
where the time goes in v13:
time: 199 us; the launch traced here: 198 us
  waiting for transfers between devices  143 us (72%)
  between operations  17.9 us (9%)
  matrix products  11.3 us (6%)
  local copies, waits for them, and re-layouts  10.4 us (5%)
  other arithmetic  9.13 us (5%)
  Pallas kernels  5.32 us (3%)
    reduce_scatter x1, waiting for transfers between devices, on_device(): lax.psum_scatter(partial_slots, 'tp', scatter_dimension=0, tiled=True)  104 us
    all_gather x1, waiting for transfers between devices, on_device(): kv_all = lax.all_gather(kv_pair, 'ctx', axis=0, tiled=True)  39.3 us
    dot_general x1, matrix products, on_device(): jnp.dot(attended_slots, out_proj, preferred_element_type=jnp.float32)  10.1 us
    pallas_call x1, Pallas kernels, attend_window(): kernel(block_info, queries_t, kv_all, kv_all, jnp.tile(query_seg, group)....  5.32 us
  transfers between devices with their start and end apart: 2, of which 2 were waited for; matrix products, arithmetic and copies ran while one was open for 7% of the time, Pallas kernels for 0%

profile of v13, /device:TPU:1, one launch (start us, length us, event | category | flops | bytes accessed | tf_op | source)
XLA Modules:
  0.0 197.5 jit_solution(6141112668226852758)
XLA Ops:
  7.2 0.0 copy-start
  7.2 0.0 all-gather.2.cloned.1.call-start
  7.2 1.5 pad_maximum_fusion
  8.8 0.0 all-gather.2.cloned.1.call-update
  8.8 0.0 reduce-scatter.2.cloned.1.call-start
  8.8 0.8 dynamic_slice.3
  9.6 0.6 fusion.7
  10.2 2.0 %convert_reduce_fusion = s32[]{:T(128)} fusion(s32[8192]{0:T(1024)} %param.11, s32[]{:T(128)} %bitcast.5), kind=kLoop, calls=%fused_computation.11 | loop fusion | flops 24575 | bytes 32776 | tf_op jit(solution)/shard_map/reduce_sum | solution.py:187
  16.0 0.6 copy.15
  16.6 1.5 gather_fusion
  18.1 1.5 gather_fusion.1
  19.5 0.7 fusion.4
  20.2 0.6 reduce-window.6
  20.8 0.2 slice_reduce_fusion
  21.0 1.0 reshape.84
  22.1 0.2 copy.11
  22.3 0.7 copy.14
  23.0 0.0 copy-done
  23.0 0.0 copy-start.4
  23.0 2.6 %copy.12.kseg_ref.kseg_next_ref = s32[8192,1]{1,0:T(8,128)} copy(s32[8192,1]{0,1:T(1,128)S(1)} %bitcast.31) | data formatting | bytes 65536 | tf_op jit(solution)/shard_map/reshape | solution.py:168
  25.7 0.6 and_convert_fusion
  26.3 0.6 concatenate.6.block_info
  26.9 0.0 copy-done.4
  26.9 0.1 fusion.3
  27.0 39.3 %all-gather.2.cloned.1.call-done.kv_ref.kv_next_ref = bf16[8192,256]{1,0:T(8,128)(2,1)} async-done(((bf16[256,256]{1,0:T(8,128)(2,1)}), bf16[8192,256]{1,0:T(8,128)(2,1)}) %all-gather.2.cloned.1.call-update) | async-done | bytes 4194320 | tf_op jit(solution)/shard_map/all_gather | solution.py:186
  66.4 5.3 %shard_map.95 = bf16[256,512]{1,0:T(8,128)(2,1)} custom-call(s32[21]{0:T(128)} %concatenate.6.block_info, bf16[128,1024]{1,0:T(8,128)(2,1)} %bitcast.32, bf16[8192,256]{1,0:T(8,128)(2,1)} %all-gather.2.cloned.1.call-done.kv_ref.kv_next_ref, bf16[8192,256]{1,0:T(8,128)(2,1)} %all-gather.2.cloned.1.call-done.kv_ref.kv_next_ref, s32[1,1024]{1,0:T(1,128)} %bitcast.34, ...), custom_call_target="tpu_custom_call" | custom-call | tf_op jit(solution)/shard_map/pallas_call | solution.py:162
  71.7 1.2 convolution_convert_fusion.1
  72.9 10.1 %convolution_convert_fusion = bf16[512,8192]{1,0:T(8,128)(2,1)} fusion(bf16[512,512]{1,0:T(8,128)(2,1)S(1)} %convolution_convert_fusion.1, bf16[512,8192]{1,0:T(8,128)(2,1)} %param.13), kind=kOutput, calls=%fused_computation.2 | convolution fusion | flops 4299161600 | bytes 17301504 | tf_op jit(solution)/shard_map/dot_general | solution.py:205
  83.0 0.0 copy-start.1
  83.0 0.0 reduce-scatter.2.cloned.1.call-update
  83.0 0.0 copy-start.3
  83.1 104.1 %reduce-scatter.2.cloned.1.call-done = bf16[64,8192]{1,0:T(8,128)(2,1)} async-done(((bf16[512,8192]{1,0:T(8,128)(2,1)}), bf16[64,8192]{1,0:T(8,128)(2,1)}) %reduce-scatter.2.cloned.1.call-update) | async-done | bytes 1048592 | tf_op jit(solution)/shard_map/reduce_scatter | solution.py:208
  187.1 0.0 copy-done.1
  187.1 0.0 copy-start.2
  187.1 1.8 multiply_reduce_fusion
  188.9 0.0 copy-done.3
  188.9 0.0 copy-done.2
  188.9 1.8 multiply_convert_fusion
  (8 shorter events, 0.1 us)
Async XLA Ops:
  7.2 15.9 %copy-start = (s32[8192]{0:T(1024)S(1)}, s32[8192]{0:T(1024)}, u32[]{:S(2)}) copy-start(s32[8192]{0:T(1024)} %param.11) | copy-start | bytes 98308
  7.2 59.2 %all-gather.2.cloned.1.call-start = ((), (), s32[]{:S(2)}) async-start(), calls=%async_computation.1 | async-start | bytes 4325376 | tf_op jit(solution)/shard_map/all_gather | solution.py:186
  8.8 178.3 %reduce-scatter.2.cloned.1.call-start = ((), (), s32[]{:S(2)}) async-start(), calls=%async_computation.2 | async-start | bytes 9437184 | tf_op jit(solution)/shard_map/reduce_scatter | solution.py:208
  23.0 3.9 %copy-start.4 = (s32[256,1]{0,1:T(1,128)S(1)}, s32[256,1]{0,1:T(1,128)}, u32[]{:S(2)}) copy-start(s32[256,1]{0,1:T(1,128)} %param.12) | copy-start | bytes 3076
  83.0 104.1 %copy-start.1 = (bf16[64,8192]{1,0:T(8,128)(2,1)S(1)}, bf16[64,8192]{1,0:T(8,128)(2,1)}, u32[]{:S(2)}) copy-start(bf16[64,8192]{1,0:T(8,128)(2,1)} %param.14) | copy-start | bytes 3145732
  83.0 105.8 %copy-start.3 = (f32[8192]{0:T(1024)S(1)}, f32[8192]{0:T(1024)}, u32[]{:S(2)}) copy-start(f32[8192]{0:T(1024)} %param.15) | copy-start | bytes 98308
  187.1 1.8 copy-start.2
Sparse Core Ops, SparseCore 0:
  11.1 55.2 all-gather.1
  83.2 103.9 reduce-scatter.1

commit v14 on v11

--- a/solution.py
+++ b/solution.py
@@ -12,28 +12,25 @@
 KV_HEADS = 8
 HEAD_DIM = 128
 DOC_MOST = 4096
+PER_STEP = 3
 
 
 def attention_kernel(
     block_info,
     qt_ref,
-    kv_ref,
-    kv_next_ref,
-    qseg_ref,
-    kseg_ref,
-    kseg_next_ref,
-    out_ref,
-    max_ref,
-    total_ref,
-    acc_ref,
-    *,
+    *refs,
     window,
     group,
 ):
+    kv_refs = refs[:PER_STEP]
+    qseg_ref = refs[PER_STEP]
+    kseg_refs = refs[PER_STEP + 1:2 * PER_STEP + 1]
+    out_ref, max_ref, total_ref, acc_ref = refs[2 * PER_STEP + 1:]
+    kv_ref = kv_refs[0]
     step = pl.program_id(0)
     my_block = block_info[0]
     first_block = block_info[1]
-    steps = (window + 1) // 2
+    steps = -(-window // PER_STEP)
     rows = qt_ref.shape[1] // group
     key_width = kv_ref.shape[0]
     local_heads = acc_ref.shape[0] * group
@@ -72,8 +69,8 @@
             )
             max_ref[kv_head] = new_max
 
-    for sub, (kv_sub, kseg_sub) in enumerate(((kv_ref, kseg_ref), (kv_next_ref, kseg_next_ref))):
-        place = 2 * step + sub
+    for sub, (kv_sub, kseg_sub) in enumerate(zip(kv_refs, kseg_refs)):
+        place = PER_STEP * step + sub
         key_block = my_block - (window - 1) + place
         active = (key_block >= first_block) & (place < window)
         whole = block_info[3 + place] == 1
@@ -119,12 +116,12 @@
         & (global_blocks < my_block)
         & (global_blocks >= 0)
     )
-    steps = (window + 1) // 2
+    steps = -(-window // PER_STEP)
     block_info = jnp.concatenate(
         [
             jnp.stack([my_block, first_block, my_block * rows]),
             whole.astype(jnp.int32),
-            jnp.zeros((2 * steps - window,), jnp.int32),
+            jnp.zeros((PER_STEP * steps - window,), jnp.int32),
         ]
     ).astype(jnp.int32)
 
@@ -134,17 +131,21 @@
     grid_spec = pltpu.PrefetchScalarGridSpec(
         num_scalar_prefetch=1,
         grid=(steps,),
-        in_specs=[
-            pl.BlockSpec((kv_cols, group * rows), lambda step, info: (0, 0)),
+        in_specs=[pl.BlockSpec((kv_cols, group * rows), lambda step, info: (0, 0))]
+        + [
             pl.BlockSpec(
-                (key_width, 2 * kv_cols), lambda step, info: (key_index(2 * step, info), 0)
-            ),
+                (key_width, 2 * kv_cols),
+                functools.partial(lambda sub, step, info: (key_index(PER_STEP * step + sub, info), 0), sub),
+            )
+            for sub in range(PER_STEP)
+        ]
+        + [pl.BlockSpec((1, group * rows), lambda step, info: (0, 0))]
+        + [
             pl.BlockSpec(
-                (key_width, 2 * kv_cols), lambda step, info: (key_index(2 * step + 1, info), 0)
-            ),
-            pl.BlockSpec((1, group * rows), lambda step, info: (0, 0)),
-            pl.BlockSpec((key_width, 1), lambda step, info: (key_index(2 * step, info), 0)),
-            pl.BlockSpec((key_width, 1), lambda step, info: (key_index(2 * step + 1, info), 0)),
+                (key_width, 1),
+                functools.partial(lambda sub, step, info: (key_index(PER_STEP * step + sub, info), 0), sub),
+            )
+            for sub in range(PER_STEP)
         ],
         out_specs=pl.BlockSpec((rows, q_cols), lambda step, info: (0, 0)),
         scratch_shapes=[
@@ -162,11 +163,9 @@
     attended_t = kernel(
         block_info,
         queries_t,
-        kv_all,
-        kv_all,
+        *([kv_all] * PER_STEP),
         jnp.tile(query_seg, group).reshape(1, group * rows),
-        segments.reshape(-1, 1),
-        segments.reshape(-1, 1),
+        *([segments.reshape(-1, 1)] * PER_STEP),
     )
     return attended_t
 

time: 196 us -> 196 us (level)
  no operation moved by 1% of the time
where the time goes in v14:
time: 196 us
  waiting for transfers between devices  143 us (73%)
  between operations  17.9 us (9%)
  local copies, waits for them, and re-layouts  10.4 us (5%)
  matrix products  9.27 us (5%)
  other arithmetic  9.13 us (5%)
  Pallas kernels  6.05 us (3%)
    reduce_scatter x1, waiting for transfers between devices, on_device(): lax.psum_scatter(partial_slots, 'tp', scatter_dimension=0, tiled=True)  104 us
    all_gather x1, waiting for transfers between devices, on_device(): kv_all = lax.all_gather(kv_pair, 'ctx', axis=0, tiled=True)  39.3 us
    dot_general x1, matrix products, on_device(): jnp.dot(attended_slots, out_proj, preferred_element_type=jnp.float32)  9.27 us
    pallas_call x1, Pallas kernels, attend_window(): kernel(block_info, queries_t, *[kv_all] * PER_STEP, jnp.tile(query_seg, g...  6.05 us
  transfers between devices with their start and end apart: 2, of which 2 were waited for; matrix products, arithmetic and copies ran while one was open for 7% of the time, Pallas kernels for 0%

profile of v14, /device:TPU:1, one launch (start us, length us, event | category | flops | bytes accessed | tf_op | source)
XLA Modules:
  0.0 196.1 jit_solution(10183012515657614236)
XLA Ops:
  7.2 0.0 copy-start
  7.2 0.0 all-gather.2.cloned.1.call-start
  7.2 1.5 pad_maximum_fusion
  8.8 0.0 all-gather.2.cloned.1.call-update
  8.8 0.0 reduce-scatter.2.cloned.1.call-start
  8.8 0.8 dynamic_slice.3
  9.6 0.6 fusion.8
  10.2 2.0 %convert_reduce_fusion = s32[]{:T(128)} fusion(s32[8192]{0:T(1024)} %param.11, s32[]{:T(128)} %bitcast.5), kind=kLoop, calls=%fused_computation.11 | loop fusion | flops 24575 | bytes 32776 | tf_op jit(solution)/shard_map/reduce_sum | solution.py:186
  16.0 0.6 copy.16
  16.6 1.5 gather_fusion
  18.1 1.5 gather_fusion.1
  19.5 0.7 fusion.5
  20.2 0.6 reduce-window.6
  20.8 0.2 slice_reduce_fusion
  21.0 1.0 reshape.83
  22.1 0.2 copy.11
  22.3 0.7 copy.15
  23.0 0.0 copy-done
  23.0 0.0 copy-start.4
  23.0 2.6 %copy.12.refs_4_.refs_5_.refs_6_ = s32[8192,1]{1,0:T(8,128)} copy(s32[8192,1]{0,1:T(1,128)S(1)} %bitcast.30) | data formatting | bytes 65536 | tf_op jit(solution)/shard_map/reshape | solution.py:168
  25.7 0.6 and_convert_fusion
  26.3 0.6 concatenate.6.block_info
  26.9 0.0 copy-done.4
  26.9 0.1 fusion.4
  27.0 39.3 %all-gather.2.cloned.1.call-done.refs_0_.refs_1_.refs_2_ = bf16[8192,256]{1,0:T(8,128)(2,1)} async-done(((bf16[256,256]{1,0:T(8,128)(2,1)}), bf16[8192,256]{1,0:T(8,128)(2,1)}) %all-gather.2.cloned.1.call-update) | async-done | bytes 4194320 | tf_op jit(solution)/shard_map/all_gather | solution.py:185
  66.4 6.0 %shard_map.95 = bf16[256,512]{1,0:T(8,128)(2,1)} custom-call(s32[21]{0:T(128)} %concatenate.6.block_info, bf16[128,1024]{1,0:T(8,128)(2,1)} %bitcast.31, bf16[8192,256]{1,0:T(8,128)(2,1)} %all-gather.2.cloned.1.call-done.refs_0_.refs_1_.refs_2_, bf16[8192,256]{1,0:T(8,128)(2,1)} %all-gather.2.cloned.1.call-done.refs_0_.refs_1_.refs_2_, ...), custom_call_target="tpu_custom_call" | custom-call | tf_op jit(solution)/shard_map/pallas_call | solution.py:163
  72.4 9.3 %convolution_convert_fusion = bf16[512,8192]{1,0:T(8,128)(2,1)} fusion(bf16[512,8192]{1,0:T(8,128)(2,1)} %param.13, bf16[256,512]{1,0:T(8,128)(2,1)} %shard_map.95, s32[256]{0:T(256)S(1)} %multiply_add_fusion), kind=kOutput, calls=%fused_computation.2 | convolution fusion | flops 4433772544 | bytes 17040384 | tf_op jit(solution)/shard_map/dot_general | solution.py:203
  81.7 0.0 copy-start.1
  81.7 0.0 reduce-scatter.2.cloned.1.call-update
  81.7 0.0 copy-start.3
  81.7 104.0 %reduce-scatter.2.cloned.1.call-done = bf16[64,8192]{1,0:T(8,128)(2,1)} async-done(((bf16[512,8192]{1,0:T(8,128)(2,1)}), bf16[64,8192]{1,0:T(8,128)(2,1)}) %reduce-scatter.2.cloned.1.call-update) | async-done | bytes 1048592 | tf_op jit(solution)/shard_map/reduce_scatter | solution.py:206
  185.7 0.0 copy-done.1
  185.7 0.0 copy-start.2
  185.7 1.8 multiply_reduce_fusion
  187.5 0.0 copy-done.3
  187.5 0.0 copy-done.2
  187.5 1.8 multiply_convert_fusion
  (8 shorter events, 0.1 us)
Async XLA Ops:
  7.2 15.9 %copy-start = (s32[8192]{0:T(1024)S(1)}, s32[8192]{0:T(1024)}, u32[]{:S(2)}) copy-start(s32[8192]{0:T(1024)} %param.11) | copy-start | bytes 98308
  7.2 59.2 %all-gather.2.cloned.1.call-start = ((), (), s32[]{:S(2)}) async-start(), calls=%async_computation.1 | async-start | bytes 4325376 | tf_op jit(solution)/shard_map/all_gather | solution.py:185
  8.8 176.9 %reduce-scatter.2.cloned.1.call-start = ((), (), s32[]{:S(2)}) async-start(), calls=%async_computation.2 | async-start | bytes 9437184 | tf_op jit(solution)/shard_map/reduce_scatter | solution.py:206
  23.0 3.9 %copy-start.4 = (s32[256,1]{0,1:T(1,128)S(1)}, s32[256,1]{0,1:T(1,128)}, u32[]{:S(2)}) copy-start(s32[256,1]{0,1:T(1,128)} %param.12) | copy-start | bytes 3076
  81.7 104.0 %copy-start.1 = (bf16[64,8192]{1,0:T(8,128)(2,1)S(1)}, bf16[64,8192]{1,0:T(8,128)(2,1)}, u32[]{:S(2)}) copy-start(bf16[64,8192]{1,0:T(8,128)(2,1)} %param.14) | copy-start | bytes 3145732
  81.7 105.8 %copy-start.3 = (f32[8192]{0:T(1024)S(1)}, f32[8192]{0:T(1024)}, u32[]{:S(2)}) copy-start(f32[8192]{0:T(1024)} %param.15) | copy-start | bytes 98308
  185.7 1.8 copy-start.2
Sparse Core Ops, SparseCore 0:
  11.1 55.2 all-gather.1
  81.8 103.8 reduce-scatter.1

commit v15 on v11

--- a/solution.py
+++ b/solution.py
@@ -35,9 +35,8 @@
     first_block = block_info[1]
     steps = (window + 1) // 2
     rows = qt_ref.shape[1] // group
-    key_width = kv_ref.shape[0]
+    key_width = kv_ref.shape[0] // 2
     local_heads = acc_ref.shape[0] * group
-    kv_cols = kv_ref.shape[1] // 2
     score_scale = 1.0 / math.sqrt(HEAD_DIM)
 
     @pl.when(step == 0)
@@ -53,8 +52,8 @@
             key_pos = key_block * key_width + lax.broadcasted_iota(jnp.int32, (key_width, 1), 0)
             allowed = (kseg_ref[...] == qseg_ref[...]) & (key_pos <= query_pos)
         for kv_head in range(local_heads // group):
-            keys = kv_ref[:, kv_head * HEAD_DIM:(kv_head + 1) * HEAD_DIM]
-            values = kv_ref[:, kv_cols + kv_head * HEAD_DIM:kv_cols + (kv_head + 1) * HEAD_DIM]
+            keys = kv_ref[:key_width, kv_head * HEAD_DIM:(kv_head + 1) * HEAD_DIM]
+            values = kv_ref[key_width:, kv_head * HEAD_DIM:(kv_head + 1) * HEAD_DIM]
             values_t = values.astype(jnp.float32).T.astype(jnp.bfloat16)
             query_t = qt_ref[kv_head * HEAD_DIM:(kv_head + 1) * HEAD_DIM, :]
             scores = jnp.dot(keys, query_t, preferred_element_type=jnp.float32) * score_scale
@@ -98,10 +97,10 @@
 def attend_window(queries, kv_all, query_seg, segments, my_block, first_block, group):
     rows, q_cols = queries.shape
     key_width = rows
-    block_count = kv_all.shape[0] // key_width
+    block_count = kv_all.shape[0] // (2 * key_width)
     window = min(block_count, DOC_MOST // key_width + 1)
     local_heads = q_cols // HEAD_DIM
-    kv_cols = kv_all.shape[1] // 2
+    kv_cols = kv_all.shape[1]
     kv_local = local_heads // group
     queries_t = (
         queries.reshape(rows, kv_local, group, HEAD_DIM)
@@ -137,10 +136,10 @@
         in_specs=[
             pl.BlockSpec((kv_cols, group * rows), lambda step, info: (0, 0)),
             pl.BlockSpec(
-                (key_width, 2 * kv_cols), lambda step, info: (key_index(2 * step, info), 0)
+                (2 * key_width, kv_cols), lambda step, info: (key_index(2 * step, info), 0)
             ),
             pl.BlockSpec(
-                (key_width, 2 * kv_cols), lambda step, info: (key_index(2 * step + 1, info), 0)
+                (2 * key_width, kv_cols), lambda step, info: (key_index(2 * step + 1, info), 0)
             ),
             pl.BlockSpec((1, group * rows), lambda step, info: (0, 0)),
             pl.BlockSpec((key_width, 1), lambda step, info: (key_index(2 * step, info), 0)),
@@ -182,7 +181,7 @@
     query_heads = queries.reshape(rows_here, kv_local, group_size, HEAD_DIM)
     query_pos = my_start + jnp.arange(rows_here, dtype=jnp.int32)
     query_seg = lax.dynamic_slice_in_dim(segments, my_start, rows_here, 0)
-    kv_pair = jnp.concatenate([key_rows, value_rows], axis=1)
+    kv_pair = jnp.concatenate([key_rows, value_rows], axis=0)
     kv_all = lax.all_gather(kv_pair, "ctx", axis=0, tiled=True)
     doc_start = jnp.sum((segments < query_seg[0]).astype(jnp.int32))
     first_block = doc_start // rows_here

time: 196 us -> 196 us (level)
  no operation moved by 1% of the time
where the time goes in v15:
time: 196 us
  waiting for transfers between devices  143 us (73%)
  between operations  17.9 us (9%)
  local copies, waits for them, and re-layouts  10.4 us (5%)
  matrix products  9.26 us (5%)
  other arithmetic  9.12 us (5%)
  Pallas kernels  5.32 us (3%)
    reduce_scatter x1, waiting for transfers between devices, on_device(): lax.psum_scatter(partial_slots, 'tp', scatter_dimension=0, tiled=True)  104 us
    all_gather x1, waiting for transfers between devices, on_device(): kv_all = lax.all_gather(kv_pair, 'ctx', axis=0, tiled=True)  39.3 us
    dot_general x1, matrix products, on_device(): jnp.dot(attended_slots, out_proj, preferred_element_type=jnp.float32)  9.26 us
    pallas_call x1, Pallas kernels, attend_window(): kernel(block_info, queries_t, kv_all, kv_all, jnp.tile(query_seg, group)....  5.32 us
  transfers between devices with their start and end apart: 2, of which 2 were waited for; matrix products, arithmetic and copies ran while one was open for 7% of the time, Pallas kernels for 0%

profile of v15, /device:TPU:1, one launch (start us, length us, event | category | flops | bytes accessed | tf_op | source)
XLA Modules:
  0.0 195.5 jit_solution(5855398722569603807)
XLA Ops:
  7.2 0.0 copy-start
  7.2 0.0 all-gather.2.cloned.1.call-start
  7.2 1.5 pad_maximum_fusion
  8.8 0.0 all-gather.2.cloned.1.call-update
  8.8 0.0 reduce-scatter.2.cloned.1.call-start
  8.8 0.8 dynamic_slice.3
  9.6 0.6 fusion.8
  10.2 2.0 %convert_reduce_fusion = s32[]{:T(128)} fusion(s32[8192]{0:T(1024)} %param.11, s32[]{:T(128)} %bitcast.5), kind=kLoop, calls=%fused_computation.11 | loop fusion | flops 24575 | bytes 32776 | tf_op jit(solution)/shard_map/reduce_sum | solution.py:186
  16.0 0.6 copy.15
  16.6 1.5 gather_fusion
  18.1 1.5 gather_fusion.1
  19.5 0.7 fusion.5
  20.2 0.6 reduce-window.6
  20.8 0.2 slice_reduce_fusion
  21.0 1.0 reshape.84
  22.1 0.2 copy.11
  22.3 0.7 copy.14
  23.0 0.0 copy-done
  23.0 0.0 copy-start.4
  23.0 2.6 %copy.12.kseg_ref.kseg_next_ref = s32[8192,1]{1,0:T(8,128)} copy(s32[8192,1]{0,1:T(1,128)S(1)} %bitcast.30) | data formatting | bytes 65536 | tf_op jit(solution)/shard_map/reshape | solution.py:167
  25.7 0.6 and_convert_fusion
  26.3 0.6 concatenate.6.block_info
  26.9 0.0 copy-done.4
  26.9 0.1 fusion.4
  27.0 39.3 %all-gather.2.cloned.1.call-done.kv_ref.kv_next_ref = bf16[16384,128]{1,0:T(8,128)(2,1)} async-done(((bf16[512,128]{1,0:T(8,128)(2,1)}), bf16[16384,128]{1,0:T(8,128)(2,1)}) %all-gather.2.cloned.1.call-update) | async-done | bytes 4194320 | tf_op jit(solution)/shard_map/all_gather | solution.py:185
  66.4 5.3 %shard_map.95 = bf16[256,512]{1,0:T(8,128)(2,1)} custom-call(s32[21]{0:T(128)} %concatenate.6.block_info, bf16[128,1024]{1,0:T(8,128)(2,1)} %bitcast.31, bf16[16384,128]{1,0:T(8,128)(2,1)} %all-gather.2.cloned.1.call-done.kv_ref.kv_next_ref, bf16[16384,128]{1,0:T(8,128)(2,1)} %all-gather.2.cloned.1.call-done.kv_ref.kv_next_ref, s32[1,1024]{1,0:T(1,128)} %bitcast.33, ...), custom_call_target="tpu_custom_call" | custom-call | tf_op jit(solution)/shard_map/pallas_call | solution.py:161
  71.7 9.3 %convolution_convert_fusion = bf16[512,8192]{1,0:T(8,128)(2,1)} fusion(bf16[512,8192]{1,0:T(8,128)(2,1)} %param.13, bf16[256,512]{1,0:T(8,128)(2,1)} %shard_map.95, s32[256]{0:T(256)S(1)} %multiply_add_fusion), kind=kOutput, calls=%fused_computation.2 | convolution fusion | flops 4433772544 | bytes 17040384 | tf_op jit(solution)/shard_map/dot_general | solution.py:203
  80.9 0.0 copy-start.1
  80.9 0.0 reduce-scatter.2.cloned.1.call-update
  81.0 0.0 copy-start.3
  81.0 104.1 %reduce-scatter.2.cloned.1.call-done = bf16[64,8192]{1,0:T(8,128)(2,1)} async-done(((bf16[512,8192]{1,0:T(8,128)(2,1)}), bf16[64,8192]{1,0:T(8,128)(2,1)}) %reduce-scatter.2.cloned.1.call-update) | async-done | bytes 1048592 | tf_op jit(solution)/shard_map/reduce_scatter | solution.py:206
  185.1 0.0 copy-done.1
  185.1 0.0 copy-start.2
  185.1 1.8 multiply_reduce_fusion
  186.9 0.0 copy-done.3
  186.9 0.0 copy-done.2
  186.9 1.8 multiply_convert_fusion
  (8 shorter events, 0.1 us)
Async XLA Ops:
  7.2 15.9 %copy-start = (s32[8192]{0:T(1024)S(1)}, s32[8192]{0:T(1024)}, u32[]{:S(2)}) copy-start(s32[8192]{0:T(1024)} %param.11) | copy-start | bytes 98308
  7.2 59.2 %all-gather.2.cloned.1.call-start = ((), (), s32[]{:S(2)}) async-start(), calls=%async_computation.1 | async-start | bytes 4325376 | tf_op jit(solution)/shard_map/all_gather | solution.py:185
  8.8 176.3 %reduce-scatter.2.cloned.1.call-start = ((), (), s32[]{:S(2)}) async-start(), calls=%async_computation.2 | async-start | bytes 9437184 | tf_op jit(solution)/shard_map/reduce_scatter | solution.py:206
  23.0 3.9 %copy-start.4 = (s32[256,1]{0,1:T(1,128)S(1)}, s32[256,1]{0,1:T(1,128)}, u32[]{:S(2)}) copy-start(s32[256,1]{0,1:T(1,128)} %param.12) | copy-start | bytes 3076
  80.9 104.2 %copy-start.1 = (bf16[64,8192]{1,0:T(8,128)(2,1)S(1)}, bf16[64,8192]{1,0:T(8,128)(2,1)}, u32[]{:S(2)}) copy-start(bf16[64,8192]{1,0:T(8,128)(2,1)} %param.14) | copy-start | bytes 3145732
  81.0 105.9 %copy-start.3 = (f32[8192]{0:T(1024)S(1)}, f32[8192]{0:T(1024)}, u32[]{:S(2)}) copy-start(f32[8192]{0:T(1024)} %param.15) | copy-start | bytes 98308
  185.1 1.8 copy-start.2
Sparse Core Ops, SparseCore 0:
  11.1 55.2 all-gather.1
  81.1 103.9 reduce-scatter.1
